TPU v7x, 512 devices: a whole 4x4x16 slice. The times are simulated.
512 devices in a mesh: dp: 32 (over x, z_lo), tensor: 16 (over z_hi, y, core).
Axes of the slice: x: 4, y: 4, z: 16 (z_hi: 2, z_lo: 8; z = z_hi * 8 + z_lo), core: 2. Of those that a mesh axis runs over, the one named last changes fastest.
Arguments:
- tokens: bfloat16 [8192, 8192], P(('dp', 'tensor')), may hold values from -6 to 6
- norm_gain: float32 [8192], replicated, may hold values from 0.1 to 1.9
- w_query: bfloat16 [8192, 4096], P('dp', 'tensor'), may hold values from -0.0625 to 0.0625
- w_key: bfloat16 [8192, 512], P('dp', 'tensor'), may hold values from -0.0625 to 0.0625
- w_value: bfloat16 [8192, 512], P('dp', 'tensor'), may hold values from -0.0625 to 0.0625
- w_out: bfloat16 [4096, 8192], P('tensor', 'dp'), may hold values from -0.25 to 0.25
Outputs:
- layer_out: bfloat16 [8192, 8192], P(('dp', 'tensor'))
All inputs are finite; a program needn't handle non-finite values.
Results may differ from a plain program's by a relative error of at most 0.019.
Values may be sent and summed in bfloat16 or wider, within the bound.
No kernel may reach another device: no remote copies, remote signals or barrier semaphores. Data moves between devices by JAX's collectives and lax.ppermute only.
A program may use at most 64 MiB of HBM per device.

v0:
```python
import math

import jax
import jax.numpy as jnp
from jax import lax
from jax.sharding import PartitionSpec as P

QH = 32
KVH = 4
HD = 128
SEQ = 128


theta_base = 500000.0
epsilon = 1e-05


def normalize(tokens, norm_gain):
    widened = tokens.astype(jnp.float32)
    mean_square = jnp.mean(widened * widened, axis=-1, keepdims=True)
    return (widened * lax.rsqrt(mean_square + epsilon) * norm_gain[None, :]).astype(jnp.bfloat16)


def head_major(matrix, head_count):
    row_count = matrix.shape[0]
    head_width = matrix.shape[1] // head_count
    return jnp.transpose(matrix.reshape(row_count, head_width, head_count), (0, 2, 1)).reshape(
        row_count, head_count * head_width
    )


def rotary(matrix, head_count, seq_span):
    row_count = matrix.shape[0]
    head_width = matrix.shape[1] // head_count
    half_width = head_width // 2
    position = (jnp.arange(row_count, dtype=jnp.int32) % seq_span).astype(jnp.float32)
    frequency = jnp.exp(
        jnp.arange(half_width, dtype=jnp.float32) * (-2.0 * math.log(theta_base) / head_width)
    )
    angles = position[:, None] * frequency[None, :]
    cosine = jnp.cos(angles)[:, None, :]
    sine_part = jnp.sin(angles)[:, None, :]
    shaped = matrix.reshape(row_count, head_count, head_width)
    first_half = shaped[..., :half_width]
    second_half = shaped[..., half_width:]
    joined = jnp.concatenate(
        [
            first_half * cosine - second_half * sine_part,
            second_half * cosine + first_half * sine_part,
        ],
        axis=-1,
    )
    return joined.reshape(row_count, head_count * head_width)


def attend(queries, key_heads, value_heads, seq_span):
    row_count, head_count, head_width = queries.shape
    seq_count = row_count // seq_span
    query_four = queries.reshape(seq_count, seq_span, head_count, head_width)
    key_four = key_heads.reshape(seq_count, seq_span, head_count, head_width)
    value_four = value_heads.reshape(seq_count, seq_span, head_count, head_width)
    scores = jnp.einsum(
        "nqhd,nkhd->nhqk", query_four, key_four, preferred_element_type=jnp.float32
    ) * (1.0 / math.sqrt(head_width))
    causal = jnp.arange(seq_span)[:, None] >= jnp.arange(seq_span)[None, :]
    raw_weights = jnp.where(causal[None, None], jnp.exp(scores), 0.0)
    weights = (raw_weights / jnp.sum(raw_weights, axis=-1, keepdims=True)).astype(jnp.bfloat16)
    attended = jnp.einsum(
        "nhqk,nkhd->nqhd", weights, value_four, preferred_element_type=jnp.float32
    )
    return attended.astype(jnp.bfloat16).reshape(row_count, head_count * head_width)


def body(tokens, norm_gain, w_query, w_key, w_value, w_out):
    tensor_rank = lax.axis_index("tensor")
    normed = normalize(tokens, norm_gain)
    gathered = lax.all_gather(normed, "tensor", axis=0, tiled=True)
    row_count = gathered.shape[0]

    def add_rows(shard_piece):
        return jnp.dot(gathered, shard_piece, preferred_element_type=jnp.float32)

    query_part = add_rows(lax.all_gather(w_query, "dp", axis=0, tiled=True))
    key_part = add_rows(lax.all_gather(w_key, "dp", axis=0, tiled=True))
    value_part = add_rows(lax.all_gather(w_value, "dp", axis=0, tiled=True))
    key_whole, value_whole = (
        lax.all_gather(key_part.astype(jnp.bfloat16), "tensor", axis=1, tiled=True).astype(
            key_part.dtype
        ),
        lax.all_gather(value_part.astype(jnp.bfloat16), "tensor", axis=1, tiled=True).astype(
            value_part.dtype
        ),
    )
    local_heads = w_query.shape[1] // HD
    queries = (
        rotary(query_part, local_heads, SEQ)
        .astype(jnp.bfloat16)
        .reshape(row_count, local_heads, HD)
    )
    key_heads = (
        rotary(head_major(key_whole, KVH), KVH, SEQ)
        .astype(jnp.bfloat16)
        .reshape(row_count, KVH, HD)
    )
    value_heads = head_major(value_whole, KVH).astype(jnp.bfloat16).reshape(row_count, KVH, HD)
    owner = (tensor_rank * local_heads + jnp.arange(local_heads, dtype=jnp.int32)) // (QH // KVH)
    key_heads = jnp.take(key_heads, owner, axis=1)
    value_heads = jnp.take(value_heads, owner, axis=1)
    mixed = attend(queries, key_heads, value_heads, SEQ)
    partial_out = jnp.dot(
        mixed, lax.all_gather(w_out, "dp", axis=1, tiled=True), preferred_element_type=jnp.float32
    )
    summed = lax.psum_scatter(
        partial_out.astype(jnp.bfloat16), "tensor", scatter_dimension=0, tiled=True
    ).astype(jnp.float32)
    return (tokens.astype(jnp.float32) + summed).astype(jnp.bfloat16)


def solution(mesh):
    in_specs = (
        P(("dp", "tensor"), None),
        P(),
        P("dp", "tensor"),
        P("dp", "tensor"),
        P("dp", "tensor"),
        P("tensor", "dp"),
    )
    out_specs = P(("dp", "tensor"), None)
    return jax.shard_map(body, mesh=mesh, in_specs=in_specs, out_specs=out_specs, check_vma=False)
```

profile of v0, /device:TPU:1, one launch (start us, length us, event | category | flops | bytes accessed | tf_op | source)
XLA Modules:
  0.0 749.2 jit_solution(13739372647137769479)
XLA Ops:
  6.5 0.0 all-gather.4.cloned.1.call-start
  6.5 1.1 fusion.3
  7.7 1.8 fusion.5
  9.5 0.0 all-gather.4.cloned.1.call-update
  9.5 0.0 all-gather.6.cloned.1.call-start
  9.5 0.7 all-gather.6.cloned.1.call-update
  10.2 0.0 all-gather.8.cloned.1.call-start
  10.3 0.7 all-gather.8.cloned.1.call-update
  11.0 0.0 reduce-scatter.2.cloned.1.call-start
  11.1 0.5 multiply_cosine_fusion
  11.7 136.3 %all_gather.25 = bf16[8192,32]{0,1:T(8,128)(2,1)S(1)} all-gather(bf16[256,32]{0,1:T(8,128)(2,1)} %param.11), channel_id=1, replica_groups=mesh['dp'=32,'tensor'=16] {'dp'}, dimensions={0}, use_global_device_ids=true | all-gather | bytes 540672 | tf_op jit(solution)/shard_map/all_gather | solution.py:84
  148.0 105.9 %all_gather.22 = bf16[8192,32]{0,1:T(8,128)(2,1)S(1)} all-gather(bf16[256,32]{0,1:T(8,128)(2,1)} %param.12), channel_id=1, replica_groups=mesh['dp'=32,'tensor'=16] {'dp'}, dimensions={0}, use_global_device_ids=true | all-gather | bytes 540672 | tf_op jit(solution)/shard_map/all_gather | solution.py:85
  253.9 0.0 all-gather.4.cloned.1.call-done
  253.9 3.5 convolution_convert_fusion.2
  257.4 82.2 %all_gather.26 = bf16[256,512]{0,1:T(8,128)(2,1)S(1)} all-gather(bf16[256,32]{0,1:T(8,128)(2,1)S(1)} %convolution_convert_fusion.2), channel_id=1, replica_groups=mesh['dp'=32,'tensor'=16] {'tensor'}, dimensions={1}, use_global_device_ids=true | all-gather | bytes 278528 | tf_op jit(solution)/shard_map/all_gather | solution.py:87
  339.7 0.1 reshape.119
  339.8 0.2 copy.11
  340.1 3.6 convolution_convert_fusion.3
  343.6 34.6 %all_gather.23 = bf16[256,512]{0,1:T(8,128)(2,1)S(1)} all-gather(bf16[256,32]{0,1:T(8,128)(2,1)S(1)} %convolution_convert_fusion.3), channel_id=1, replica_groups=mesh['dp'=32,'tensor'=16] {'tensor'}, dimensions={1}, use_global_device_ids=true | all-gather | bytes 278528 | tf_op jit(solution)/shard_map/all_gather | solution.py:90
  378.2 0.1 convert_element_type.73
  378.2 0.2 copy.8
  378.5 0.3 subtract_convert_fusion
  378.7 0.1 pad_maximum_fusion
  378.9 0.6 gather_fusion.1
  379.5 0.6 gather_fusion
  380.0 0.1 broadcast_select_fusion.1
  380.1 0.0 all-gather.6.cloned.1.call-done
  380.2 5.2 fusion.17
  385.4 0.1 copy.20
  385.5 0.1 copy.21
  385.7 0.1 subtract_convert_fusion.1
  385.8 0.1 pad_maximum_fusion.1
  385.9 0.2 fusion.1
  386.1 0.2 fusion.2
  386.3 0.1 copy.16
  386.5 184.0 %all-gather.8.cloned.1.call-done = bf16[256,8192]{1,0:T(8,128)(2,1)} async-done(((bf16[256,256]{1,0:T(8,128)(2,1)}), bf16[256,8192]{1,0:T(8,128)(2,1)}) %all-gather.8.cloned.1.call-update) | async-done | bytes 4194320 | tf_op jit(solution)/shard_map/all_gather | solution.py:111
  570.4 5.4 convolution_convert_fusion
  575.9 0.0 copy-start
  575.9 0.0 reduce-scatter.2.cloned.1.call-update
  575.9 165.0 %reduce-scatter.2.cloned.1.call-done = bf16[16,8192]{1,0:T(8,128)(2,1)} async-done(((bf16[256,8192]{1,0:T(8,128)(2,1)}), bf16[16,8192]{1,0:T(8,128)(2,1)}) %reduce-scatter.2.cloned.1.call-update) | async-done | bytes 262160 | tf_op jit(solution)/shard_map/reduce_scatter | solution.py:113
  740.9 0.0 copy-done
  740.9 1.7 fusion.6
  (8 shorter events, 0.1 us)
Async XLA Ops:
  6.5 247.4 %all-gather.4.cloned.1.call-start = ((), (), s32[]{:S(2)}) async-start(), calls=%async_computation.1 | async-start | bytes 4456448 | tf_op jit(solution)/shard_map/all_gather | solution.py:77
  9.5 370.7 %all-gather.6.cloned.1.call-start = ((), (), s32[]{:S(2)}) async-start(), calls=%async_computation.2 | async-start | bytes 4325376 | tf_op jit(solution)/shard_map/all_gather | solution.py:83
  10.2 560.2 %all-gather.8.cloned.1.call-start = ((), (), s32[]{:S(2)}) async-start(), calls=%async_computation.3 | async-start | bytes 4325376 | tf_op jit(solution)/shard_map/all_gather | solution.py:111
  11.0 729.9 %reduce-scatter.2.cloned.1.call-start = ((), (), s32[]{:S(2)}) async-start(), calls=%async_computation.4 | async-start | bytes 4456448 | tf_op jit(solution)/shard_map/reduce_scatter | solution.py:113
  575.9 165.1 %copy-start = (bf16[16,8192]{1,0:T(8,128)(2,1)S(1)}, bf16[16,8192]{1,0:T(8,128)(2,1)}, u32[]{:S(2)}) copy-start(bf16[16,8192]{1,0:T(8,128)(2,1)} %param.8) | copy-start | bytes 786436
Sparse Core Ops, SparseCore 0:
  10.7 130.7 all-gather.3
  143.5 212.1 all-gather.5
  357.7 212.7 all-gather.7
  576.0 164.8 reduce-scatter.1
where the time goes:
time: 750 us; the launch traced here: 749 us
  blocking collectives  359 us (48%)
  waiting for transfers between devices  350 us (47%)
  matrix products  18.2 us (2%)
  between operations  13.3 us (2%)
    all_gather x1, waiting for transfers between devices, body(): lax.all_gather(w_out, 'dp', axis=1, tiled=True)  184 us
    reduce_scatter x1, waiting for transfers between devices, body(): lax.psum_scatter(partial_out.astype(jnp.bfloat16), 'tensor', scatter_dime...  165 us
    all_gather x1, blocking collectives, body(): key_part = add_rows(lax.all_gather(w_key, 'dp', axis=0, tiled=True))  136 us
    all_gather x1, blocking collectives, body(): value_part = add_rows(lax.all_gather(w_value, 'dp', axis=0, tiled=True))  106 us
    all_gather x1, blocking collectives, body(): lax.all_gather(key_part.astype(jnp.bfloat16), 'tensor', axis=1, tiled=True)  82.2 us
    all_gather x1, blocking collectives, body(): lax.all_gather(value_part.astype(jnp.bfloat16), 'tensor', axis=1, tiled=T...  34.6 us
  transfers between devices with their start and end apart: 4, of which 2 were waited for; matrix products, arithmetic and copies ran while one was open for 2% of the time, Pallas kernels for 0%

commit v1 on v0

--- a/solution.py
+++ b/solution.py
@@ -3,7 +3,7 @@
 import jax
 import jax.numpy as jnp
 from jax import lax
-from jax.sharding import PartitionSpec as P
+from jax.sharding import Mesh, PartitionSpec as P
 
 QH = 32
 KVH = 4
@@ -71,27 +71,54 @@
     return attended.astype(jnp.bfloat16).reshape(row_count, head_count * head_width)
 
 
+def ring_gather(block, axis_name, size):
+    if size == 1:
+        return block[None]
+    index = lax.axis_index(axis_name)
+    forward = [(s, (s + 1) % size) for s in range(size)]
+    backward = [(s, (s - 1) % size) for s in range(size)]
+    relative = [None] * size
+    relative[0] = block
+    ahead = block
+    behind = block
+    for step in range(1, size // 2 + 1):
+        ahead = lax.ppermute(ahead, axis_name, forward)
+        relative[(-step) % size] = ahead
+        if step < size - size // 2:
+            behind = lax.ppermute(behind, axis_name, backward)
+            relative[step] = behind
+    stacked = jnp.stack(relative)
+    return jnp.roll(stacked, index, axis=0)
+
+
+def group_gather(block):
+    along_y = ring_gather(block, "y", 4)
+    along_zh = ring_gather(along_y, "zh", 2)
+    along_c = ring_gather(along_zh, "c", 2)
+    ordered = jnp.moveaxis(along_c, 0, 2)
+    return ordered.reshape((-1,) + block.shape[1:])
+
+
+def dp_gather(block, axis):
+    return lax.all_gather(lax.all_gather(block, "zl", axis=axis, tiled=True), "x", axis=axis, tiled=True)
+
+
 def body(tokens, norm_gain, w_query, w_key, w_value, w_out):
-    tensor_rank = lax.axis_index("tensor")
+    tensor_rank = (lax.axis_index("zh") * 4 + lax.axis_index("y")) * 2 + lax.axis_index("c")
     normed = normalize(tokens, norm_gain)
-    gathered = lax.all_gather(normed, "tensor", axis=0, tiled=True)
+    gathered = group_gather(normed)
     row_count = gathered.shape[0]
-
-    def add_rows(shard_piece):
-        return jnp.dot(gathered, shard_piece, preferred_element_type=jnp.float32)
-
-    query_part = add_rows(lax.all_gather(w_query, "dp", axis=0, tiled=True))
-    key_part = add_rows(lax.all_gather(w_key, "dp", axis=0, tiled=True))
-    value_part = add_rows(lax.all_gather(w_value, "dp", axis=0, tiled=True))
-    key_whole, value_whole = (
-        lax.all_gather(key_part.astype(jnp.bfloat16), "tensor", axis=1, tiled=True).astype(
-            key_part.dtype
-        ),
-        lax.all_gather(value_part.astype(jnp.bfloat16), "tensor", axis=1, tiled=True).astype(
-            value_part.dtype
-        ),
-    )
-    local_heads = w_query.shape[1] // HD
+    q_cols = w_query.shape[1]
+    k_cols = w_key.shape[1]
+    weights = dp_gather(jnp.concatenate([w_query, w_key, w_value], axis=1), 0)
+    projected = jnp.dot(gathered, weights, preferred_element_type=jnp.float32)
+    query_part = projected[:, :q_cols]
+    kv_part = projected[:, q_cols:].astype(jnp.bfloat16)
+    kv_all = group_gather(kv_part.T)
+    kv_all = kv_all.reshape(-1, 2, k_cols, row_count)
+    key_whole = jnp.transpose(kv_all[:, 0], (2, 0, 1)).reshape(row_count, -1).astype(jnp.float32)
+    value_whole = jnp.transpose(kv_all[:, 1], (2, 0, 1)).reshape(row_count, -1).astype(jnp.float32)
+    local_heads = q_cols // HD
     queries = (
         rotary(query_part, local_heads, SEQ)
         .astype(jnp.bfloat16)
@@ -108,22 +135,27 @@
     value_heads = jnp.take(value_heads, owner, axis=1)
     mixed = attend(queries, key_heads, value_heads, SEQ)
     partial_out = jnp.dot(
-        mixed, lax.all_gather(w_out, "dp", axis=1, tiled=True), preferred_element_type=jnp.float32
-    )
-    summed = lax.psum_scatter(
-        partial_out.astype(jnp.bfloat16), "tensor", scatter_dimension=0, tiled=True
-    ).astype(jnp.float32)
+        mixed, dp_gather(w_out, 1), preferred_element_type=jnp.float32
+    ).astype(jnp.bfloat16)
+    width = partial_out.shape[1]
+    regrouped = partial_out.reshape(2, -1, row_count // 16, width).transpose(1, 0, 2, 3)
+    regrouped = regrouped.reshape(row_count, width)
+    summed = lax.psum_scatter(regrouped, ("y", "c"), scatter_dimension=0, tiled=True)
+    summed = lax.psum_scatter(summed, "zh", scatter_dimension=0, tiled=True).astype(jnp.float32)
     return (tokens.astype(jnp.float32) + summed).astype(jnp.bfloat16)
 
 
 def solution(mesh):
+    fine = Mesh(mesh.devices.reshape(4, 8, 2, 4, 2), ("x", "zl", "zh", "y", "c"))
+    dp = ("x", "zl")
+    tensor = ("zh", "y", "c")
     in_specs = (
-        P(("dp", "tensor"), None),
+        P(dp + tensor, None),
         P(),
-        P("dp", "tensor"),
-        P("dp", "tensor"),
-        P("dp", "tensor"),
-        P("tensor", "dp"),
+        P(dp, tensor),
+        P(dp, tensor),
+        P(dp, tensor),
+        P(tensor, dp),
     )
-    out_specs = P(("dp", "tensor"), None)
-    return jax.shard_map(body, mesh=mesh, in_specs=in_specs, out_specs=out_specs, check_vma=False)
+    out_specs = P(dp + tensor, None)
+    return jax.shard_map(body, mesh=fine, in_specs=in_specs, out_specs=out_specs, check_vma=False)

time: 750 us -> 448 us (0.60)
  blocking collectives: 359 us -> 0 us
  starting transfers between devices: 0.12 us -> 53.7 us
  other arithmetic: 5.92 us -> 18.5 us
  waiting for transfers between devices: 350 us -> 342 us
  matrix products: 18.2 us -> 10.3 us
    all_gather x4 -> x0, blocking collectives: 359 us -> none  [the longest x1 136 us: body(): key_part = add_rows(lax.all_gather(w_key, 'dp', axis=0, tiled=True))]
    ppermute x0 -> x10, waiting for transfers between devices: none -> 126 us  [the longest x8 126 us: ring_gather(): ahead = lax.ppermute(ahead, axis_name, forward)]
    all_gather x3 -> x4, waiting for transfers between devices: 184 us -> 117 us  [the longest x2 69 us: dp_gather(): lax.all_gather(lax.all_gather(block, 'zl', axis=axis, tiled=True), 'x', a...]
    reduce_scatter x1 -> x2, waiting for transfers between devices: 165 us -> 98.8 us  [the longest x1 54.9 us: body(): lax.psum_scatter(summed, 'zh', scatter_dimension=0, tiled=True)]
    ppermute x0 -> x10, starting transfers between devices: none -> 53.5 us  [the longest x8 45.8 us: ring_gather(): ahead = lax.ppermute(ahead, axis_name, forward)]
    concatenate x0 -> x4, other arithmetic: none -> 11.1 us  [the longest x3 9.45 us: ring_gather(): return jnp.roll(stacked, index, axis=0)]
    dot_general x4 -> x2, matrix products: 17.7 us -> 9.88 us  [the longest x1 6.44 us: body(): projected = jnp.dot(gathered, weights, preferred_element_type=jnp.float32)]
  transfers between devices with their start and end apart: 4 -> 16, of which waited for: 2 -> 13; matrix products, arithmetic and copies ran while one was open for 2% -> 6% of each run, Pallas kernels for 0% -> 0%
where the time goes in v1:
time: 448 us; the launch traced here: 447 us
  waiting for transfers between devices  342 us (76%)
  starting transfers between devices  53.7 us (12%)
  other arithmetic  18.5 us (4%)
  between operations  14 us (3%)
  matrix products  10.3 us (2%)
  local copies, waits for them, and re-layouts  9.12 us (2%)
    ppermute x8, waiting for transfers between devices, ring_gather(): ahead = lax.ppermute(ahead, axis_name, forward)  126 us
    all_gather x2, waiting for transfers between devices, dp_gather(): lax.all_gather(lax.all_gather(block, 'zl', axis=axis, tiled=True), 'x', a...  69 us
    reduce_scatter x1, waiting for transfers between devices, body(): lax.psum_scatter(summed, 'zh', scatter_dimension=0, tiled=True)  54.9 us
    all_gather x2, waiting for transfers between devices, dp_gather(): lax.all_gather(block, 'zl', axis=axis, tiled=True)  48 us
    ppermute x8, starting transfers between devices, ring_gather(): ahead = lax.ppermute(ahead, axis_name, forward)  45.8 us
    reduce_scatter x1, waiting for transfers between devices, body(): lax.psum_scatter(regrouped, ('y', 'c'), scatter_dimension=0, tiled=True)  43.9 us
    concatenate x3, other arithmetic, ring_gather(): return jnp.roll(stacked, index, axis=0)  9.45 us
  transfers between devices with their start and end apart: 16, of which 13 were waited for; matrix products, arithmetic and copies ran while one was open for 6% of the time, Pallas kernels for 0%

profile of v1, /device:TPU:1, one launch (start us, length us, event | category | flops | bytes accessed | tf_op | source)
XLA Modules:
  0.0 447.4 jit_solution(180573802535583890)
XLA Ops:
  6.5 0.8 copy.22
  7.4 0.8 copy.23
  8.2 1.7 pad_maximum_fusion.1
  10.0 1.1 fusion.9
  11.1 1.1 bitcast_dynamic-update-slice_fusion.6
  12.2 4.0 collective-permute-start.1
  16.3 3.4 collective-permute-start
  19.7 1.7 collective-permute-done.1
  21.4 3.0 collective-permute-start.2
  24.4 6.2 %collective-permute-done.2 = bf16[16,8192]{1,0:T(8,128)(2,1)S(1)} collective-permute-done((bf16[16,8192]{1,0:T(8,128)(2,1)S(1)}, bf16[16,8192]{1,0:T(8,128)(2,1)S(1)}, u32[]{:S(2)}, u32[]{:S(2)}) %collective-permute-start.2) | collective-permute-done | bytes 262176 | tf_op jit(solution)/shard_map/ppermute | solution.py:85
  30.8 48.0 %all-gather.5.cloned.1.call-done = bf16[2048,320]{1,0:T(8,128)(2,1)} async-done(((bf16[256,320]{1,0:T(8,128)(2,1)}), bf16[2048,320]{1,0:T(8,128)(2,1)}) %all-gather.5.cloned.1.call-update) | async-done | bytes 1310736 | tf_op jit(solution)/shard_map/all_gather | solution.py:103
  78.9 1.4 copy-done
  80.3 8.2 %collective-permute-start.3 = (bf16[4,16,8192]{2,1,0:T(8,128)(2,1)S(1)}, bf16[4,16,8192]{2,1,0:T(8,128)(2,1)S(1)}, u32[]{:S(2)}, u32[]{:S(2)}) collective-permute-start(bf16[4,16,8192]{2,1,0:T(8,128)(2,1)S(1)} %constant_dynamic-slice_fusion.1), channel_id=1, source_target_pairs={{0,8},{8,0},{1,9},{9,1},{2,10},{10,2},{3,11},{11,3},{4,12},{12,4},... | collective-permute-start | bytes 3145736 | tf_op jit(solution)/shard_map/ppermute | solution.py:85
  88.5 1.3 fusion.40
  89.8 105.3 %collective-permute-done.3 = bf16[4,16,8192]{2,1,0:T(8,128)(2,1)S(1)} collective-permute-done((bf16[4,16,8192]{2,1,0:T(8,128)(2,1)S(1)}, bf16[4,16,8192]{2,1,0:T(8,128)(2,1)S(1)}, u32[]{:S(2)}, u32[]{:S(2)}) %collective-permute-start.3) | collective-permute-done | bytes 1048608 | tf_op jit(solution)/shard_map/ppermute | solution.py:85
  195.1 2.8 fusion.5
  197.9 2.9 collective-permute-start.4
  200.9 0.5 multiply_cosine_fusion
  201.5 1.5 fusion.39
  203.0 1.9 collective-permute-done.4
  204.9 6.5 %fusion.2 = bf16[2,2,4,16,8192]{4,3,0,2,1:T(8,128)(2,1)} fusion(s32[]{:T(128)S(6)} %select_n.97, bf16[1,2,4,16,8192]{4,3,0,2,1:T(8,128)(2,1)S(1)} %fusion.39, bf16[1,2,4,16,8192]{4,3,0,2,1:T(8,128)(2,1)} %bitcast.7), kind=kLoop, calls=%fused_computation.9 | loop fusion | flops 6291456 | bytes 8388612 | tf_op jit(solution)/shard_map/jit(_roll_dynamic)/concatenate | solution.py:91
  211.4 64.3 %all-gather.7.cloned.1.call-done = bf16[8192,320]{1,0:T(8,128)(2,1)} async-done(((bf16[2048,320]{1,0:T(8,128)(2,1)}), bf16[8192,320]{1,0:T(8,128)(2,1)}) %all-gather.7.cloned.1.call-update) | async-done | bytes 5242896 | tf_op jit(solution)/shard_map/all_gather | solution.py:103
  275.6 6.4 %fusion.32 = f32[256,320]{0,1:T(8,128)S(1)} fusion(bf16[256,8192]{1,0:T(8,128)(2,1)} %bitcast.87, bf16[8192,320]{1,0:T(8,128)(2,1)} %all-gather.7.cloned.1.call-done), kind=kOutput, calls=%fused_computation.99 | convolution fusion | flops 1342177280 | bytes 9764864 | tf_op jit(solution)/shard_map/dot_general | solution.py:114
  282.1 4.4 collective-permute-start.5
  286.5 1.9 collective-permute-start.6
  288.5 3.9 collective-permute-done.6
  292.4 1.9 collective-permute-start.7
  294.3 3.9 collective-permute-done.7
  298.3 12.5 %collective-permute-start.8 = (bf16[4,64,256]{2,1,0:T(8,128)(2,1)S(1)}, bf16[4,64,256]{2,1,0:T(8,128)(2,1)S(1)}, u32[]{:S(2)}, u32[]{:S(2)}) collective-permute-start(bf16[4,64,256]{2,1,0:T(8,128)(2,1)S(1)} %constant_dynamic-slice_fusion), channel_id=1, source_target_pairs={{0,8},{8,0},{1,9},{9,1},{2,10},{10,2},{3,11},{11,3},{4,12},{12,4},... | collective-permute-start | bytes 393224 | tf_op jit(solution)/shard_map/ppermute | solution.py:85
  311.2 2.3 collective-permute-done.8
  313.5 0.2 fusion.19
  313.7 11.4 %collective-permute-start.9 = (bf16[2,4,64,256]{3,2,1,0:T(8,128)(2,1)S(1)}, bf16[2,4,64,256]{3,2,1,0:T(8,128)(2,1)S(1)}, u32[]{:S(2)}, u32[]{:S(2)}) collective-permute-start(bf16[2,4,64,256]{3,2,1,0:T(8,128)(2,1)S(1)} %fusion.19), channel_id=1, source_target_pairs={{0,1},{1,0},{2,3},{3,2},{4,5},{5,4},{6,7},{7,6},{8,9},{9,8},{10,11... | collective-permute-start | bytes 786440 | tf_op jit(solution)/shard_map/ppermute | solution.py:85
  325.3 0.2 fusion.37
  325.5 0.6 collective-permute-done.9
  326.0 0.4 fusion.16
  326.7 0.2 copy.28
  327.0 0.2 copy.25
  327.2 0.3 subtract_convert_fusion
  327.6 0.6 gather_fusion.1
  328.2 0.6 gather_fusion
  328.9 0.2 fusion.7
  329.1 0.2 fusion.8
  329.5 4.8 %all-gather.11.cloned.1.call-done = bf16[256,8192]{1,0:T(8,128)(2,1)} async-done(((bf16[256,2048]{1,0:T(8,128)(2,1)}), bf16[256,8192]{1,0:T(8,128)(2,1)}) %all-gather.11.cloned.1.call-update) | async-done | bytes 4194320 | tf_op jit(solution)/shard_map/all_gather | solution.py:103
  334.3 3.4 convolution_convert_fusion
  337.7 2.2 copy.34
  340.0 43.9 %reduce-scatter.3.cloned.1.call-done = bf16[32,8192]{1,0:T(8,128)(2,1)} async-done(((bf16[256,8192]{1,0:T(8,128)(2,1)}), bf16[32,8192]{1,0:T(8,128)(2,1)}) %reduce-scatter.3.cloned.1.call-update) | async-done | bytes 524304 | tf_op jit(solution)/shard_map/reduce_scatter | solution.py:143
  383.9 54.9 %reduce-scatter.5.cloned.1.call-done = bf16[16,8192]{1,0:T(8,128)(2,1)} async-done(((bf16[32,8192]{1,0:T(8,128)(2,1)}), bf16[16,8192]{1,0:T(8,128)(2,1)}) %reduce-scatter.5.cloned.1.call-update) | async-done | bytes 262160 | tf_op jit(solution)/shard_map/reduce_scatter | solution.py:144
  438.8 1.7 fusion.12
  (57 shorter events, 1.9 us)
Async XLA Ops:
  6.5 72.2 %all-gather.5.cloned.1.call-start = ((), (), s32[]{:S(2)}) async-start(), calls=%async_computation.2 | async-start | bytes 1769472 | tf_op jit(solution)/shard_map/all_gather | solution.py:103
  9.9 191.5 %all-gather.9.cloned.1.call-start = ((), (), s32[]{:S(2)}) async-start(), calls=%async_computation.4 | async-start | bytes 1179648 | tf_op jit(solution)/shard_map/all_gather | solution.py:103
  12.2 9.2 %collective-permute-start.1 = (bf16[16,8192]{1,0:T(8,128)(2,1)S(1)}, bf16[16,8192]{1,0:T(8,128)(2,1)S(1)}, u32[]{:S(2)}, u32[]{:S(2)}) collective-permute-start(bf16[16,8192]{1,0:T(8,128)(2,1)S(1)} %get-tuple-element.7), channel_id=1, source_target_pairs={{0,2},{2,4},{4,6},{6,0},{1,3},{3,5},{5,7},{7,1},{8,10},{10,12},{12... | collective-permute-start | bytes 786440 | tf_op jit(solution)/shard_map/ppermute | solution.py:85
  16.3 8.2 %collective-permute-start = (bf16[16,8192]{1,0:T(8,128)(2,1)S(1)}, bf16[16,8192]{1,0:T(8,128)(2,1)S(1)}, u32[]{:S(2)}, u32[]{:S(2)}) collective-permute-start(bf16[16,8192]{1,0:T(8,128)(2,1)S(1)} %get-tuple-element.7), channel_id=1, source_target_pairs={{0,6},{2,0},{4,2},{6,4},{1,7},{3,1},{5,3},{7,5},{8,14},{10,8},{12,... | collective-permute-start | bytes 786440 | tf_op jit(solution)/shard_map/ppermute | solution.py:88
  19.6 256.0 %all-gather.7.cloned.1.call-start = ((), (), s32[]{:S(2)}) async-start(), calls=%async_computation.3 | async-start | bytes 7864320 | tf_op jit(solution)/shard_map/all_gather | solution.py:103
  21.4 9.2 %collective-permute-start.2 = (bf16[16,8192]{1,0:T(8,128)(2,1)S(1)}, bf16[16,8192]{1,0:T(8,128)(2,1)S(1)}, u32[]{:S(2)}, u32[]{:S(2)}) collective-permute-start(bf16[16,8192]{1,0:T(8,128)(2,1)S(1)} %collective-permute-done.1), channel_id=1, source_target_pairs={{0,2},{2,4},{4,6},{6,0},{1,3},{3,5},{5,7},{7,1},{8,10},{10,12},{12... | collective-permute-start | bytes 786440 | tf_op jit(solution)/shard_map/ppermute | solution.py:85
  78.7 255.5 %all-gather.11.cloned.1.call-start = ((), (), s32[]{:S(2)}) async-start(), calls=%async_computation.5 | async-start | bytes 5242880 | tf_op jit(solution)/shard_map/all_gather | solution.py:103
  78.9 1.4 copy-start
  80.3 114.8 %collective-permute-start.3 = (bf16[4,16,8192]{2,1,0:T(8,128)(2,1)S(1)}, bf16[4,16,8192]{2,1,0:T(8,128)(2,1)S(1)}, u32[]{:S(2)}, u32[]{:S(2)}) collective-permute-start(bf16[4,16,8192]{2,1,0:T(8,128)(2,1)S(1)} %constant_dynamic-slice_fusion.1), channel_id=1, source_target_pairs={{0,8},{8,0},{1,9},{9,1},{2,10},{10,2},{3,11},{11,3},{4,12},{12,4},... | collective-permute-start | bytes 3145736 | tf_op jit(solution)/shard_map/ppermute | solution.py:85
  197.9 7.0 %collective-permute-start.4 = (bf16[2,4,16,8192]{3,2,1,0:T(8,128)(2,1)}, bf16[2,4,16,8192]{3,2,1,0:T(8,128)(2,1)}, u32[]{:S(2)}, u32[]{:S(2)}) collective-permute-start(bf16[2,4,16,8192]{3,2,1,0:T(8,128)(2,1)} %fusion.5), channel_id=1, source_target_pairs={{0,1},{1,0},{2,3},{3,2},{4,5},{5,4},{6,7},{7,6},{8,9},{9,8},{10,11... | collective-permute-start | bytes 6291464 | tf_op jit(solution)/shard_map/ppermute | solution.py:85
  201.5 182.4 %reduce-scatter.3.cloned.1.call-start = ((), (), s32[]{:S(2)}) async-start(), calls=%async_computation.6 | async-start | bytes 4718592 | tf_op jit(solution)/shard_map/reduce_scatter | solution.py:143
  282.1 12.2 %collective-permute-start.5 = (bf16[64,256]{1,0:T(8,128)(2,1)S(1)}, bf16[64,256]{1,0:T(8,128)(2,1)S(1)}, u32[]{:S(2)}, u32[]{:S(2)}) collective-permute-start(bf16[64,256]{1,0:T(8,128)(2,1)S(1)} %fusion.29), channel_id=1, source_target_pairs={{0,6},{2,0},{4,2},{6,4},{1,7},{3,1},{5,3},{7,5},{8,14},{10,8},{12,... | collective-permute-start | bytes 98312 | tf_op jit(solution)/shard_map/ppermute | solution.py:88
  286.5 5.9 %collective-permute-start.6 = (bf16[64,256]{1,0:T(8,128)(2,1)S(1)}, bf16[64,256]{1,0:T(8,128)(2,1)S(1)}, u32[]{:S(2)}, u32[]{:S(2)}) collective-permute-start(bf16[64,256]{1,0:T(8,128)(2,1)S(1)} %fusion.29), channel_id=1, source_target_pairs={{0,2},{2,4},{4,6},{6,0},{1,3},{3,5},{5,7},{7,1},{8,10},{10,12},{12... | collective-permute-start | bytes 98312 | tf_op jit(solution)/shard_map/ppermute | solution.py:85
  292.4 5.9 %collective-permute-start.7 = (bf16[64,256]{1,0:T(8,128)(2,1)S(1)}, bf16[64,256]{1,0:T(8,128)(2,1)S(1)}, u32[]{:S(2)}, u32[]{:S(2)}) collective-permute-start(bf16[64,256]{1,0:T(8,128)(2,1)S(1)} %collective-permute-done.6), channel_id=1, source_target_pairs={{0,2},{2,4},{4,6},{6,0},{1,3},{3,5},{5,7},{7,1},{8,10},{10,12},{12... | collective-permute-start | bytes 98312 | tf_op jit(solution)/shard_map/ppermute | solution.py:85
  298.3 15.2 %collective-permute-start.8 = (bf16[4,64,256]{2,1,0:T(8,128)(2,1)S(1)}, bf16[4,64,256]{2,1,0:T(8,128)(2,1)S(1)}, u32[]{:S(2)}, u32[]{:S(2)}) collective-permute-start(bf16[4,64,256]{2,1,0:T(8,128)(2,1)S(1)} %constant_dynamic-slice_fusion), channel_id=1, source_target_pairs={{0,8},{8,0},{1,9},{9,1},{2,10},{10,2},{3,11},{11,3},{4,12},{12,4},... | collective-permute-start | bytes 393224 | tf_op jit(solution)/shard_map/ppermute | solution.py:85
  313.7 12.4 %collective-permute-start.9 = (bf16[2,4,64,256]{3,2,1,0:T(8,128)(2,1)S(1)}, bf16[2,4,64,256]{3,2,1,0:T(8,128)(2,1)S(1)}, u32[]{:S(2)}, u32[]{:S(2)}) collective-permute-start(bf16[2,4,64,256]{3,2,1,0:T(8,128)(2,1)S(1)} %fusion.19), channel_id=1, source_target_pairs={{0,1},{1,0},{2,3},{3,2},{4,5},{5,4},{6,7},{7,6},{8,9},{9,8},{10,11... | collective-permute-start | bytes 786440 | tf_op jit(solution)/shard_map/ppermute | solution.py:85
  339.9 98.9 %copy-start.1 = (bf16[16,8192]{1,0:T(8,128)(2,1)S(1)}, bf16[16,8192]{1,0:T(8,128)(2,1)}, u32[]{:S(2)}) copy-start(bf16[16,8192]{1,0:T(8,128)(2,1)} %param.8) | copy-start | bytes 786436
  340.0 98.8 %reduce-scatter.5.cloned.1.call-start = ((), (), s32[]{:S(2)}) async-start(), calls=%async_computation.7 | async-start | bytes 786432 | tf_op jit(solution)/shard_map/reduce_scatter | solution.py:144
Sparse Core Ops, SparseCore 0:
  10.0 68.6 all-gather.4
  80.7 119.5 all-gather.8
  202.4 73.1 all-gather.6
  277.6 56.6 all-gather.10
  340.1 43.7 reduce-scatter.2
  386.5 52.2 reduce-scatter.4

commit v2 on v1

--- a/solution.py
+++ b/solution.py
@@ -92,10 +92,10 @@
 
 
 def group_gather(block):
-    along_y = ring_gather(block, "y", 4)
-    along_zh = ring_gather(along_y, "zh", 2)
-    along_c = ring_gather(along_zh, "c", 2)
-    ordered = jnp.moveaxis(along_c, 0, 2)
+    along_zh = ring_gather(block, "zh", 2)
+    along_y = ring_gather(along_zh, "y", 4)
+    along_c = ring_gather(along_y, "c", 2)
+    ordered = jnp.transpose(along_c, (2, 1, 0) + tuple(range(3, along_c.ndim)))
     return ordered.reshape((-1,) + block.shape[1:])
 
 
@@ -111,6 +111,7 @@
     q_cols = w_query.shape[1]
     k_cols = w_key.shape[1]
     weights = dp_gather(jnp.concatenate([w_query, w_key, w_value], axis=1), 0)
+    weights, w_out = lax.optimization_barrier((weights, w_out))
     projected = jnp.dot(gathered, weights, preferred_element_type=jnp.float32)
     query_part = projected[:, :q_cols]
     kv_part = projected[:, q_cols:].astype(jnp.bfloat16)

time: 448 us -> 429 us (0.958)
  waiting for transfers between devices: 342 us -> 324 us
  local copies, waits for them, and re-layouts: 9.12 us -> 15.9 us
    ppermute x8, waiting for transfers between devices: 126 us -> 36.1 us  [ring_gather(): ahead = lax.ppermute(ahead, axis_name, forward)]
    all_gather x2, waiting for transfers between devices: 48 us -> 114 us  [dp_gather(): lax.all_gather(block, 'zl', axis=axis, tiled=True)]
    all_gather x2, waiting for transfers between devices: 69 us -> 75.2 us  [dp_gather(): lax.all_gather(lax.all_gather(block, 'zl', axis=axis, tiled=True), 'x', a...]
    concatenate x3 -> x1, other arithmetic: 9.45 us -> 5.24 us  [ring_gather(): return jnp.roll(stacked, index, axis=0)]
where the time goes in v2:
time: 429 us
  waiting for transfers between devices  324 us (76%)
  starting transfers between devices  54.1 us (13%)
  local copies, waits for them, and re-layouts  15.9 us (4%)
  other arithmetic  14.8 us (3%)
  between operations  14 us (3%)
  matrix products  6.35 us (1%)
    all_gather x2, waiting for transfers between devices, dp_gather(): lax.all_gather(block, 'zl', axis=axis, tiled=True)  114 us
    all_gather x2, waiting for transfers between devices, dp_gather(): lax.all_gather(lax.all_gather(block, 'zl', axis=axis, tiled=True), 'x', a...  75.2 us
    reduce_scatter x1, waiting for transfers between devices, body(): lax.psum_scatter(summed, 'zh', scatter_dimension=0, tiled=True)  54.9 us
    ppermute x8, starting transfers between devices, ring_gather(): ahead = lax.ppermute(ahead, axis_name, forward)  46.2 us
    reduce_scatter x1, waiting for transfers between devices, body(): lax.psum_scatter(regrouped, ('y', 'c'), scatter_dimension=0, tiled=True)  43.9 us
    ppermute x8, waiting for transfers between devices, ring_gather(): ahead = lax.ppermute(ahead, axis_name, forward)  36.1 us
  transfers between devices with their start and end apart: 16, of which 13 were waited for; matrix products, arithmetic and copies ran while one was open for 6% of the time, Pallas kernels for 0%

profile of v2, /device:TPU:1, one launch (start us, length us, event | category | flops | bytes accessed | tf_op | source)
XLA Modules:
  0.0 428.8 jit_solution(17359271518315427143)
XLA Ops:
  6.5 1.1 fusion.6
  7.7 1.1 fusion.8
  8.8 16.3 %collective-permute-start = (bf16[16,8192]{1,0:T(8,128)(2,1)S(1)}, bf16[16,8192]{1,0:T(8,128)(2,1)S(1)}, u32[]{:S(2)}, u32[]{:S(2)}) collective-permute-start(bf16[16,8192]{1,0:T(8,128)(2,1)S(1)} %fusion.8), channel_id=1, source_target_pairs={{0,8},{8,0},{1,9},{9,1},{2,10},{10,2},{3,11},{11,3},{4,12},{12,4},... | collective-permute-start | bytes 786440 | tf_op jit(solution)/shard_map/ppermute | solution.py:85
  25.0 1.1 fusion.41
  26.2 4.1 collective-permute-done
  30.3 1.1 bitcast_dynamic-update-slice_fusion.6
  31.4 3.9 collective-permute-start.2
  35.4 3.4 collective-permute-start.1
  38.8 0.8 copy.30
  39.6 0.8 copy.31
  40.4 1.7 pad_maximum_fusion.1
  42.2 4.9 %collective-permute-done.2 = bf16[2,16,8192]{2,1,0:T(8,128)(2,1)S(1)} collective-permute-done((bf16[2,16,8192]{2,1,0:T(8,128)(2,1)S(1)}, bf16[2,16,8192]{2,1,0:T(8,128)(2,1)S(1)}, u32[]{:S(2)}, u32[]{:S(2)}) %collective-permute-start.2) | collective-permute-done | bytes 524320 | tf_op jit(solution)/shard_map/ppermute | solution.py:85
  47.1 2.1 collective-permute-start.3
  49.2 0.9 bitcast_dynamic-update-slice_fusion.2
  50.1 10.9 %collective-permute-done.3 = bf16[2,16,8192]{2,1,0:T(8,128)(2,1)S(1)} collective-permute-done((bf16[2,16,8192]{2,1,0:T(8,128)(2,1)S(1)}, bf16[2,16,8192]{2,1,0:T(8,128)(2,1)S(1)}, u32[]{:S(2)}, u32[]{:S(2)}) %collective-permute-start.3) | collective-permute-done | bytes 524320 | tf_op jit(solution)/shard_map/ppermute | solution.py:85
  61.0 0.8 bitcast_dynamic-update-slice_fusion
  61.8 60.5 %all-gather.5.cloned.1.call-done = bf16[2048,320]{1,0:T(8,128)(2,1)} async-done(((bf16[256,320]{1,0:T(8,128)(2,1)}), bf16[2048,320]{1,0:T(8,128)(2,1)}) %all-gather.5.cloned.1.call-update) | async-done | bytes 1310736 | tf_op jit(solution)/shard_map/all_gather | solution.py:103
  122.4 0.8 bitcast_dynamic-update-slice_fusion.4
  123.2 0.8 bitcast_dynamic-update-slice_fusion.7
  124.1 0.8 bitcast_dynamic-update-slice_fusion.3
  124.9 0.8 bitcast_dynamic-update-slice_fusion.1
  125.7 0.9 bitcast_dynamic-update-slice_fusion.5
  126.6 72.6 %all-gather.7.cloned.1.call-done = bf16[8192,320]{1,0:T(8,128)(2,1)} async-done(((bf16[2048,320]{1,0:T(8,128)(2,1)}), bf16[8192,320]{1,0:T(8,128)(2,1)}) %all-gather.7.cloned.1.call-update) | async-done | bytes 5242896 | tf_op jit(solution)/shard_map/all_gather | solution.py:103
  199.3 1.7 constant_dynamic-slice_fusion.1
  201.0 2.6 collective-permute-start.4
  203.8 0.5 multiply_cosine_fusion
  204.3 53.0 %all-gather.9.cloned.1.call-done = bf16[256,2048]{1,0:T(8,128)(2,1)} async-done(((bf16[256,256]{1,0:T(8,128)(2,1)}), bf16[256,2048]{1,0:T(8,128)(2,1)}) %all-gather.9.cloned.1.call-update) | async-done | bytes 1048592 | tf_op jit(solution)/shard_map/all_gather | solution.py:103
  257.4 1.9 fusion.40
  259.3 5.2 %fusion.2 = bf16[2,4,2,16,8192]{4,3,0,1,2:T(8,128)(2,1)S(1)} fusion(s32[]{:T(128)S(6)} %select_n.97, bf16[1,4,2,16,8192]{4,3,0,1,2:T(8,128)(2,1)S(1)} %fusion.40, bf16[1,4,2,16,8192]{4,3,0,1,2:T(8,128)(2,1)} %bitcast.11), kind=kLoop, calls=%fused_computation.9 | loop fusion | flops 6291456 | bytes 8388612 | tf_op jit(solution)/shard_map/jit(_roll_dynamic)/concatenate | solution.py:91
  264.6 2.5 fusion.34
  267.1 7.3 %collective-permute-start.5 = (bf16[64,256]{1,0:T(8,128)(2,1)S(1)}, bf16[64,256]{1,0:T(8,128)(2,1)S(1)}, u32[]{:S(2)}, u32[]{:S(2)}) collective-permute-start(bf16[64,256]{1,0:T(8,128)(2,1)S(1)} %get-tuple-element.21), channel_id=1, source_target_pairs={{0,8},{8,0},{1,9},{9,1},{2,10},{10,2},{3,11},{11,3},{4,12},{12,4},... | collective-permute-start | bytes 98312 | tf_op jit(solution)/shard_map/ppermute | solution.py:85
  274.5 6.0 %collective-permute-done.5 = bf16[64,256]{1,0:T(8,128)(2,1)S(1)} collective-permute-done((bf16[64,256]{1,0:T(8,128)(2,1)S(1)}, bf16[64,256]{1,0:T(8,128)(2,1)S(1)}, u32[]{:S(2)}, u32[]{:S(2)}) %collective-permute-start.5) | collective-permute-done | bytes 32800 | tf_op jit(solution)/shard_map/ppermute | solution.py:85
  280.5 4.4 %collective-permute-start.6 = (bf16[2,64,256]{2,1,0:T(8,128)(2,1)S(1)}, bf16[2,64,256]{2,1,0:T(8,128)(2,1)S(1)}, u32[]{:S(2)}, u32[]{:S(2)}) collective-permute-start(bf16[2,64,256]{2,1,0:T(8,128)(2,1)S(1)} %get-tuple-element.11), channel_id=1, source_target_pairs={{0,6},{2,0},{4,2},{6,4},{1,7},{3,1},{5,3},{7,5},{8,14},{10,8},{12,... | collective-permute-start | bytes 196616 | tf_op jit(solution)/shard_map/ppermute | solution.py:88
  284.9 1.9 collective-permute-start.7
  287.1 4.4 %collective-permute-done.7 = bf16[2,64,256]{2,1,0:T(8,128)(2,1)S(1)} collective-permute-done((bf16[2,64,256]{2,1,0:T(8,128)(2,1)S(1)}, bf16[2,64,256]{2,1,0:T(8,128)(2,1)S(1)}, u32[]{:S(2)}, u32[]{:S(2)}) %collective-permute-start.7) | collective-permute-done | bytes 65568 | tf_op jit(solution)/shard_map/ppermute | solution.py:85
  291.5 1.9 collective-permute-start.8
  293.4 4.8 %collective-permute-done.8 = bf16[2,64,256]{2,1,0:T(8,128)(2,1)S(1)} collective-permute-done((bf16[2,64,256]{2,1,0:T(8,128)(2,1)S(1)}, bf16[2,64,256]{2,1,0:T(8,128)(2,1)S(1)}, u32[]{:S(2)}, u32[]{:S(2)}) %collective-permute-start.8) | collective-permute-done | bytes 65568 | tf_op jit(solution)/shard_map/ppermute | solution.py:85
  298.4 10.1 %collective-permute-start.9 = (bf16[4,2,64,256]{3,2,1,0:T(8,128)(2,1)S(1)}, bf16[4,2,64,256]{3,2,1,0:T(8,128)(2,1)S(1)}, u32[]{:S(2)}, u32[]{:S(2)}) collective-permute-start(bf16[4,2,64,256]{3,2,1,0:T(8,128)(2,1)S(1)} %constant_dynamic-slice_fusion), channel_id=1, source_target_pairs={{0,1},{1,0},{2,3},{3,2},{4,5},{5,4},{6,7},{7,6},{8,9},{9,8},{10,11... | collective-permute-start | bytes 786440 | tf_op jit(solution)/shard_map/ppermute | solution.py:85
  308.7 0.9 collective-permute-done.9
  309.6 0.4 fusion.13
  311.2 0.6 gather_fusion.1
  311.8 0.6 gather_fusion
  313.1 2.6 all-gather.11.cloned.1.call-done
  315.6 3.4 convolution_convert_fusion
  319.1 2.2 copy.42
  321.4 43.9 %reduce-scatter.3.cloned.1.call-done = bf16[32,8192]{1,0:T(8,128)(2,1)} async-done(((bf16[256,8192]{1,0:T(8,128)(2,1)}), bf16[32,8192]{1,0:T(8,128)(2,1)}) %reduce-scatter.3.cloned.1.call-update) | async-done | bytes 524304 | tf_op jit(solution)/shard_map/reduce_scatter | solution.py:144
  365.3 54.9 %reduce-scatter.5.cloned.1.call-done = bf16[16,8192]{1,0:T(8,128)(2,1)} async-done(((bf16[32,8192]{1,0:T(8,128)(2,1)}), bf16[16,8192]{1,0:T(8,128)(2,1)}) %reduce-scatter.5.cloned.1.call-update) | async-done | bytes 262160 | tf_op jit(solution)/shard_map/reduce_scatter | solution.py:145
  420.2 1.7 fusion.9
  (58 shorter events, 2.9 us)
Async XLA Ops:
  6.5 115.8 %all-gather.5.cloned.1.call-start = ((), (), s32[]{:S(2)}) async-start(), calls=%async_computation.2 | async-start | bytes 1769472 | tf_op jit(solution)/shard_map/all_gather | solution.py:103
  8.8 21.5 %collective-permute-start = (bf16[16,8192]{1,0:T(8,128)(2,1)S(1)}, bf16[16,8192]{1,0:T(8,128)(2,1)S(1)}, u32[]{:S(2)}, u32[]{:S(2)}) collective-permute-start(bf16[16,8192]{1,0:T(8,128)(2,1)S(1)} %fusion.8), channel_id=1, source_target_pairs={{0,8},{8,0},{1,9},{9,1},{2,10},{10,2},{3,11},{11,3},{4,12},{12,4},... | collective-permute-start | bytes 786440 | tf_op jit(solution)/shard_map/ppermute | solution.py:85
  31.4 15.6 %collective-permute-start.2 = (bf16[2,16,8192]{2,1,0:T(8,128)(2,1)S(1)}, bf16[2,16,8192]{2,1,0:T(8,128)(2,1)S(1)}, u32[]{:S(2)}, u32[]{:S(2)}) collective-permute-start(bf16[2,16,8192]{2,1,0:T(8,128)(2,1)S(1)} %get-tuple-element.13), channel_id=1, source_target_pairs={{0,2},{2,4},{4,6},{6,0},{1,3},{3,5},{5,7},{7,1},{8,10},{10,12},{12... | collective-permute-start | bytes 1572872 | tf_op jit(solution)/shard_map/ppermute | solution.py:85
  35.4 13.8 %collective-permute-start.1 = (bf16[2,16,8192]{2,1,0:T(8,128)(2,1)S(1)}, bf16[2,16,8192]{2,1,0:T(8,128)(2,1)S(1)}, u32[]{:S(2)}, u32[]{:S(2)}) collective-permute-start(bf16[2,16,8192]{2,1,0:T(8,128)(2,1)S(1)} %get-tuple-element.13), channel_id=1, source_target_pairs={{0,6},{2,0},{4,2},{6,4},{1,7},{3,1},{5,3},{7,5},{8,14},{10,8},{12,... | collective-permute-start | bytes 1572872 | tf_op jit(solution)/shard_map/ppermute | solution.py:88
  42.1 157.1 %all-gather.7.cloned.1.call-start = ((), (), s32[]{:S(2)}) async-start(), calls=%async_computation.3 | async-start | bytes 7864320 | tf_op jit(solution)/shard_map/all_gather | solution.py:103
  47.1 13.9 %collective-permute-start.3 = (bf16[2,16,8192]{2,1,0:T(8,128)(2,1)S(1)}, bf16[2,16,8192]{2,1,0:T(8,128)(2,1)S(1)}, u32[]{:S(2)}, u32[]{:S(2)}) collective-permute-start(bf16[2,16,8192]{2,1,0:T(8,128)(2,1)S(1)} %collective-permute-done.2), channel_id=1, source_target_pairs={{0,2},{2,4},{4,6},{6,0},{1,3},{3,5},{5,7},{7,1},{8,10},{10,12},{12... | collective-permute-start | bytes 1572872 | tf_op jit(solution)/shard_map/ppermute | solution.py:85
  122.4 134.9 %all-gather.9.cloned.1.call-start = ((), (), s32[]{:S(2)}) async-start(), calls=%async_computation.4 | async-start | bytes 1179648 | tf_op jit(solution)/shard_map/all_gather | solution.py:103
  199.2 116.4 %all-gather.11.cloned.1.call-start = ((), (), s32[]{:S(2)}) async-start(), calls=%async_computation.5 | async-start | bytes 5242880 | tf_op jit(solution)/shard_map/all_gather | solution.py:103
  201.0 58.3 %collective-permute-start.4 = (bf16[4,2,16,8192]{3,2,0,1:T(8,128)(2,1)S(1)}, bf16[4,2,16,8192]{3,2,0,1:T(8,128)(2,1)}, u32[]{:S(2)}, u32[]{:S(2)}) collective-permute-start(bf16[4,2,16,8192]{3,2,0,1:T(8,128)(2,1)S(1)} %constant_dynamic-slice_fusion.1), channel_id=1, source_target_pairs={{0,1},{1,0},{2,3},{3,2},{4,5},{5,4},{6,7},{7,6},{8,9},{9,8},{10,11... | collective-permute-start | bytes 6291464 | tf_op jit(solution)/shard_map/ppermute | solution.py:85
  257.3 108.0 %reduce-scatter.3.cloned.1.call-start = ((), (), s32[]{:S(2)}) async-start(), calls=%async_computation.6 | async-start | bytes 4718592 | tf_op jit(solution)/shard_map/reduce_scatter | solution.py:144
  257.4 7.2 %slice-start = ((s8[6291456]{0:T(1024)(128)(4,1)}), s8[4194304]{0:T(1024)(128)(4,1)S(1)}, s32[]{:S(2)}) async-start(s8[6291456]{0:T(1024)(128)(4,1)} %bitcast.94), calls=%async_computation.8 | async-start | bytes 8388608
  259.3 5.3 %slice-start.1 = ((s8[6291456]{0:T(1024)(128)(4,1)}), s8[2097152]{0:T(1024)(128)(4,1)S(1)}, s32[]{:S(2)}) async-start(s8[6291456]{0:T(1024)(128)(4,1)} %bitcast.94), calls=%async_computation.9 | async-start | bytes 4194304
  267.1 13.4 %collective-permute-start.5 = (bf16[64,256]{1,0:T(8,128)(2,1)S(1)}, bf16[64,256]{1,0:T(8,128)(2,1)S(1)}, u32[]{:S(2)}, u32[]{:S(2)}) collective-permute-start(bf16[64,256]{1,0:T(8,128)(2,1)S(1)} %get-tuple-element.21), channel_id=1, source_target_pairs={{0,8},{8,0},{1,9},{9,1},{2,10},{10,2},{3,11},{11,3},{4,12},{12,4},... | collective-permute-start | bytes 98312 | tf_op jit(solution)/shard_map/ppermute | solution.py:85
  280.5 12.9 %collective-permute-start.6 = (bf16[2,64,256]{2,1,0:T(8,128)(2,1)S(1)}, bf16[2,64,256]{2,1,0:T(8,128)(2,1)S(1)}, u32[]{:S(2)}, u32[]{:S(2)}) collective-permute-start(bf16[2,64,256]{2,1,0:T(8,128)(2,1)S(1)} %get-tuple-element.11), channel_id=1, source_target_pairs={{0,6},{2,0},{4,2},{6,4},{1,7},{3,1},{5,3},{7,5},{8,14},{10,8},{12,... | collective-permute-start | bytes 196616 | tf_op jit(solution)/shard_map/ppermute | solution.py:88
  284.9 6.6 %collective-permute-start.7 = (bf16[2,64,256]{2,1,0:T(8,128)(2,1)S(1)}, bf16[2,64,256]{2,1,0:T(8,128)(2,1)S(1)}, u32[]{:S(2)}, u32[]{:S(2)}) collective-permute-start(bf16[2,64,256]{2,1,0:T(8,128)(2,1)S(1)} %get-tuple-element.11), channel_id=1, source_target_pairs={{0,2},{2,4},{4,6},{6,0},{1,3},{3,5},{5,7},{7,1},{8,10},{10,12},{12... | collective-permute-start | bytes 196616 | tf_op jit(solution)/shard_map/ppermute | solution.py:85
  291.5 6.8 %collective-permute-start.8 = (bf16[2,64,256]{2,1,0:T(8,128)(2,1)S(1)}, bf16[2,64,256]{2,1,0:T(8,128)(2,1)S(1)}, u32[]{:S(2)}, u32[]{:S(2)}) collective-permute-start(bf16[2,64,256]{2,1,0:T(8,128)(2,1)S(1)} %collective-permute-done.7), channel_id=1, source_target_pairs={{0,2},{2,4},{4,6},{6,0},{1,3},{3,5},{5,7},{7,1},{8,10},{10,12},{12... | collective-permute-start | bytes 196616 | tf_op jit(solution)/shard_map/ppermute | solution.py:85
  298.4 11.3 %collective-permute-start.9 = (bf16[4,2,64,256]{3,2,1,0:T(8,128)(2,1)S(1)}, bf16[4,2,64,256]{3,2,1,0:T(8,128)(2,1)S(1)}, u32[]{:S(2)}, u32[]{:S(2)}) collective-permute-start(bf16[4,2,64,256]{3,2,1,0:T(8,128)(2,1)S(1)} %constant_dynamic-slice_fusion), channel_id=1, source_target_pairs={{0,1},{1,0},{2,3},{3,2},{4,5},{5,4},{6,7},{7,6},{8,9},{9,8},{10,11... | collective-permute-start | bytes 786440 | tf_op jit(solution)/shard_map/ppermute | solution.py:85
  321.3 98.9 %copy-start = (bf16[16,8192]{1,0:T(8,128)(2,1)S(1)}, bf16[16,8192]{1,0:T(8,128)(2,1)}, u32[]{:S(2)}) copy-start(bf16[16,8192]{1,0:T(8,128)(2,1)} %param.8) | copy-start | bytes 786436
  321.4 98.8 %reduce-scatter.5.cloned.1.call-start = ((), (), s32[]{:S(2)}) async-start(), calls=%async_computation.7 | async-start | bytes 786432 | tf_op jit(solution)/shard_map/reduce_scatter | solution.py:145
Sparse Core Ops, SparseCore 0:
  42.3 80.0 all-gather.4
  124.4 74.7 all-gather.6
  201.2 56.0 all-gather.8
  259.3 56.3 all-gather.10
  321.5 43.7 reduce-scatter.2
  367.9 52.2 reduce-scatter.4

commit v3 on v2

--- a/solution.py
+++ b/solution.py
@@ -99,8 +99,28 @@
     return ordered.reshape((-1,) + block.shape[1:])
 
 
-def dp_gather(block, axis):
-    return lax.all_gather(lax.all_gather(block, "zl", axis=axis, tiled=True), "x", axis=axis, tiled=True)
+def dp_gather(block):
+    along_x = ring_gather(block, "x", 4)
+    return lax.all_gather(along_x, "zl", axis=1)
+
+
+def take(array, index, axis):
+    return lax.dynamic_index_in_dim(array, index, axis=axis, keepdims=False)
+
+
+def group_reduce_scatter(partial):
+    c_index = lax.axis_index("c")
+    y_index = lax.axis_index("y")
+    zh_index = lax.axis_index("zh")
+    swap = [(0, 1), (1, 0)]
+    sent = lax.ppermute(take(partial, 1 - c_index, 2), "c", swap)
+    acc = take(partial, c_index, 2).astype(jnp.float32) + sent.astype(jnp.float32)
+    mine = take(acc, y_index, 1)
+    for shift in range(1, 4):
+        outgoing = take(acc, (y_index + shift) % 4, 1).astype(jnp.bfloat16)
+        mine = mine + lax.ppermute(outgoing, "y", [(s, (s + shift) % 4) for s in range(4)]).astype(jnp.float32)
+    sent = lax.ppermute(take(mine, 1 - zh_index, 0).astype(jnp.bfloat16), "zh", swap)
+    return take(mine, zh_index, 0) + sent.astype(jnp.float32)
 
 
 def body(tokens, norm_gain, w_query, w_key, w_value, w_out):
@@ -110,7 +130,8 @@
     row_count = gathered.shape[0]
     q_cols = w_query.shape[1]
     k_cols = w_key.shape[1]
-    weights = dp_gather(jnp.concatenate([w_query, w_key, w_value], axis=1), 0)
+    weights = dp_gather(jnp.concatenate([w_query, w_key, w_value], axis=1))
+    weights = weights.reshape(-1, weights.shape[-1])
     weights, w_out = lax.optimization_barrier((weights, w_out))
     projected = jnp.dot(gathered, weights, preferred_element_type=jnp.float32)
     query_part = projected[:, :q_cols]
@@ -135,14 +156,12 @@
     key_heads = jnp.take(key_heads, owner, axis=1)
     value_heads = jnp.take(value_heads, owner, axis=1)
     mixed = attend(queries, key_heads, value_heads, SEQ)
-    partial_out = jnp.dot(
-        mixed, dp_gather(w_out, 1), preferred_element_type=jnp.float32
+    out_weights = dp_gather(w_out)
+    partial_out = jnp.einsum(
+        "rk,xzkc->rxzc", mixed, out_weights, preferred_element_type=jnp.float32
     ).astype(jnp.bfloat16)
-    width = partial_out.shape[1]
-    regrouped = partial_out.reshape(2, -1, row_count // 16, width).transpose(1, 0, 2, 3)
-    regrouped = regrouped.reshape(row_count, width)
-    summed = lax.psum_scatter(regrouped, ("y", "c"), scatter_dimension=0, tiled=True)
-    summed = lax.psum_scatter(summed, "zh", scatter_dimension=0, tiled=True).astype(jnp.float32)
+    width = partial_out.shape[1] * partial_out.shape[2] * partial_out.shape[3]
+    summed = group_reduce_scatter(partial_out.reshape(2, 4, 2, row_count // 16, width))
     return (tokens.astype(jnp.float32) + summed).astype(jnp.bfloat16)
 
 

time: 429 us -> 441 us (1.028)
  waiting for transfers between devices: 324 us -> 270 us
  starting transfers between devices: 54.1 us -> 91.4 us
  local copies, waits for them, and re-layouts: 15.9 us -> 39.7 us
    reduce_scatter x2 -> x0, waiting for transfers between devices: 98.8 us -> none  [the longest x1 54.9 us: body(): lax.psum_scatter(summed, 'zh', scatter_dimension=0, tiled=True)]
    ppermute x0 -> x5, waiting for transfers between devices: none -> 50.2 us  [the longest x1 27 us: group_reduce_scatter(): lax.ppermute(take(mine, 1 - zh_index, 0).astype(jnp.bfloat16), 'zh', swap)]
    ppermute x0 -> x5, starting transfers between devices: none -> 19.2 us  [the longest x3 10.5 us: group_reduce_scatter(): lax.ppermute(outgoing, 'y', [(s, (s + shift) % 4) for s in range(4)])]
    all_gather x4 -> x2, waiting for transfers between devices: 189 us -> 177 us  [dp_gather(): return lax.all_gather(along_x, 'zl', axis=1)]
    ppermute x8 -> x12, starting transfers between devices: 46.2 us -> 55.5 us  [ring_gather(): ahead = lax.ppermute(ahead, axis_name, forward)]
    ppermute x2 -> x4, starting transfers between devices: 7.72 us -> 16.6 us  [ring_gather(): behind = lax.ppermute(behind, axis_name, backward)]
    reshape x0 -> x2, local copies, waits for them, and re-layouts: none -> 7.5 us  [the longest x1 7.41 us: body(): partial_out.reshape(2, 4, 2, row_count // 16, width)]
    unnamed x22 -> x39, local copies, waits for them, and re-layouts: 7.02 us -> 13.3 us
  transfers between devices with their start and end apart: 16 -> 23, of which waited for: 13 -> 16; matrix products, arithmetic and copies ran while one was open for 6% -> 8% of each run, Pallas kernels for 0% -> 0%
where the time goes in v3:
time: 441 us; the launch traced here: 439 us
  waiting for transfers between devices  270 us (61%)
  starting transfers between devices  91.4 us (21%)
  local copies, waits for them, and re-layouts  39.7 us (9%)
  other arithmetic  17.3 us (4%)
  between operations  14.2 us (3%)
  matrix products  6.34 us (1%)
    all_gather x2, waiting for transfers between devices, dp_gather(): return lax.all_gather(along_x, 'zl', axis=1)  177 us
    ppermute x12, starting transfers between devices, ring_gather(): ahead = lax.ppermute(ahead, axis_name, forward)  55.5 us
    ppermute x12, waiting for transfers between devices, ring_gather(): ahead = lax.ppermute(ahead, axis_name, forward)  42 us
    ppermute x1, waiting for transfers between devices, group_reduce_scatter(): lax.ppermute(take(mine, 1 - zh_index, 0).astype(jnp.bfloat16), 'zh', swap)  27 us
    ppermute x3, waiting for transfers between devices, group_reduce_scatter(): lax.ppermute(outgoing, 'y', [(s, (s + shift) % 4) for s in range(4)])  19.1 us
    ppermute x4, starting transfers between devices, ring_gather(): behind = lax.ppermute(behind, axis_name, backward)  16.6 us
    unnamed x39, local copies, waits for them, and re-layouts  13.3 us
    ppermute x3, starting transfers between devices, group_reduce_scatter(): lax.ppermute(outgoing, 'y', [(s, (s + shift) % 4) for s in range(4)])  10.5 us
  transfers between devices with their start and end apart: 23, of which 16 were waited for; matrix products, arithmetic and copies ran while one was open for 8% of the time, Pallas kernels for 0%

profile of v3, /device:TPU:1, one launch (start us, length us, event | category | flops | bytes accessed | tf_op | source)
XLA Modules:
  0.0 438.6 jit_solution(11810966377740639772)
XLA Ops:
  8.2 1.7 bitcast_dynamic-update-slice_fusion.14
  9.9 3.9 collective-permute-start.6
  13.8 3.2 collective-permute-start.5
  19.3 15.6 %collective-permute-start = (bf16[16,8192]{1,0:T(8,128)(2,1)S(1)}, bf16[16,8192]{1,0:T(8,128)(2,1)S(1)}, u32[]{:S(2)}, u32[]{:S(2)}) collective-permute-start(bf16[16,8192]{1,0:T(8,128)(2,1)S(1)} %fusion.10), channel_id=1, source_target_pairs={{0,8},{8,0},{1,9},{9,1},{2,10},{10,2},{3,11},{11,3},{4,12},{12,4},... | collective-permute-start | bytes 786440 | tf_op jit(solution)/shard_map/ppermute | solution.py:85
  36.1 1.9 collective-permute-start.7
  38.8 1.4 collective-permute-done
  41.3 4.7 %collective-permute-start.1 = (bf16[2,16,8192]{2,1,0:T(8,128)(2,1)S(1)}, bf16[2,16,8192]{2,1,0:T(8,128)(2,1)S(1)}, u32[]{:S(2)}, u32[]{:S(2)}) collective-permute-start(bf16[2,16,8192]{2,1,0:T(8,128)(2,1)S(1)} %get-tuple-element.13), channel_id=1, source_target_pairs={{0,6},{2,0},{4,2},{6,4},{1,7},{3,1},{5,3},{7,5},{8,14},{10,8},{12,... | collective-permute-start | bytes 1572872 | tf_op jit(solution)/shard_map/ppermute | solution.py:88
  46.0 1.9 collective-permute-start.2
  52.2 2.1 constant_dynamic-slice_fusion.4
  54.4 3.6 collective-permute-done.2
  58.0 1.9 collective-permute-start.3
  60.8 8.3 %collective-permute-done.3 = bf16[2,16,8192]{2,1,0:T(8,128)(2,1)S(1)} collective-permute-done((bf16[2,16,8192]{2,1,0:T(8,128)(2,1)S(1)}, bf16[2,16,8192]{2,1,0:T(8,128)(2,1)S(1)}, u32[]{:S(2)}, u32[]{:S(2)}) %collective-permute-start.3) | collective-permute-done | bytes 524320 | tf_op jit(solution)/shard_map/ppermute | solution.py:85
  74.1 1.7 constant_dynamic-slice_fusion.5
  75.8 8.6 %collective-permute-start.4 = (bf16[4,2,16,8192]{3,2,0,1:T(8,128)(2,1)S(1)}, bf16[4,2,16,8192]{3,2,0,1:T(8,128)(2,1)}, u32[]{:S(2)}, u32[]{:S(2)}) collective-permute-start(bf16[4,2,16,8192]{3,2,0,1:T(8,128)(2,1)S(1)} %constant_dynamic-slice_fusion.5), channel_id=1, source_target_pairs={{0,1},{1,0},{2,3},{3,2},{4,5},{5,4},{6,7},{7,6},{8,9},{9,8},{10,11... | collective-permute-start | bytes 6291464 | tf_op jit(solution)/shard_map/ppermute | solution.py:85
  84.4 130.9 %all-gather.5.cloned.1.call-done = bf16[4,2048,320]{2,1,0:T(8,128)(2,1)} async-done(((bf16[4,256,320]{2,1,0:T(8,128)(2,1)}), bf16[4,2048,320]{2,1,0:T(8,128)(2,1)}) %all-gather.5.cloned.1.call-update) | async-done | bytes 5242896 | tf_op jit(solution)/shard_map/all_gather | solution.py:104
  215.3 4.3 collective-permute-start.13
  219.7 1.9 collective-permute-start.14
  221.6 5.0 %collective-permute-done.14 = bf16[256,256]{1,0:T(8,128)(2,1)S(1)} collective-permute-done((bf16[256,256]{1,0:T(8,128)(2,1)S(1)}, bf16[256,256]{1,0:T(8,128)(2,1)S(1)}, u32[]{:S(2)}, u32[]{:S(2)}) %collective-permute-start.14) | collective-permute-done | bytes 131104 | tf_op jit(solution)/shard_map/ppermute | solution.py:85
  226.6 1.9 collective-permute-start.15
  228.6 5.0 %collective-permute-done.15 = bf16[256,256]{1,0:T(8,128)(2,1)S(1)} collective-permute-done((bf16[256,256]{1,0:T(8,128)(2,1)S(1)}, bf16[256,256]{1,0:T(8,128)(2,1)S(1)}, u32[]{:S(2)}, u32[]{:S(2)}) %collective-permute-start.15) | collective-permute-done | bytes 131104 | tf_op jit(solution)/shard_map/ppermute | solution.py:85
  235.1 1.9 fusion.45
  237.0 5.2 %fusion.2 = bf16[2,4,2,16,8192]{4,3,0,1,2:T(8,128)(2,1)S(1)} fusion(s32[]{:T(128)S(6)} %select_n.154, bf16[1,4,2,16,8192]{4,3,0,1,2:T(8,128)(2,1)S(1)} %fusion.45, bf16[1,4,2,16,8192]{4,3,0,1,2:T(8,128)(2,1)} %bitcast.11), kind=kLoop, calls=%fused_computation.8 | loop fusion | flops 6291456 | bytes 8388612 | tf_op jit(solution)/shard_map/jit(_roll_dynamic)/concatenate | solution.py:91
  242.2 2.5 fusion.39
  244.7 5.1 %collective-permute-start.8 = (bf16[64,256]{1,0:T(8,128)(2,1)S(1)}, bf16[64,256]{1,0:T(8,128)(2,1)S(1)}, u32[]{:S(2)}, u32[]{:S(2)}) collective-permute-start(bf16[64,256]{1,0:T(8,128)(2,1)S(1)} %get-tuple-element.28), channel_id=1, source_target_pairs={{0,8},{8,0},{1,9},{9,1},{2,10},{10,2},{3,11},{11,3},{4,12},{12,4},... | collective-permute-start | bytes 98312 | tf_op jit(solution)/shard_map/ppermute | solution.py:85
  249.8 8.9 %collective-permute-done.8 = bf16[64,256]{1,0:T(8,128)(2,1)S(1)} collective-permute-done((bf16[64,256]{1,0:T(8,128)(2,1)S(1)}, bf16[64,256]{1,0:T(8,128)(2,1)S(1)}, u32[]{:S(2)}, u32[]{:S(2)}) %collective-permute-start.8) | collective-permute-done | bytes 32800 | tf_op jit(solution)/shard_map/ppermute | solution.py:85
  258.7 4.4 collective-permute-start.9
  263.1 1.9 collective-permute-start.10
  265.3 4.4 %collective-permute-done.10 = bf16[2,64,256]{2,1,0:T(8,128)(2,1)S(1)} collective-permute-done((bf16[2,64,256]{2,1,0:T(8,128)(2,1)S(1)}, bf16[2,64,256]{2,1,0:T(8,128)(2,1)S(1)}, u32[]{:S(2)}, u32[]{:S(2)}) %collective-permute-start.10) | collective-permute-done | bytes 65568 | tf_op jit(solution)/shard_map/ppermute | solution.py:85
  269.7 1.9 collective-permute-start.11
  271.7 4.7 %collective-permute-done.11 = bf16[2,64,256]{2,1,0:T(8,128)(2,1)S(1)} collective-permute-done((bf16[2,64,256]{2,1,0:T(8,128)(2,1)S(1)}, bf16[2,64,256]{2,1,0:T(8,128)(2,1)S(1)}, u32[]{:S(2)}, u32[]{:S(2)}) %collective-permute-start.11) | collective-permute-done | bytes 65568 | tf_op jit(solution)/shard_map/ppermute | solution.py:85
  276.5 8.9 %collective-permute-start.12 = (bf16[4,2,64,256]{3,2,1,0:T(8,128)(2,1)S(1)}, bf16[4,2,64,256]{3,2,1,0:T(8,128)(2,1)S(1)}, u32[]{:S(2)}, u32[]{:S(2)}) collective-permute-start(bf16[4,2,64,256]{3,2,1,0:T(8,128)(2,1)S(1)} %constant_dynamic-slice_fusion.3), channel_id=1, source_target_pairs={{0,1},{1,0},{2,3},{3,2},{4,5},{5,4},{6,7},{7,6},{8,9},{9,8},{10,11... | collective-permute-start | bytes 786440 | tf_op jit(solution)/shard_map/ppermute | solution.py:85
  289.9 46.4 %all-gather.7.cloned.1.call-done = bf16[4,2048,256]{2,1,0:T(8,128)(2,1)} async-done(((bf16[4,256,256]{2,1,0:T(8,128)(2,1)}), bf16[4,2048,256]{2,1,0:T(8,128)(2,1)}) %all-gather.7.cloned.1.call-update) | async-done | bytes 4194320 | tf_op jit(solution)/shard_map/all_gather | solution.py:104
  336.3 3.4 convolution_convert_fusion
  339.8 4.4 %copy.43 = bf16[256,4,8,256]{3,2,1,0:T(8,128)(2,1)} copy(bf16[256,4,8,256]{3,0,2,1:T(8,128)(2,1)S(1)} %convolution_convert_fusion) | data formatting | bytes 8388608 | tf_op jit(solution)/shard_map/convert_element_type | solution.py:162
  344.2 7.4 %reshape.143 = bf16[2,4,2,16,8192]{4,3,2,1,0:T(8,128)(2,1)} reshape(bf16[256,4,8,256]{3,2,1,0:T(8,128)(2,1)} %copy.43) | data formatting | bytes 8388608 | tf_op jit(solution)/shard_map/reshape | solution.py:164
  351.6 2.6 constant_dynamic-slice_fusion.1
  354.2 1.5 copy.63
  355.7 2.4 collective-permute-start.16
  358.1 4.1 collective-permute-done.16
  362.2 2.1 convert_add_fusion
  364.3 2.0 copy-done
  366.5 3.1 collective-permute-start.17
  369.6 4.3 collective-permute-start.18
  373.9 3.1 collective-permute-start.19
  377.0 5.7 %collective-permute-done.17 = bf16[2,16,8192]{2,1,0:T(8,128)(2,1)S(1)} collective-permute-done((bf16[2,16,8192]{2,1,0:T(8,128)(2,1)S(1)}, bf16[2,16,8192]{2,1,0:T(8,128)(2,1)S(1)}, u32[]{:S(2)}, u32[]{:S(2)}) %collective-permute-start.17) | collective-permute-done | bytes 524320 | tf_op jit(solution)/shard_map/ppermute | solution.py:121
  382.7 12.2 %collective-permute-done.18 = bf16[2,16,8192]{2,1,0:T(8,128)(2,1)S(1)} collective-permute-done((bf16[2,16,8192]{2,1,0:T(8,128)(2,1)S(1)}, bf16[2,16,8192]{2,1,0:T(8,128)(2,1)S(1)}, u32[]{:S(2)}, u32[]{:S(2)}) %collective-permute-start.18) | collective-permute-done | bytes 524320 | tf_op jit(solution)/shard_map/ppermute | solution.py:121
  397.6 6.3 %collective-permute-start.20 = (bf16[16,8192]{1,0:T(8,128)(2,1)S(1)}, bf16[16,8192]{1,0:T(8,128)(2,1)S(1)}, u32[]{:S(2)}, u32[]{:S(2)}) collective-permute-start(bf16[16,8192]{1,0:T(8,128)(2,1)S(1)} %fusion.22), channel_id=1, source_target_pairs={{0,8},{8,0},{1,9},{9,1},{2,10},{10,2},{3,11},{11,3},{4,12},{12,4},... | collective-permute-start | bytes 786440 | tf_op jit(solution)/shard_map/ppermute | solution.py:122
  403.9 27.0 %collective-permute-done.20 = bf16[16,8192]{1,0:T(8,128)(2,1)S(1)} collective-permute-done((bf16[16,8192]{1,0:T(8,128)(2,1)S(1)}, bf16[16,8192]{1,0:T(8,128)(2,1)S(1)}, u32[]{:S(2)}, u32[]{:S(2)}) %collective-permute-start.20) | collective-permute-done | bytes 262176 | tf_op jit(solution)/shard_map/ppermute | solution.py:122
  (97 shorter events, 27.0 us)
Async XLA Ops:
  6.5 208.8 %all-gather.5.cloned.1.call-start = ((), (), s32[]{:S(2)}) async-start(), calls=%async_computation | async-start | bytes 7077888 | tf_op jit(solution)/shard_map/all_gather | solution.py:104
  9.9 26.2 %collective-permute-start.6 = (bf16[256,320]{1,0:T(8,128)(2,1)S(1)}, bf16[256,320]{1,0:T(8,128)(2,1)S(1)}, u32[]{:S(2)}, u32[]{:S(2)}) collective-permute-start(bf16[256,320]{1,0:T(8,128)(2,1)S(1)} %get-tuple-element.15), channel_id=1, source_target_pairs={{0,128},{128,256},{256,384},{384,0},{1,129},{129,257},{257,385},{3... | collective-permute-start | bytes 491528 | tf_op jit(solution)/shard_map/ppermute | solution.py:85
  13.8 24.2 %collective-permute-start.5 = (bf16[256,320]{1,0:T(8,128)(2,1)S(1)}, bf16[256,320]{1,0:T(8,128)(2,1)S(1)}, u32[]{:S(2)}, u32[]{:S(2)}) collective-permute-start(bf16[256,320]{1,0:T(8,128)(2,1)S(1)} %get-tuple-element.15), channel_id=1, source_target_pairs={{0,384},{128,0},{256,128},{384,256},{1,385},{129,1},{257,129},{385... | collective-permute-start | bytes 491528 | tf_op jit(solution)/shard_map/ppermute | solution.py:88
  19.3 21.0 %collective-permute-start = (bf16[16,8192]{1,0:T(8,128)(2,1)S(1)}, bf16[16,8192]{1,0:T(8,128)(2,1)S(1)}, u32[]{:S(2)}, u32[]{:S(2)}) collective-permute-start(bf16[16,8192]{1,0:T(8,128)(2,1)S(1)} %fusion.10), channel_id=1, source_target_pairs={{0,8},{8,0},{1,9},{9,1},{2,10},{10,2},{3,11},{11,3},{4,12},{12,4},... | collective-permute-start | bytes 786440 | tf_op jit(solution)/shard_map/ppermute | solution.py:85
  36.1 11.8 %collective-permute-start.7 = (bf16[256,320]{1,0:T(8,128)(2,1)S(1)}, bf16[256,320]{1,0:T(8,128)(2,1)S(1)}, u32[]{:S(2)}, u32[]{:S(2)}) collective-permute-start(bf16[256,320]{1,0:T(8,128)(2,1)S(1)} %collective-permute-done.6), channel_id=1, source_target_pairs={{0,128},{128,256},{256,384},{384,0},{1,129},{129,257},{257,385},{3... | collective-permute-start | bytes 491528 | tf_op jit(solution)/shard_map/ppermute | solution.py:85
  41.3 18.6 %collective-permute-start.1 = (bf16[2,16,8192]{2,1,0:T(8,128)(2,1)S(1)}, bf16[2,16,8192]{2,1,0:T(8,128)(2,1)S(1)}, u32[]{:S(2)}, u32[]{:S(2)}) collective-permute-start(bf16[2,16,8192]{2,1,0:T(8,128)(2,1)S(1)} %get-tuple-element.13), channel_id=1, source_target_pairs={{0,6},{2,0},{4,2},{6,4},{1,7},{3,1},{5,3},{7,5},{8,14},{10,8},{12,... | collective-permute-start | bytes 1572872 | tf_op jit(solution)/shard_map/ppermute | solution.py:88
  46.0 11.9 %collective-permute-start.2 = (bf16[2,16,8192]{2,1,0:T(8,128)(2,1)S(1)}, bf16[2,16,8192]{2,1,0:T(8,128)(2,1)S(1)}, u32[]{:S(2)}, u32[]{:S(2)}) collective-permute-start(bf16[2,16,8192]{2,1,0:T(8,128)(2,1)S(1)} %get-tuple-element.13), channel_id=1, source_target_pairs={{0,2},{2,4},{4,6},{6,0},{1,3},{3,5},{5,7},{7,1},{8,10},{10,12},{12... | collective-permute-start | bytes 1572872 | tf_op jit(solution)/shard_map/ppermute | solution.py:85
  54.3 282.0 %all-gather.7.cloned.1.call-start = ((), (), s32[]{:S(2)}) async-start(), calls=%async_computation.1 | async-start | bytes 4718592 | tf_op jit(solution)/shard_map/all_gather | solution.py:104
  58.0 11.1 %collective-permute-start.3 = (bf16[2,16,8192]{2,1,0:T(8,128)(2,1)S(1)}, bf16[2,16,8192]{2,1,0:T(8,128)(2,1)S(1)}, u32[]{:S(2)}, u32[]{:S(2)}) collective-permute-start(bf16[2,16,8192]{2,1,0:T(8,128)(2,1)S(1)} %collective-permute-done.2), channel_id=1, source_target_pairs={{0,2},{2,4},{4,6},{6,0},{1,3},{3,5},{5,7},{7,1},{8,10},{10,12},{12... | collective-permute-start | bytes 1572872 | tf_op jit(solution)/shard_map/ppermute | solution.py:85
  70.7 144.6 %copy-start.2 = (bf16[256,256]{1,0:T(8,128)(2,1)S(1)}, bf16[256,256]{1,0:T(8,128)(2,1)}, u32[]{:S(2)}) copy-start(bf16[256,256]{1,0:T(8,128)(2,1)} %param.13) | copy-start | bytes 393220
  75.8 161.1 %collective-permute-start.4 = (bf16[4,2,16,8192]{3,2,0,1:T(8,128)(2,1)S(1)}, bf16[4,2,16,8192]{3,2,0,1:T(8,128)(2,1)}, u32[]{:S(2)}, u32[]{:S(2)}) collective-permute-start(bf16[4,2,16,8192]{3,2,0,1:T(8,128)(2,1)S(1)} %constant_dynamic-slice_fusion.5), channel_id=1, source_target_pairs={{0,1},{1,0},{2,3},{3,2},{4,5},{5,4},{6,7},{7,6},{8,9},{9,8},{10,11... | collective-permute-start | bytes 6291464 | tf_op jit(solution)/shard_map/ppermute | solution.py:85
  215.3 13.2 %collective-permute-start.13 = (bf16[256,256]{1,0:T(8,128)(2,1)S(1)}, bf16[256,256]{1,0:T(8,128)(2,1)S(1)}, u32[]{:S(2)}, u32[]{:S(2)}) collective-permute-start(bf16[256,256]{1,0:T(8,128)(2,1)S(1)} %copy-done.2), channel_id=1, source_target_pairs={{0,384},{128,0},{256,128},{384,256},{1,385},{129,1},{257,129},{385... | collective-permute-start | bytes 393224 | tf_op jit(solution)/shard_map/ppermute | solution.py:88
  219.7 6.9 %collective-permute-start.14 = (bf16[256,256]{1,0:T(8,128)(2,1)S(1)}, bf16[256,256]{1,0:T(8,128)(2,1)S(1)}, u32[]{:S(2)}, u32[]{:S(2)}) collective-permute-start(bf16[256,256]{1,0:T(8,128)(2,1)S(1)} %copy-done.2), channel_id=1, source_target_pairs={{0,128},{128,256},{256,384},{384,0},{1,129},{129,257},{257,385},{3... | collective-permute-start | bytes 393224 | tf_op jit(solution)/shard_map/ppermute | solution.py:85
  226.6 6.9 %collective-permute-start.15 = (bf16[256,256]{1,0:T(8,128)(2,1)S(1)}, bf16[256,256]{1,0:T(8,128)(2,1)S(1)}, u32[]{:S(2)}, u32[]{:S(2)}) collective-permute-start(bf16[256,256]{1,0:T(8,128)(2,1)S(1)} %collective-permute-done.14), channel_id=1, source_target_pairs={{0,128},{128,256},{256,384},{384,0},{1,129},{129,257},{257,385},{3... | collective-permute-start | bytes 393224 | tf_op jit(solution)/shard_map/ppermute | solution.py:85
  235.1 7.1 %slice-start = ((s8[6291456]{0:T(1024)(128)(4,1)}), s8[4194304]{0:T(1024)(128)(4,1)S(1)}, s32[]{:S(2)}) async-start(s8[6291456]{0:T(1024)(128)(4,1)} %bitcast.140), calls=%async_computation.2 | async-start | bytes 8388608
  237.0 5.2 %slice-start.1 = ((s8[6291456]{0:T(1024)(128)(4,1)}), s8[2097152]{0:T(1024)(128)(4,1)S(1)}, s32[]{:S(2)}) async-start(s8[6291456]{0:T(1024)(128)(4,1)} %bitcast.140), calls=%async_computation.3 | async-start | bytes 4194304
  244.7 14.0 %collective-permute-start.8 = (bf16[64,256]{1,0:T(8,128)(2,1)S(1)}, bf16[64,256]{1,0:T(8,128)(2,1)S(1)}, u32[]{:S(2)}, u32[]{:S(2)}) collective-permute-start(bf16[64,256]{1,0:T(8,128)(2,1)S(1)} %get-tuple-element.28), channel_id=1, source_target_pairs={{0,8},{8,0},{1,9},{9,1},{2,10},{10,2},{3,11},{11,3},{4,12},{12,4},... | collective-permute-start | bytes 98312 | tf_op jit(solution)/shard_map/ppermute | solution.py:85
  258.7 12.9 %collective-permute-start.9 = (bf16[2,64,256]{2,1,0:T(8,128)(2,1)S(1)}, bf16[2,64,256]{2,1,0:T(8,128)(2,1)S(1)}, u32[]{:S(2)}, u32[]{:S(2)}) collective-permute-start(bf16[2,64,256]{2,1,0:T(8,128)(2,1)S(1)} %get-tuple-element.11), channel_id=1, source_target_pairs={{0,6},{2,0},{4,2},{6,4},{1,7},{3,1},{5,3},{7,5},{8,14},{10,8},{12,... | collective-permute-start | bytes 196616 | tf_op jit(solution)/shard_map/ppermute | solution.py:88
  263.1 6.6 %collective-permute-start.10 = (bf16[2,64,256]{2,1,0:T(8,128)(2,1)S(1)}, bf16[2,64,256]{2,1,0:T(8,128)(2,1)S(1)}, u32[]{:S(2)}, u32[]{:S(2)}) collective-permute-start(bf16[2,64,256]{2,1,0:T(8,128)(2,1)S(1)} %get-tuple-element.11), channel_id=1, source_target_pairs={{0,2},{2,4},{4,6},{6,0},{1,3},{3,5},{5,7},{7,1},{8,10},{10,12},{12... | collective-permute-start | bytes 196616 | tf_op jit(solution)/shard_map/ppermute | solution.py:85
  269.7 6.6 %collective-permute-start.11 = (bf16[2,64,256]{2,1,0:T(8,128)(2,1)S(1)}, bf16[2,64,256]{2,1,0:T(8,128)(2,1)S(1)}, u32[]{:S(2)}, u32[]{:S(2)}) collective-permute-start(bf16[2,64,256]{2,1,0:T(8,128)(2,1)S(1)} %collective-permute-done.10), channel_id=1, source_target_pairs={{0,2},{2,4},{4,6},{6,0},{1,3},{3,5},{5,7},{7,1},{8,10},{10,12},{12... | collective-permute-start | bytes 196616 | tf_op jit(solution)/shard_map/ppermute | solution.py:85
  276.5 9.9 %collective-permute-start.12 = (bf16[4,2,64,256]{3,2,1,0:T(8,128)(2,1)S(1)}, bf16[4,2,64,256]{3,2,1,0:T(8,128)(2,1)S(1)}, u32[]{:S(2)}, u32[]{:S(2)}) collective-permute-start(bf16[4,2,64,256]{3,2,1,0:T(8,128)(2,1)S(1)} %constant_dynamic-slice_fusion.3), channel_id=1, source_target_pairs={{0,1},{1,0},{2,3},{3,2},{4,5},{5,4},{6,7},{7,6},{8,9},{9,8},{10,11... | collective-permute-start | bytes 786440 | tf_op jit(solution)/shard_map/ppermute | solution.py:85
  355.7 6.5 %collective-permute-start.16 = (bf16[2,4,16,8192]{3,2,0,1:T(8,128)(2,1)}, bf16[2,4,16,8192]{3,2,0,1:T(8,128)(2,1)}, u32[]{:S(2)}, u32[]{:S(2)}) collective-permute-start(bf16[2,4,16,8192]{3,2,0,1:T(8,128)(2,1)} %bitcast.138), channel_id=1, source_target_pairs={{0,1},{1,0},{2,3},{3,2},{4,5},{5,4},{6,7},{7,6},{8,9},{9,8},{10,11... | collective-permute-start | bytes 6291464 | tf_op jit(solution)/shard_map/ppermute | solution.py:116
  364.3 2.0 copy-start
  366.3 64.7 %copy-start.1 = (bf16[16,8192]{1,0:T(8,128)(2,1)S(1)}, bf16[16,8192]{1,0:T(8,128)(2,1)}, u32[]{:S(2)}) copy-start(bf16[16,8192]{1,0:T(8,128)(2,1)} %param.8) | copy-start | bytes 786436
  366.5 16.2 %collective-permute-start.17 = (bf16[2,16,8192]{2,1,0:T(8,128)(2,1)S(1)}, bf16[2,16,8192]{2,1,0:T(8,128)(2,1)S(1)}, u32[]{:S(2)}, u32[]{:S(2)}) collective-permute-start(bf16[2,16,8192]{2,1,0:T(8,128)(2,1)S(1)} %get-tuple-element.16), channel_id=1, source_target_pairs={{0,2},{2,4},{4,6},{6,0},{1,3},{3,5},{5,7},{7,1},{8,10},{10,12},{12... | collective-permute-start | bytes 1572872 | tf_op jit(solution)/shard_map/ppermute | solution.py:121
  369.6 25.3 %collective-permute-start.18 = (bf16[2,16,8192]{2,1,0:T(8,128)(2,1)S(1)}, bf16[2,16,8192]{2,1,0:T(8,128)(2,1)S(1)}, u32[]{:S(2)}, u32[]{:S(2)}) collective-permute-start(bf16[2,16,8192]{2,1,0:T(8,128)(2,1)S(1)} %get-tuple-element.18), channel_id=1, source_target_pairs={{0,4},{2,6},{4,0},{6,2},{1,5},{3,7},{5,1},{7,3},{8,12},{10,14},{12... | collective-permute-start | bytes 1572872 | tf_op jit(solution)/shard_map/ppermute | solution.py:121
  373.9 22.2 %collective-permute-start.19 = (bf16[2,16,8192]{2,1,0:T(8,128)(2,1)S(1)}, bf16[2,16,8192]{2,1,0:T(8,128)(2,1)S(1)}, u32[]{:S(2)}, u32[]{:S(2)}) collective-permute-start(bf16[2,16,8192]{2,1,0:T(8,128)(2,1)S(1)} %get-tuple-element.17), channel_id=1, source_target_pairs={{0,6},{2,0},{4,2},{6,4},{1,7},{3,1},{5,3},{7,5},{8,14},{10,8},{12,... | collective-permute-start | bytes 1572872 | tf_op jit(solution)/shard_map/ppermute | solution.py:121
  397.6 33.3 %collective-permute-start.20 = (bf16[16,8192]{1,0:T(8,128)(2,1)S(1)}, bf16[16,8192]{1,0:T(8,128)(2,1)S(1)}, u32[]{:S(2)}, u32[]{:S(2)}) collective-permute-start(bf16[16,8192]{1,0:T(8,128)(2,1)S(1)} %fusion.22), channel_id=1, source_target_pairs={{0,8},{8,0},{1,9},{9,1},{2,10},{10,2},{3,11},{11,3},{4,12},{12,4},... | collective-permute-start | bytes 786440 | tf_op jit(solution)/shard_map/ppermute | solution.py:122
Sparse Core Ops, SparseCore 0:
  54.5 160.8 all-gather.4
  234.6 101.6 all-gather.6

commit v4 on v3

--- a/solution.py
+++ b/solution.py
@@ -99,9 +99,8 @@
     return ordered.reshape((-1,) + block.shape[1:])
 
 
-def dp_gather(block):
-    along_x = ring_gather(block, "x", 4)
-    return lax.all_gather(along_x, "zl", axis=1)
+def dp_gather(block, axis):
+    return lax.all_gather(lax.all_gather(block, "zl", axis=axis, tiled=True), "x", axis=axis, tiled=True)
 
 
 def take(array, index, axis):
@@ -125,13 +124,14 @@
 
 def body(tokens, norm_gain, w_query, w_key, w_value, w_out):
     tensor_rank = (lax.axis_index("zh") * 4 + lax.axis_index("y")) * 2 + lax.axis_index("c")
+    q_cols = w_query.shape[1]
+    k_cols = w_key.shape[1]
+    stacked = jnp.concatenate([w_query, w_key, w_value], axis=1)
     normed = normalize(tokens, norm_gain)
+    stacked, normed = lax.optimization_barrier((stacked, normed))
+    weights = dp_gather(stacked, 0)
     gathered = group_gather(normed)
     row_count = gathered.shape[0]
-    q_cols = w_query.shape[1]
-    k_cols = w_key.shape[1]
-    weights = dp_gather(jnp.concatenate([w_query, w_key, w_value], axis=1))
-    weights = weights.reshape(-1, weights.shape[-1])
     weights, w_out = lax.optimization_barrier((weights, w_out))
     projected = jnp.dot(gathered, weights, preferred_element_type=jnp.float32)
     query_part = projected[:, :q_cols]
@@ -156,11 +156,10 @@
     key_heads = jnp.take(key_heads, owner, axis=1)
     value_heads = jnp.take(value_heads, owner, axis=1)
     mixed = attend(queries, key_heads, value_heads, SEQ)
-    out_weights = dp_gather(w_out)
-    partial_out = jnp.einsum(
-        "rk,xzkc->rxzc", mixed, out_weights, preferred_element_type=jnp.float32
+    partial_out = jnp.dot(
+        mixed, dp_gather(w_out, 1), preferred_element_type=jnp.float32
     ).astype(jnp.bfloat16)
-    width = partial_out.shape[1] * partial_out.shape[2] * partial_out.shape[3]
+    width = partial_out.shape[1]
     summed = group_reduce_scatter(partial_out.reshape(2, 4, 2, row_count // 16, width))
     return (tokens.astype(jnp.float32) + summed).astype(jnp.bfloat16)
 

time: 441 us -> 406 us (0.921)
  the two profiles are of different devices: /device:TPU:1 before, /device:TPU:40 now
where the time goes in v4:
time: 406 us; the launch traced here: 405 us
  waiting for transfers between devices  279 us (69%)
  starting transfers between devices  71.5 us (18%)
  local copies, waits for them, and re-layouts  17.6 us (4%)
  other arithmetic  16.3 us (4%)
  between operations  13.8 us (3%)
  matrix products  6.34 us (2%)
    all_gather x2, waiting for transfers between devices, dp_gather(): lax.all_gather(block, 'zl', axis=axis, tiled=True)  94.6 us
    all_gather x2, waiting for transfers between devices, dp_gather(): lax.all_gather(lax.all_gather(block, 'zl', axis=axis, tiled=True), 'x', a...  82 us
    ppermute x8, waiting for transfers between devices, ring_gather(): ahead = lax.ppermute(ahead, axis_name, forward)  55 us
    ppermute x8, starting transfers between devices, ring_gather(): ahead = lax.ppermute(ahead, axis_name, forward)  42.2 us
    ppermute x1, waiting for transfers between devices, group_reduce_scatter(): lax.ppermute(take(mine, 1 - zh_index, 0).astype(jnp.bfloat16), 'zh', swap)  21.9 us
    ppermute x3, waiting for transfers between devices, group_reduce_scatter(): lax.ppermute(outgoing, 'y', [(s, (s + shift) % 4) for s in range(4)])  21.2 us
    ppermute x1, starting transfers between devices, group_reduce_scatter(): lax.ppermute(take(mine, 1 - zh_index, 0).astype(jnp.bfloat16), 'zh', swap)  11.9 us
    ppermute x3, starting transfers between devices, group_reduce_scatter(): lax.ppermute(outgoing, 'y', [(s, (s + shift) % 4) for s in range(4)])  10.5 us
  transfers between devices with their start and end apart: 19, of which 16 were waited for; matrix products, arithmetic and copies ran while one was open for 5% of the time, Pallas kernels for 0%

profile of v4, /device:TPU:40, one launch (start us, length us, event | category | flops | bytes accessed | tf_op | source)
XLA Modules:
  0.0 404.8 jit_solution(8296050216321554539)
XLA Ops:
  7.4 0.8 copy.29
  8.2 1.1 fusion.8
  9.4 1.1 fusion.10
  10.4 1.7 pad_maximum_fusion.1
  12.1 14.8 %collective-permute-start = (bf16[16,8192]{1,0:T(8,128)(2,1)S(1)}, bf16[16,8192]{1,0:T(8,128)(2,1)S(1)}, u32[]{:S(2)}, u32[]{:S(2)}) collective-permute-start(bf16[16,8192]{1,0:T(8,128)(2,1)S(1)} %fusion.10), channel_id=1, source_target_pairs={{0,8},{8,0},{1,9},{9,1},{2,10},{10,2},{3,11},{11,3},{4,12},{12,4},... | collective-permute-start | bytes 786440 | tf_op jit(solution)/shard_map/ppermute | solution.py:85
  27.0 23.4 %collective-permute-done = bf16[16,8192]{1,0:T(8,128)(2,1)S(1)} collective-permute-done((bf16[16,8192]{1,0:T(8,128)(2,1)S(1)}, bf16[16,8192]{1,0:T(8,128)(2,1)S(1)}, u32[]{:S(2)}, u32[]{:S(2)}) %collective-permute-start) | collective-permute-done | bytes 262176 | tf_op jit(solution)/shard_map/ppermute | solution.py:85
  50.3 1.1 bitcast_dynamic-update-slice_fusion.6
  51.4 3.5 collective-permute-start.2
  54.9 2.4 collective-permute-start.1
  57.4 8.9 %collective-permute-done.2 = bf16[2,16,8192]{2,1,0:T(8,128)(2,1)S(1)} collective-permute-done((bf16[2,16,8192]{2,1,0:T(8,128)(2,1)S(1)}, bf16[2,16,8192]{2,1,0:T(8,128)(2,1)S(1)}, u32[]{:S(2)}, u32[]{:S(2)}) %collective-permute-start.2) | collective-permute-done | bytes 524320 | tf_op jit(solution)/shard_map/ppermute | solution.py:85
  66.2 3.5 collective-permute-start.3
  69.7 0.8 bitcast_dynamic-update-slice_fusion.2
  70.6 9.6 %collective-permute-done.3 = bf16[2,16,8192]{2,1,0:T(8,128)(2,1)S(1)} collective-permute-done((bf16[2,16,8192]{2,1,0:T(8,128)(2,1)S(1)}, bf16[2,16,8192]{2,1,0:T(8,128)(2,1)S(1)}, u32[]{:S(2)}, u32[]{:S(2)}) %collective-permute-start.3) | collective-permute-done | bytes 524320 | tf_op jit(solution)/shard_map/ppermute | solution.py:85
  81.0 40.9 %all-gather.5.cloned.1.call-done = bf16[2048,320]{1,0:T(8,128)(2,1)} async-done(((bf16[256,320]{1,0:T(8,128)(2,1)}), bf16[2048,320]{1,0:T(8,128)(2,1)}) %all-gather.5.cloned.1.call-update) | async-done | bytes 1310736 | tf_op jit(solution)/shard_map/all_gather | solution.py:103
  122.0 0.9 bitcast_dynamic-update-slice_fusion.4
  124.5 0.9 bitcast_dynamic-update-slice_fusion.1
  126.2 71.8 %all-gather.7.cloned.1.call-done = bf16[8192,320]{1,0:T(8,128)(2,1)} async-done(((bf16[2048,320]{1,0:T(8,128)(2,1)}), bf16[8192,320]{1,0:T(8,128)(2,1)}) %all-gather.7.cloned.1.call-update) | async-done | bytes 5242896 | tf_op jit(solution)/shard_map/all_gather | solution.py:103
  198.0 1.7 constant_dynamic-slice_fusion.3
  199.7 1.9 collective-permute-start.4
  202.3 53.7 %all-gather.9.cloned.1.call-done = bf16[256,2048]{1,0:T(8,128)(2,1)} async-done(((bf16[256,256]{1,0:T(8,128)(2,1)}), bf16[256,2048]{1,0:T(8,128)(2,1)}) %all-gather.9.cloned.1.call-update) | async-done | bytes 1048592 | tf_op jit(solution)/shard_map/all_gather | solution.py:103
  256.1 1.9 fusion.46
  258.0 5.2 %fusion.2 = bf16[2,4,2,16,8192]{4,3,0,1,2:T(8,128)(2,1)S(1)} fusion(s32[]{:T(128)S(6)} %select_n.138, bf16[1,4,2,16,8192]{4,3,0,1,2:T(8,128)(2,1)S(1)} %fusion.46, bf16[1,4,2,16,8192]{4,3,0,1,2:T(8,128)(2,1)} %bitcast.11), kind=kLoop, calls=%fused_computation.9 | loop fusion | flops 6291456 | bytes 8388612 | tf_op jit(solution)/shard_map/jit(_roll_dynamic)/concatenate | solution.py:91
  263.2 2.5 fusion.40
  265.7 10.6 %collective-permute-start.5 = (bf16[64,256]{1,0:T(8,128)(2,1)S(1)}, bf16[64,256]{1,0:T(8,128)(2,1)S(1)}, u32[]{:S(2)}, u32[]{:S(2)}) collective-permute-start(bf16[64,256]{1,0:T(8,128)(2,1)S(1)} %get-tuple-element.30), channel_id=1, source_target_pairs={{0,8},{8,0},{1,9},{9,1},{2,10},{10,2},{3,11},{11,3},{4,12},{12,4},... | collective-permute-start | bytes 98312 | tf_op jit(solution)/shard_map/ppermute | solution.py:85
  276.3 3.9 collective-permute-done.5
  280.3 2.5 collective-permute-start.6
  282.7 3.4 collective-permute-start.7
  286.4 3.2 collective-permute-done.7
  289.6 2.7 collective-permute-start.8
  292.4 4.8 %collective-permute-done.8 = bf16[2,64,256]{2,1,0:T(8,128)(2,1)S(1)} collective-permute-done((bf16[2,64,256]{2,1,0:T(8,128)(2,1)S(1)}, bf16[2,64,256]{2,1,0:T(8,128)(2,1)S(1)}, u32[]{:S(2)}, u32[]{:S(2)}) %collective-permute-start.8) | collective-permute-done | bytes 65568 | tf_op jit(solution)/shard_map/ppermute | solution.py:85
  297.3 1.9 collective-permute-start.9
  299.4 1.3 collective-permute-done.9
  304.2 10.2 %all-gather.11.cloned.1.call-done = bf16[256,8192]{1,0:T(8,128)(2,1)} async-done(((bf16[256,2048]{1,0:T(8,128)(2,1)}), bf16[256,8192]{1,0:T(8,128)(2,1)}) %all-gather.11.cloned.1.call-update) | async-done | bytes 4194320 | tf_op jit(solution)/shard_map/all_gather | solution.py:103
  314.4 3.4 convolution_convert_fusion
  318.2 1.6 copy.67
  319.7 1.9 collective-permute-start.10
  321.7 4.4 %collective-permute-done.10 = bf16[2,4,16,8192]{3,2,0,1:T(8,128)(2,1)} collective-permute-done((bf16[2,4,16,8192]{3,2,0,1:T(8,128)(2,1)}, bf16[2,4,16,8192]{3,2,0,1:T(8,128)(2,1)}, u32[]{:S(2)}, u32[]{:S(2)}) %collective-permute-start.10) | collective-permute-done | bytes 2097184 | tf_op jit(solution)/shard_map/ppermute | solution.py:115
  326.1 2.1 convert_add_fusion
  328.2 2.0 copy-done
  330.4 3.4 collective-permute-start.11
  333.8 3.0 collective-permute-start.12
  336.8 4.0 collective-permute-start.13
  340.9 6.2 %collective-permute-done.11 = bf16[2,16,8192]{2,1,0:T(8,128)(2,1)S(1)} collective-permute-done((bf16[2,16,8192]{2,1,0:T(8,128)(2,1)S(1)}, bf16[2,16,8192]{2,1,0:T(8,128)(2,1)S(1)}, u32[]{:S(2)}, u32[]{:S(2)}) %collective-permute-start.11) | collective-permute-done | bytes 524320 | tf_op jit(solution)/shard_map/ppermute | solution.py:120
  347.0 5.0 %collective-permute-done.12 = bf16[2,16,8192]{2,1,0:T(8,128)(2,1)S(1)} collective-permute-done((bf16[2,16,8192]{2,1,0:T(8,128)(2,1)S(1)}, bf16[2,16,8192]{2,1,0:T(8,128)(2,1)S(1)}, u32[]{:S(2)}, u32[]{:S(2)}) %collective-permute-start.12) | collective-permute-done | bytes 524320 | tf_op jit(solution)/shard_map/ppermute | solution.py:120
  352.0 10.1 %collective-permute-done.13 = bf16[2,16,8192]{2,1,0:T(8,128)(2,1)S(1)} collective-permute-done((bf16[2,16,8192]{2,1,0:T(8,128)(2,1)S(1)}, bf16[2,16,8192]{2,1,0:T(8,128)(2,1)S(1)}, u32[]{:S(2)}, u32[]{:S(2)}) %collective-permute-start.13) | collective-permute-done | bytes 524320 | tf_op jit(solution)/shard_map/ppermute | solution.py:120
  362.1 1.4 fusion.7
  363.6 11.9 %collective-permute-start.14 = (bf16[16,8192]{1,0:T(8,128)(2,1)S(1)}, bf16[16,8192]{1,0:T(8,128)(2,1)S(1)}, u32[]{:S(2)}, u32[]{:S(2)}) collective-permute-start(bf16[16,8192]{1,0:T(8,128)(2,1)S(1)} %fusion.22), channel_id=1, source_target_pairs={{0,8},{8,0},{1,9},{9,1},{2,10},{10,2},{3,11},{11,3},{4,12},{12,4},... | collective-permute-start | bytes 786440 | tf_op jit(solution)/shard_map/ppermute | solution.py:121
  375.5 21.9 %collective-permute-done.14 = bf16[16,8192]{1,0:T(8,128)(2,1)S(1)} collective-permute-done((bf16[16,8192]{1,0:T(8,128)(2,1)S(1)}, bf16[16,8192]{1,0:T(8,128)(2,1)S(1)}, u32[]{:S(2)}, u32[]{:S(2)}) %collective-permute-start.14) | collective-permute-done | bytes 262176 | tf_op jit(solution)/shard_map/ppermute | solution.py:121
  (68 shorter events, 10.3 us)
Async XLA Ops:
  6.5 115.3 %all-gather.5.cloned.1.call-start = ((), (), s32[]{:S(2)}) async-start(), calls=%async_computation | async-start | bytes 1769472 | tf_op jit(solution)/shard_map/all_gather | solution.py:103
  12.1 38.2 %collective-permute-start = (bf16[16,8192]{1,0:T(8,128)(2,1)S(1)}, bf16[16,8192]{1,0:T(8,128)(2,1)S(1)}, u32[]{:S(2)}, u32[]{:S(2)}) collective-permute-start(bf16[16,8192]{1,0:T(8,128)(2,1)S(1)} %fusion.10), channel_id=1, source_target_pairs={{0,8},{8,0},{1,9},{9,1},{2,10},{10,2},{3,11},{11,3},{4,12},{12,4},... | collective-permute-start | bytes 786440 | tf_op jit(solution)/shard_map/ppermute | solution.py:85
  51.4 14.8 %collective-permute-start.2 = (bf16[2,16,8192]{2,1,0:T(8,128)(2,1)S(1)}, bf16[2,16,8192]{2,1,0:T(8,128)(2,1)S(1)}, u32[]{:S(2)}, u32[]{:S(2)}) collective-permute-start(bf16[2,16,8192]{2,1,0:T(8,128)(2,1)S(1)} %get-tuple-element.17), channel_id=1, source_target_pairs={{0,2},{2,4},{4,6},{6,0},{1,3},{3,5},{5,7},{7,1},{8,10},{10,12},{12... | collective-permute-start | bytes 1572872 | tf_op jit(solution)/shard_map/ppermute | solution.py:85
  54.9 14.8 %collective-permute-start.1 = (bf16[2,16,8192]{2,1,0:T(8,128)(2,1)S(1)}, bf16[2,16,8192]{2,1,0:T(8,128)(2,1)S(1)}, u32[]{:S(2)}, u32[]{:S(2)}) collective-permute-start(bf16[2,16,8192]{2,1,0:T(8,128)(2,1)S(1)} %get-tuple-element.17), channel_id=1, source_target_pairs={{0,6},{2,0},{4,2},{6,4},{1,7},{3,1},{5,3},{7,5},{8,14},{10,8},{12,... | collective-permute-start | bytes 1572872 | tf_op jit(solution)/shard_map/ppermute | solution.py:88
  57.3 140.6 %all-gather.7.cloned.1.call-start = ((), (), s32[]{:S(2)}) async-start(), calls=%async_computation.1 | async-start | bytes 7864320 | tf_op jit(solution)/shard_map/all_gather | solution.py:103
  66.2 13.9 %collective-permute-start.3 = (bf16[2,16,8192]{2,1,0:T(8,128)(2,1)S(1)}, bf16[2,16,8192]{2,1,0:T(8,128)(2,1)S(1)}, u32[]{:S(2)}, u32[]{:S(2)}) collective-permute-start(bf16[2,16,8192]{2,1,0:T(8,128)(2,1)S(1)} %collective-permute-done.2), channel_id=1, source_target_pairs={{0,2},{2,4},{4,6},{6,0},{1,3},{3,5},{5,7},{7,1},{8,10},{10,12},{12... | collective-permute-start | bytes 1572872 | tf_op jit(solution)/shard_map/ppermute | solution.py:85
  121.9 134.1 %all-gather.9.cloned.1.call-start = ((), (), s32[]{:S(2)}) async-start(), calls=%async_computation.2 | async-start | bytes 1179648 | tf_op jit(solution)/shard_map/all_gather | solution.py:103
  198.0 116.4 %all-gather.11.cloned.1.call-start = ((), (), s32[]{:S(2)}) async-start(), calls=%async_computation.3 | async-start | bytes 5242880 | tf_op jit(solution)/shard_map/all_gather | solution.py:103
  199.7 58.2 %collective-permute-start.4 = (bf16[4,2,16,8192]{3,2,0,1:T(8,128)(2,1)S(1)}, bf16[4,2,16,8192]{3,2,0,1:T(8,128)(2,1)}, u32[]{:S(2)}, u32[]{:S(2)}) collective-permute-start(bf16[4,2,16,8192]{3,2,0,1:T(8,128)(2,1)S(1)} %constant_dynamic-slice_fusion.3), channel_id=1, source_target_pairs={{0,1},{1,0},{2,3},{3,2},{4,5},{5,4},{6,7},{7,6},{8,9},{9,8},{10,11... | collective-permute-start | bytes 6291464 | tf_op jit(solution)/shard_map/ppermute | solution.py:85
  256.1 7.1 %slice-start = ((s8[6291456]{0:T(1024)(128)(4,1)}), s8[4194304]{0:T(1024)(128)(4,1)S(1)}, s32[]{:S(2)}) async-start(s8[6291456]{0:T(1024)(128)(4,1)} %bitcast.115), calls=%async_computation.4 | async-start | bytes 8388608
  258.0 5.2 %slice-start.1 = ((s8[6291456]{0:T(1024)(128)(4,1)}), s8[2097152]{0:T(1024)(128)(4,1)S(1)}, s32[]{:S(2)}) async-start(s8[6291456]{0:T(1024)(128)(4,1)} %bitcast.115), calls=%async_computation.5 | async-start | bytes 4194304
  265.7 14.5 %collective-permute-start.5 = (bf16[64,256]{1,0:T(8,128)(2,1)S(1)}, bf16[64,256]{1,0:T(8,128)(2,1)S(1)}, u32[]{:S(2)}, u32[]{:S(2)}) collective-permute-start(bf16[64,256]{1,0:T(8,128)(2,1)S(1)} %get-tuple-element.30), channel_id=1, source_target_pairs={{0,8},{8,0},{1,9},{9,1},{2,10},{10,2},{3,11},{11,3},{4,12},{12,4},... | collective-permute-start | bytes 98312 | tf_op jit(solution)/shard_map/ppermute | solution.py:85
  280.3 12.1 %collective-permute-start.6 = (bf16[2,64,256]{2,1,0:T(8,128)(2,1)S(1)}, bf16[2,64,256]{2,1,0:T(8,128)(2,1)S(1)}, u32[]{:S(2)}, u32[]{:S(2)}) collective-permute-start(bf16[2,64,256]{2,1,0:T(8,128)(2,1)S(1)} %get-tuple-element.15), channel_id=1, source_target_pairs={{0,6},{2,0},{4,2},{6,4},{1,7},{3,1},{5,3},{7,5},{8,14},{10,8},{12,... | collective-permute-start | bytes 196616 | tf_op jit(solution)/shard_map/ppermute | solution.py:88
  282.7 6.9 %collective-permute-start.7 = (bf16[2,64,256]{2,1,0:T(8,128)(2,1)S(1)}, bf16[2,64,256]{2,1,0:T(8,128)(2,1)S(1)}, u32[]{:S(2)}, u32[]{:S(2)}) collective-permute-start(bf16[2,64,256]{2,1,0:T(8,128)(2,1)S(1)} %get-tuple-element.15), channel_id=1, source_target_pairs={{0,2},{2,4},{4,6},{6,0},{1,3},{3,5},{5,7},{7,1},{8,10},{10,12},{12... | collective-permute-start | bytes 196616 | tf_op jit(solution)/shard_map/ppermute | solution.py:85
  289.6 7.6 %collective-permute-start.8 = (bf16[2,64,256]{2,1,0:T(8,128)(2,1)S(1)}, bf16[2,64,256]{2,1,0:T(8,128)(2,1)S(1)}, u32[]{:S(2)}, u32[]{:S(2)}) collective-permute-start(bf16[2,64,256]{2,1,0:T(8,128)(2,1)S(1)} %collective-permute-done.7), channel_id=1, source_target_pairs={{0,2},{2,4},{4,6},{6,0},{1,3},{3,5},{5,7},{7,1},{8,10},{10,12},{12... | collective-permute-start | bytes 196616 | tf_op jit(solution)/shard_map/ppermute | solution.py:85
  297.3 3.4 collective-permute-start.9
  319.7 6.4 %collective-permute-start.10 = (bf16[2,4,16,8192]{3,2,0,1:T(8,128)(2,1)}, bf16[2,4,16,8192]{3,2,0,1:T(8,128)(2,1)}, u32[]{:S(2)}, u32[]{:S(2)}) collective-permute-start(bf16[2,4,16,8192]{3,2,0,1:T(8,128)(2,1)} %bitcast.112), channel_id=1, source_target_pairs={{0,1},{1,0},{2,3},{3,2},{4,5},{5,4},{6,7},{7,6},{8,9},{9,8},{10,11... | collective-permute-start | bytes 6291464 | tf_op jit(solution)/shard_map/ppermute | solution.py:115
  328.2 2.0 copy-start
  330.2 67.3 %copy-start.1 = (bf16[16,8192]{1,0:T(8,128)(2,1)S(1)}, bf16[16,8192]{1,0:T(8,128)(2,1)}, u32[]{:S(2)}) copy-start(bf16[16,8192]{1,0:T(8,128)(2,1)} %param.8) | copy-start | bytes 786436
  330.4 16.7 %collective-permute-start.11 = (bf16[2,16,8192]{2,1,0:T(8,128)(2,1)S(1)}, bf16[2,16,8192]{2,1,0:T(8,128)(2,1)S(1)}, u32[]{:S(2)}, u32[]{:S(2)}) collective-permute-start(bf16[2,16,8192]{2,1,0:T(8,128)(2,1)S(1)} %get-tuple-element.18), channel_id=1, source_target_pairs={{0,2},{2,4},{4,6},{6,0},{1,3},{3,5},{5,7},{7,1},{8,10},{10,12},{12... | collective-permute-start | bytes 1572872 | tf_op jit(solution)/shard_map/ppermute | solution.py:120
  333.8 18.3 %collective-permute-start.12 = (bf16[2,16,8192]{2,1,0:T(8,128)(2,1)S(1)}, bf16[2,16,8192]{2,1,0:T(8,128)(2,1)S(1)}, u32[]{:S(2)}, u32[]{:S(2)}) collective-permute-start(bf16[2,16,8192]{2,1,0:T(8,128)(2,1)S(1)} %get-tuple-element.20), channel_id=1, source_target_pairs={{0,4},{2,6},{4,0},{6,2},{1,5},{3,7},{5,1},{7,3},{8,12},{10,14},{12... | collective-permute-start | bytes 1572872 | tf_op jit(solution)/shard_map/ppermute | solution.py:120
  336.8 25.3 %collective-permute-start.13 = (bf16[2,16,8192]{2,1,0:T(8,128)(2,1)S(1)}, bf16[2,16,8192]{2,1,0:T(8,128)(2,1)S(1)}, u32[]{:S(2)}, u32[]{:S(2)}) collective-permute-start(bf16[2,16,8192]{2,1,0:T(8,128)(2,1)S(1)} %get-tuple-element.19), channel_id=1, source_target_pairs={{0,6},{2,0},{4,2},{6,4},{1,7},{3,1},{5,3},{7,5},{8,14},{10,8},{12,... | collective-permute-start | bytes 1572872 | tf_op jit(solution)/shard_map/ppermute | solution.py:120
  363.6 33.9 %collective-permute-start.14 = (bf16[16,8192]{1,0:T(8,128)(2,1)S(1)}, bf16[16,8192]{1,0:T(8,128)(2,1)S(1)}, u32[]{:S(2)}, u32[]{:S(2)}) collective-permute-start(bf16[16,8192]{1,0:T(8,128)(2,1)S(1)} %fusion.22), channel_id=1, source_target_pairs={{0,8},{8,0},{1,9},{9,1},{2,10},{10,2},{3,11},{11,3},{4,12},{12,4},... | collective-permute-start | bytes 786440 | tf_op jit(solution)/shard_map/ppermute | solution.py:121
Sparse Core Ops, SparseCore 0:
  57.4 64.4 all-gather.4
  124.0 73.9 all-gather.6
  199.9 56.0 all-gather.8
  258.0 56.3 all-gather.10

commit v5 on v4

--- a/solution.py
+++ b/solution.py
@@ -129,10 +129,16 @@
     stacked = jnp.concatenate([w_query, w_key, w_value], axis=1)
     normed = normalize(tokens, norm_gain)
     stacked, normed = lax.optimization_barrier((stacked, normed))
-    weights = dp_gather(stacked, 0)
+    payload = jnp.concatenate([stacked.reshape(-1), w_out.reshape(-1)])
+    along_zl = lax.all_gather(payload, "zl", axis=0)
+    in_part = along_zl[:, : stacked.size].reshape(-1, stacked.shape[1])
+    out_part = along_zl[:, stacked.size :].reshape((-1,) + w_out.shape)
+    weights = lax.all_gather(in_part, "x", axis=0, tiled=True)
+    weights, out_part = lax.optimization_barrier((weights, out_part))
+    out_part = jnp.transpose(out_part, (1, 0, 2)).reshape(w_out.shape[0], -1)
+    out_weights = lax.all_gather(out_part, "x", axis=1, tiled=True)
     gathered = group_gather(normed)
     row_count = gathered.shape[0]
-    weights, w_out = lax.optimization_barrier((weights, w_out))
     projected = jnp.dot(gathered, weights, preferred_element_type=jnp.float32)
     query_part = projected[:, :q_cols]
     kv_part = projected[:, q_cols:].astype(jnp.bfloat16)
@@ -157,7 +163,7 @@
     value_heads = jnp.take(value_heads, owner, axis=1)
     mixed = attend(queries, key_heads, value_heads, SEQ)
     partial_out = jnp.dot(
-        mixed, dp_gather(w_out, 1), preferred_element_type=jnp.float32
+        mixed, out_weights, preferred_element_type=jnp.float32
     ).astype(jnp.bfloat16)
     width = partial_out.shape[1]
     summed = group_reduce_scatter(partial_out.reshape(2, 4, 2, row_count // 16, width))

time: 406 us -> 363 us (0.89)
  waiting for transfers between devices: 279 us -> 217 us
  local copies, waits for them, and re-layouts: 17.6 us -> 34.9 us
    all_gather x4 -> x3, waiting for transfers between devices: 177 us -> 113 us  [the longest x1 61.8 us: body(): weights = lax.all_gather(in_part, 'x', axis=0, tiled=True)]
    unnamed x24 -> x33, local copies, waits for them, and re-layouts: 8.96 us -> 16.5 us
    reshape x0 -> x2, local copies, waits for them, and re-layouts: none -> 4.22 us  [the longest x1 3.96 us: body(): in_part = along_zl[:, :stacked.size].reshape(-1, stacked.shape[1])]
  transfers between devices with their start and end apart: 19 -> 18, of which waited for: 16 -> 15; matrix products, arithmetic and copies ran while one was open for 5% -> 8% of each run, Pallas kernels for 0% -> 0%
where the time goes in v5:
time: 363 us; the launch traced here: 362 us
  waiting for transfers between devices  217 us (60%)
  starting transfers between devices  71.7 us (20%)
  local copies, waits for them, and re-layouts  34.9 us (10%)
  other arithmetic  17.6 us (5%)
  between operations  13.8 us (4%)
  matrix products  6.34 us (2%)
    all_gather x1, waiting for transfers between devices, body(): weights = lax.all_gather(in_part, 'x', axis=0, tiled=True)  61.8 us
    ppermute x8, waiting for transfers between devices, ring_gather(): ahead = lax.ppermute(ahead, axis_name, forward)  56.7 us
    ppermute x8, starting transfers between devices, ring_gather(): ahead = lax.ppermute(ahead, axis_name, forward)  42.5 us
    all_gather x1, waiting for transfers between devices, body(): along_zl = lax.all_gather(payload, 'zl', axis=0)  41.9 us
    ppermute x1, waiting for transfers between devices, group_reduce_scatter(): lax.ppermute(take(mine, 1 - zh_index, 0).astype(jnp.bfloat16), 'zh', swap)  21.9 us
    ppermute x3, waiting for transfers between devices, group_reduce_scatter(): lax.ppermute(outgoing, 'y', [(s, (s + shift) % 4) for s in range(4)])  21.2 us
    unnamed x33, local copies, waits for them, and re-layouts  16.5 us
    ppermute x1, starting transfers between devices, group_reduce_scatter(): lax.ppermute(take(mine, 1 - zh_index, 0).astype(jnp.bfloat16), 'zh', swap)  11.9 us
  transfers between devices with their start and end apart: 18, of which 15 were waited for; matrix products, arithmetic and copies ran while one was open for 8% of the time, Pallas kernels for 0%

profile of v5, /device:TPU:40, one launch (start us, length us, event | category | flops | bytes accessed | tf_op | source)
XLA Modules:
  0.0 361.6 jit_solution(11794255276364451585)
XLA Ops:
  8.2 1.1 fusion.8
  11.4 14.8 %collective-permute-start = (bf16[16,8192]{1,0:T(8,128)(2,1)S(1)}, bf16[16,8192]{1,0:T(8,128)(2,1)S(1)}, u32[]{:S(2)}, u32[]{:S(2)}) collective-permute-start(bf16[16,8192]{1,0:T(8,128)(2,1)S(1)} %fusion.10), channel_id=1, source_target_pairs={{0,8},{8,0},{1,9},{9,1},{2,10},{10,2},{3,11},{11,3},{4,12},{12,4},... | collective-permute-start | bytes 786440 | tf_op jit(solution)/shard_map/ppermute | solution.py:85
  27.6 22.1 %collective-permute-done = bf16[16,8192]{1,0:T(8,128)(2,1)S(1)} collective-permute-done((bf16[16,8192]{1,0:T(8,128)(2,1)S(1)}, bf16[16,8192]{1,0:T(8,128)(2,1)S(1)}, u32[]{:S(2)}, u32[]{:S(2)}) %collective-permute-start) | collective-permute-done | bytes 262176 | tf_op jit(solution)/shard_map/ppermute | solution.py:85
  49.7 1.1 bitcast_dynamic-update-slice_fusion.6
  50.8 2.3 collective-permute-start.1
  53.1 3.5 collective-permute-start.2
  57.4 11.5 %collective-permute-done.2 = bf16[2,16,8192]{2,1,0:T(8,128)(2,1)S(1)} collective-permute-done((bf16[2,16,8192]{2,1,0:T(8,128)(2,1)S(1)}, bf16[2,16,8192]{2,1,0:T(8,128)(2,1)S(1)}, u32[]{:S(2)}, u32[]{:S(2)}) %collective-permute-start.2) | collective-permute-done | bytes 524320 | tf_op jit(solution)/shard_map/ppermute | solution.py:85
  68.9 2.2 collective-permute-start.3
  72.0 11.7 %collective-permute-done.3 = bf16[2,16,8192]{2,1,0:T(8,128)(2,1)S(1)} collective-permute-done((bf16[2,16,8192]{2,1,0:T(8,128)(2,1)S(1)}, bf16[2,16,8192]{2,1,0:T(8,128)(2,1)S(1)}, u32[]{:S(2)}, u32[]{:S(2)}) %collective-permute-start.3) | collective-permute-done | bytes 524320 | tf_op jit(solution)/shard_map/ppermute | solution.py:85
  85.4 41.9 %all-gather.9.cloned.1.call-done = bf16[1179648]{0:T(1024)(128)(2,1)} async-done(((bf16[147456]{0:T(1024)(128)(2,1)}), bf16[1179648]{0:T(1024)(128)(2,1)}) %all-gather.9.cloned.1.call-update) | async-done | bytes 2359312 | tf_op jit(solution)/shard_map/all_gather | solution.py:133
  127.3 2.7 reshape.179
  130.0 1.2 slice.45
  131.1 3.1 reshape.186
  134.2 4.0 %reshape.152 = bf16[2048,320]{1,0:T(8,128)(2,1)} reshape(bf16[655360]{0:T(1024)(128)(2,1)} %reshape.186) | data formatting | bytes 2621440 | tf_op jit(solution)/shard_map/reshape | solution.py:134
  139.0 1.9 bitcast_dynamic-update-slice_fusion.3
  140.9 1.9 bitcast_dynamic-update-slice_fusion.1
  143.6 3.1 constant_dynamic-slice_fusion.3
  146.7 1.9 collective-permute-start.4
  149.3 1.2 multiply_cosine_fusion
  150.6 61.8 %all-gather.5.cloned.1.call-done = bf16[8192,320]{1,0:T(8,128)(2,1)} async-done(((bf16[2048,320]{1,0:T(8,128)(2,1)}), bf16[8192,320]{1,0:T(8,128)(2,1)}) %all-gather.5.cloned.1.call-update) | async-done | bytes 5242896 | tf_op jit(solution)/shard_map/all_gather | solution.py:136
  212.4 1.3 copy.72
  213.7 1.9 fusion.46
  215.6 5.2 %fusion.2 = bf16[2,4,2,16,8192]{4,3,0,1,2:T(8,128)(2,1)S(1)} fusion(s32[]{:T(128)S(6)} %select_n.138, bf16[1,4,2,16,8192]{4,3,0,1,2:T(8,128)(2,1)S(1)} %fusion.46, bf16[1,4,2,16,8192]{4,3,0,1,2:T(8,128)(2,1)} %bitcast.11), kind=kLoop, calls=%fused_computation.9 | loop fusion | flops 6291456 | bytes 8388612 | tf_op jit(solution)/shard_map/jit(_roll_dynamic)/concatenate | solution.py:91
  220.8 2.5 fusion.40
  223.3 11.9 %collective-permute-start.5 = (bf16[64,256]{1,0:T(8,128)(2,1)S(1)}, bf16[64,256]{1,0:T(8,128)(2,1)S(1)}, u32[]{:S(2)}, u32[]{:S(2)}) collective-permute-start(bf16[64,256]{1,0:T(8,128)(2,1)S(1)} %get-tuple-element.30), channel_id=1, source_target_pairs={{0,8},{8,0},{1,9},{9,1},{2,10},{10,2},{3,11},{11,3},{4,12},{12,4},... | collective-permute-start | bytes 98312 | tf_op jit(solution)/shard_map/ppermute | solution.py:85
  235.3 2.6 collective-permute-done.5
  237.9 2.4 collective-permute-start.6
  240.4 3.4 collective-permute-start.7
  244.1 3.2 collective-permute-done.7
  247.2 2.7 collective-permute-start.8
  249.9 4.7 %collective-permute-done.8 = bf16[2,64,256]{2,1,0:T(8,128)(2,1)S(1)} collective-permute-done((bf16[2,64,256]{2,1,0:T(8,128)(2,1)S(1)}, bf16[2,64,256]{2,1,0:T(8,128)(2,1)S(1)}, u32[]{:S(2)}, u32[]{:S(2)}) %collective-permute-start.8) | collective-permute-done | bytes 65568 | tf_op jit(solution)/shard_map/ppermute | solution.py:85
  254.7 2.1 collective-permute-start.9
  261.8 9.3 %all-gather.7.cloned.1.call-done = bf16[256,8192]{1,0:T(8,128)(2,1)} async-done(((bf16[256,2048]{1,0:T(8,128)(2,1)}), bf16[256,8192]{1,0:T(8,128)(2,1)}) %all-gather.7.cloned.1.call-update) | async-done | bytes 4194320 | tf_op jit(solution)/shard_map/all_gather | solution.py:139
  271.2 3.4 convolution_convert_fusion
  275.0 1.6 copy.87
  276.5 1.9 collective-permute-start.10
  278.5 4.4 %collective-permute-done.10 = bf16[2,4,16,8192]{3,2,0,1:T(8,128)(2,1)} collective-permute-done((bf16[2,4,16,8192]{3,2,0,1:T(8,128)(2,1)}, bf16[2,4,16,8192]{3,2,0,1:T(8,128)(2,1)}, u32[]{:S(2)}, u32[]{:S(2)}) %collective-permute-start.10) | collective-permute-done | bytes 2097184 | tf_op jit(solution)/shard_map/ppermute | solution.py:115
  282.9 2.1 convert_add_fusion
  285.0 2.0 copy-done
  287.2 3.4 collective-permute-start.11
  290.6 3.0 collective-permute-start.12
  293.6 4.0 %collective-permute-start.13 = (bf16[2,16,8192]{2,1,0:T(8,128)(2,1)S(1)}, bf16[2,16,8192]{2,1,0:T(8,128)(2,1)S(1)}, u32[]{:S(2)}, u32[]{:S(2)}) collective-permute-start(bf16[2,16,8192]{2,1,0:T(8,128)(2,1)S(1)} %get-tuple-element.19), channel_id=1, source_target_pairs={{0,6},{2,0},{4,2},{6,4},{1,7},{3,1},{5,3},{7,5},{8,14},{10,8},{12,... | collective-permute-start | bytes 1572872 | tf_op jit(solution)/shard_map/ppermute | solution.py:120
  297.7 6.2 %collective-permute-done.11 = bf16[2,16,8192]{2,1,0:T(8,128)(2,1)S(1)} collective-permute-done((bf16[2,16,8192]{2,1,0:T(8,128)(2,1)S(1)}, bf16[2,16,8192]{2,1,0:T(8,128)(2,1)S(1)}, u32[]{:S(2)}, u32[]{:S(2)}) %collective-permute-start.11) | collective-permute-done | bytes 524320 | tf_op jit(solution)/shard_map/ppermute | solution.py:120
  303.8 5.0 %collective-permute-done.12 = bf16[2,16,8192]{2,1,0:T(8,128)(2,1)S(1)} collective-permute-done((bf16[2,16,8192]{2,1,0:T(8,128)(2,1)S(1)}, bf16[2,16,8192]{2,1,0:T(8,128)(2,1)S(1)}, u32[]{:S(2)}, u32[]{:S(2)}) %collective-permute-start.12) | collective-permute-done | bytes 524320 | tf_op jit(solution)/shard_map/ppermute | solution.py:120
  308.8 10.1 %collective-permute-done.13 = bf16[2,16,8192]{2,1,0:T(8,128)(2,1)S(1)} collective-permute-done((bf16[2,16,8192]{2,1,0:T(8,128)(2,1)S(1)}, bf16[2,16,8192]{2,1,0:T(8,128)(2,1)S(1)}, u32[]{:S(2)}, u32[]{:S(2)}) %collective-permute-start.13) | collective-permute-done | bytes 524320 | tf_op jit(solution)/shard_map/ppermute | solution.py:120
  318.9 1.4 fusion.7
  320.4 11.9 %collective-permute-start.14 = (bf16[16,8192]{1,0:T(8,128)(2,1)S(1)}, bf16[16,8192]{1,0:T(8,128)(2,1)S(1)}, u32[]{:S(2)}, u32[]{:S(2)}) collective-permute-start(bf16[16,8192]{1,0:T(8,128)(2,1)S(1)} %fusion.22), channel_id=1, source_target_pairs={{0,8},{8,0},{1,9},{9,1},{2,10},{10,2},{3,11},{11,3},{4,12},{12,4},... | collective-permute-start | bytes 786440 | tf_op jit(solution)/shard_map/ppermute | solution.py:121
  332.3 21.9 %collective-permute-done.14 = bf16[16,8192]{1,0:T(8,128)(2,1)S(1)} collective-permute-done((bf16[16,8192]{1,0:T(8,128)(2,1)S(1)}, bf16[16,8192]{1,0:T(8,128)(2,1)S(1)}, u32[]{:S(2)}, u32[]{:S(2)}) %collective-permute-start.14) | collective-permute-done | bytes 262176 | tf_op jit(solution)/shard_map/ppermute | solution.py:121
  (80 shorter events, 17.6 us)
Async XLA Ops:
  6.5 120.8 %all-gather.9.cloned.1.call-start = ((), (), s32[]{:S(2)}) async-start(), calls=%async_computation.2 | async-start | bytes 2654208 | tf_op jit(solution)/shard_map/all_gather | solution.py:133
  11.4 38.2 %collective-permute-start = (bf16[16,8192]{1,0:T(8,128)(2,1)S(1)}, bf16[16,8192]{1,0:T(8,128)(2,1)S(1)}, u32[]{:S(2)}, u32[]{:S(2)}) collective-permute-start(bf16[16,8192]{1,0:T(8,128)(2,1)S(1)} %fusion.10), channel_id=1, source_target_pairs={{0,8},{8,0},{1,9},{9,1},{2,10},{10,2},{3,11},{11,3},{4,12},{12,4},... | collective-permute-start | bytes 786440 | tf_op jit(solution)/shard_map/ppermute | solution.py:85
  50.8 20.4 %collective-permute-start.1 = (bf16[2,16,8192]{2,1,0:T(8,128)(2,1)S(1)}, bf16[2,16,8192]{2,1,0:T(8,128)(2,1)S(1)}, u32[]{:S(2)}, u32[]{:S(2)}) collective-permute-start(bf16[2,16,8192]{2,1,0:T(8,128)(2,1)S(1)} %get-tuple-element.17), channel_id=1, source_target_pairs={{0,6},{2,0},{4,2},{6,4},{1,7},{3,1},{5,3},{7,5},{8,14},{10,8},{12,... | collective-permute-start | bytes 1572872 | tf_op jit(solution)/shard_map/ppermute | solution.py:88
  53.1 15.8 %collective-permute-start.2 = (bf16[2,16,8192]{2,1,0:T(8,128)(2,1)S(1)}, bf16[2,16,8192]{2,1,0:T(8,128)(2,1)S(1)}, u32[]{:S(2)}, u32[]{:S(2)}) collective-permute-start(bf16[2,16,8192]{2,1,0:T(8,128)(2,1)S(1)} %get-tuple-element.17), channel_id=1, source_target_pairs={{0,2},{2,4},{4,6},{6,0},{1,3},{3,5},{5,7},{7,1},{8,10},{10,12},{12... | collective-permute-start | bytes 1572872 | tf_op jit(solution)/shard_map/ppermute | solution.py:85
  57.4 155.0 %all-gather.5.cloned.1.call-start = ((), (), s32[]{:S(2)}) async-start(), calls=%async_computation | async-start | bytes 7864320 | tf_op jit(solution)/shard_map/all_gather | solution.py:136
  68.9 14.8 %collective-permute-start.3 = (bf16[2,16,8192]{2,1,0:T(8,128)(2,1)S(1)}, bf16[2,16,8192]{2,1,0:T(8,128)(2,1)S(1)}, u32[]{:S(2)}, u32[]{:S(2)}) collective-permute-start(bf16[2,16,8192]{2,1,0:T(8,128)(2,1)S(1)} %collective-permute-done.2), channel_id=1, source_target_pairs={{0,2},{2,4},{4,6},{6,0},{1,3},{3,5},{5,7},{7,1},{8,10},{10,12},{12... | collective-permute-start | bytes 1572872 | tf_op jit(solution)/shard_map/ppermute | solution.py:85
  71.1 14.3 %copy-start.2 = (bf16[2,16,8192]{2,1,0:T(8,128)(2,1)}, bf16[2,16,8192]{2,1,0:T(8,128)(2,1)S(1)}, u32[]{:S(2)}) copy-start(bf16[2,16,8192]{2,1,0:T(8,128)(2,1)S(1)} %collective-permute-done.1) | copy-start | bytes 1572868
  83.7 1.7 copy-start.3
  138.2 133.0 %all-gather.7.cloned.1.call-start = ((), (), s32[]{:S(2)}) async-start(), calls=%async_computation.1 | async-start | bytes 5242880 | tf_op jit(solution)/shard_map/all_gather | solution.py:139
  146.7 68.9 %collective-permute-start.4 = (bf16[4,2,16,8192]{3,2,0,1:T(8,128)(2,1)}, bf16[4,2,16,8192]{3,2,0,1:T(8,128)(2,1)}, u32[]{:S(2)}, u32[]{:S(2)}) collective-permute-start(bf16[4,2,16,8192]{3,2,0,1:T(8,128)(2,1)} %constant_dynamic-slice_fusion.3), channel_id=1, source_target_pairs={{0,1},{1,0},{2,3},{3,2},{4,5},{5,4},{6,7},{7,6},{8,9},{9,8},{10,11... | collective-permute-start | bytes 6291464 | tf_op jit(solution)/shard_map/ppermute | solution.py:85
  213.7 7.1 %slice-start = ((s8[6291456]{0:T(1024)(128)(4,1)}), s8[4194304]{0:T(1024)(128)(4,1)S(1)}, s32[]{:S(2)}) async-start(s8[6291456]{0:T(1024)(128)(4,1)} %bitcast.121), calls=%async_computation.3 | async-start | bytes 8388608
  215.6 5.2 %slice-start.1 = ((s8[6291456]{0:T(1024)(128)(4,1)}), s8[2097152]{0:T(1024)(128)(4,1)S(1)}, s32[]{:S(2)}) async-start(s8[6291456]{0:T(1024)(128)(4,1)} %bitcast.121), calls=%async_computation.4 | async-start | bytes 4194304
  220.8 36.0 %copy-start.4 = (f32[256,64]{1,0:T(8,128)S(1)}, f32[256,64]{1,0:T(8,128)}, u32[]{:S(2)}) copy-start(f32[256,64]{1,0:T(8,128)} %get-tuple-element.34) | copy-start | bytes 196612
  223.3 14.5 %collective-permute-start.5 = (bf16[64,256]{1,0:T(8,128)(2,1)S(1)}, bf16[64,256]{1,0:T(8,128)(2,1)S(1)}, u32[]{:S(2)}, u32[]{:S(2)}) collective-permute-start(bf16[64,256]{1,0:T(8,128)(2,1)S(1)} %get-tuple-element.30), channel_id=1, source_target_pairs={{0,8},{8,0},{1,9},{9,1},{2,10},{10,2},{3,11},{11,3},{4,12},{12,4},... | collective-permute-start | bytes 98312 | tf_op jit(solution)/shard_map/ppermute | solution.py:85
  237.9 12.0 %collective-permute-start.6 = (bf16[2,64,256]{2,1,0:T(8,128)(2,1)S(1)}, bf16[2,64,256]{2,1,0:T(8,128)(2,1)S(1)}, u32[]{:S(2)}, u32[]{:S(2)}) collective-permute-start(bf16[2,64,256]{2,1,0:T(8,128)(2,1)S(1)} %get-tuple-element.15), channel_id=1, source_target_pairs={{0,6},{2,0},{4,2},{6,4},{1,7},{3,1},{5,3},{7,5},{8,14},{10,8},{12,... | collective-permute-start | bytes 196616 | tf_op jit(solution)/shard_map/ppermute | solution.py:88
  240.4 6.9 %collective-permute-start.7 = (bf16[2,64,256]{2,1,0:T(8,128)(2,1)S(1)}, bf16[2,64,256]{2,1,0:T(8,128)(2,1)S(1)}, u32[]{:S(2)}, u32[]{:S(2)}) collective-permute-start(bf16[2,64,256]{2,1,0:T(8,128)(2,1)S(1)} %get-tuple-element.15), channel_id=1, source_target_pairs={{0,2},{2,4},{4,6},{6,0},{1,3},{3,5},{5,7},{7,1},{8,10},{10,12},{12... | collective-permute-start | bytes 196616 | tf_op jit(solution)/shard_map/ppermute | solution.py:85
  247.2 7.4 %collective-permute-start.8 = (bf16[2,64,256]{2,1,0:T(8,128)(2,1)S(1)}, bf16[2,64,256]{2,1,0:T(8,128)(2,1)S(1)}, u32[]{:S(2)}, u32[]{:S(2)}) collective-permute-start(bf16[2,64,256]{2,1,0:T(8,128)(2,1)S(1)} %collective-permute-done.7), channel_id=1, source_target_pairs={{0,2},{2,4},{4,6},{6,0},{1,3},{3,5},{5,7},{7,1},{8,10},{10,12},{12... | collective-permute-start | bytes 196616 | tf_op jit(solution)/shard_map/ppermute | solution.py:85
  254.7 3.4 collective-permute-start.9
  276.5 6.4 %collective-permute-start.10 = (bf16[2,4,16,8192]{3,2,0,1:T(8,128)(2,1)}, bf16[2,4,16,8192]{3,2,0,1:T(8,128)(2,1)}, u32[]{:S(2)}, u32[]{:S(2)}) collective-permute-start(bf16[2,4,16,8192]{3,2,0,1:T(8,128)(2,1)} %bitcast.118), channel_id=1, source_target_pairs={{0,1},{1,0},{2,3},{3,2},{4,5},{5,4},{6,7},{7,6},{8,9},{9,8},{10,11... | collective-permute-start | bytes 6291464 | tf_op jit(solution)/shard_map/ppermute | solution.py:115
  285.0 2.0 copy-start
  287.0 67.3 %copy-start.1 = (bf16[16,8192]{1,0:T(8,128)(2,1)S(1)}, bf16[16,8192]{1,0:T(8,128)(2,1)}, u32[]{:S(2)}) copy-start(bf16[16,8192]{1,0:T(8,128)(2,1)} %param.8) | copy-start | bytes 786436
  287.2 16.7 %collective-permute-start.11 = (bf16[2,16,8192]{2,1,0:T(8,128)(2,1)S(1)}, bf16[2,16,8192]{2,1,0:T(8,128)(2,1)S(1)}, u32[]{:S(2)}, u32[]{:S(2)}) collective-permute-start(bf16[2,16,8192]{2,1,0:T(8,128)(2,1)S(1)} %get-tuple-element.18), channel_id=1, source_target_pairs={{0,2},{2,4},{4,6},{6,0},{1,3},{3,5},{5,7},{7,1},{8,10},{10,12},{12... | collective-permute-start | bytes 1572872 | tf_op jit(solution)/shard_map/ppermute | solution.py:120
  290.6 18.3 %collective-permute-start.12 = (bf16[2,16,8192]{2,1,0:T(8,128)(2,1)S(1)}, bf16[2,16,8192]{2,1,0:T(8,128)(2,1)S(1)}, u32[]{:S(2)}, u32[]{:S(2)}) collective-permute-start(bf16[2,16,8192]{2,1,0:T(8,128)(2,1)S(1)} %get-tuple-element.20), channel_id=1, source_target_pairs={{0,4},{2,6},{4,0},{6,2},{1,5},{3,7},{5,1},{7,3},{8,12},{10,14},{12... | collective-permute-start | bytes 1572872 | tf_op jit(solution)/shard_map/ppermute | solution.py:120
  293.6 25.3 %collective-permute-start.13 = (bf16[2,16,8192]{2,1,0:T(8,128)(2,1)S(1)}, bf16[2,16,8192]{2,1,0:T(8,128)(2,1)S(1)}, u32[]{:S(2)}, u32[]{:S(2)}) collective-permute-start(bf16[2,16,8192]{2,1,0:T(8,128)(2,1)S(1)} %get-tuple-element.19), channel_id=1, source_target_pairs={{0,6},{2,0},{4,2},{6,4},{1,7},{3,1},{5,3},{7,5},{8,14},{10,8},{12,... | collective-permute-start | bytes 1572872 | tf_op jit(solution)/shard_map/ppermute | solution.py:120
  320.4 33.9 %collective-permute-start.14 = (bf16[16,8192]{1,0:T(8,128)(2,1)S(1)}, bf16[16,8192]{1,0:T(8,128)(2,1)S(1)}, u32[]{:S(2)}, u32[]{:S(2)}) collective-permute-start(bf16[16,8192]{1,0:T(8,128)(2,1)S(1)} %fusion.22), channel_id=1, source_target_pairs={{0,8},{8,0},{1,9},{9,1},{2,10},{10,2},{3,11},{11,3},{4,12},{12,4},... | collective-permute-start | bytes 786440 | tf_op jit(solution)/shard_map/ppermute | solution.py:121
Sparse Core Ops, SparseCore 0:
  57.5 69.7 all-gather.8
  138.3 74.0 all-gather.4
  214.5 56.6 all-gather.6

commit v6 on v5

--- a/solution.py
+++ b/solution.py
@@ -131,6 +131,7 @@
     stacked, normed = lax.optimization_barrier((stacked, normed))
     payload = jnp.concatenate([stacked.reshape(-1), w_out.reshape(-1)])
     along_zl = lax.all_gather(payload, "zl", axis=0)
+    along_zl, normed = lax.optimization_barrier((along_zl, normed))
     in_part = along_zl[:, : stacked.size].reshape(-1, stacked.shape[1])
     out_part = along_zl[:, stacked.size :].reshape((-1,) + w_out.shape)
     weights = lax.all_gather(in_part, "x", axis=0, tiled=True)

time: 363 us -> 356 us (0.981)
  starting transfers between devices: 71.7 us -> 66.4 us
    all_gather x1, waiting for transfers between devices: 41.9 us -> 72 us  [body(): along_zl = lax.all_gather(payload, 'zl', axis=0)]
    ppermute x8, waiting for transfers between devices: 56.7 us -> 39.4 us  [ring_gather(): ahead = lax.ppermute(ahead, axis_name, forward)]
    all_gather x1, waiting for transfers between devices: 61.8 us -> 47.9 us  [body(): weights = lax.all_gather(in_part, 'x', axis=0, tiled=True)]
    ppermute x8, starting transfers between devices: 42.5 us -> 37.1 us  [ring_gather(): ahead = lax.ppermute(ahead, axis_name, forward)]
    unnamed x33 -> x29, local copies, waits for them, and re-layouts: 16.5 us -> 16.3 us
  transfers between devices with their start and end apart: 18 -> 18, of which waited for: 15 -> 15; matrix products, arithmetic and copies ran while one was open for 8% -> 10% of each run, Pallas kernels for 0% -> 0%
where the time goes in v6:
time: 356 us; the launch traced here: 355 us
  waiting for transfers between devices  216 us (61%)
  starting transfers between devices  66.4 us (19%)
  local copies, waits for them, and re-layouts  34.8 us (10%)
  other arithmetic  17.6 us (5%)
  between operations  13.8 us (4%)
  matrix products  6.34 us (2%)
    all_gather x1, waiting for transfers between devices, body(): along_zl = lax.all_gather(payload, 'zl', axis=0)  72 us
    all_gather x1, waiting for transfers between devices, body(): weights = lax.all_gather(in_part, 'x', axis=0, tiled=True)  47.9 us
    ppermute x8, waiting for transfers between devices, ring_gather(): ahead = lax.ppermute(ahead, axis_name, forward)  39.4 us
    ppermute x8, starting transfers between devices, ring_gather(): ahead = lax.ppermute(ahead, axis_name, forward)  37.1 us
    ppermute x1, waiting for transfers between devices, group_reduce_scatter(): lax.ppermute(take(mine, 1 - zh_index, 0).astype(jnp.bfloat16), 'zh', swap)  22 us
    ppermute x3, waiting for transfers between devices, group_reduce_scatter(): lax.ppermute(outgoing, 'y', [(s, (s + shift) % 4) for s in range(4)])  21.2 us
    unnamed x29, local copies, waits for them, and re-layouts  16.3 us
    ppermute x1, starting transfers between devices, group_reduce_scatter(): lax.ppermute(take(mine, 1 - zh_index, 0).astype(jnp.bfloat16), 'zh', swap)  11.9 us
  transfers between devices with their start and end apart: 18, of which 15 were waited for; matrix products, arithmetic and copies ran while one was open for 10% of the time, Pallas kernels for 0%

profile of v6, /device:TPU:40, one launch (start us, length us, event | category | flops | bytes accessed | tf_op | source)
XLA Modules:
  0.0 355.2 jit_solution(2958315863968727837)
XLA Ops:
  8.2 1.1 fusion.8
  13.6 72.0 %all-gather.9.cloned.1.call-done = bf16[1179648]{0:T(1024)(128)(2,1)} async-done(((bf16[147456]{0:T(1024)(128)(2,1)}), bf16[1179648]{0:T(1024)(128)(2,1)}) %all-gather.9.cloned.1.call-update) | async-done | bytes 2359312 | tf_op jit(solution)/shard_map/all_gather | solution.py:133
  85.5 2.7 reshape.179
  88.2 8.4 %collective-permute-start = (bf16[16,8192]{1,0:T(8,128)(2,1)S(1)}, bf16[16,8192]{1,0:T(8,128)(2,1)S(1)}, u32[]{:S(2)}, u32[]{:S(2)}) collective-permute-start(bf16[16,8192]{1,0:T(8,128)(2,1)S(1)} %fusion.10), channel_id=1, source_target_pairs={{0,8},{8,0},{1,9},{9,1},{2,10},{10,2},{3,11},{11,3},{4,12},{12,4},... | collective-permute-start | bytes 786440 | tf_op jit(solution)/shard_map/ppermute | solution.py:85
  96.7 17.1 %collective-permute-done = bf16[16,8192]{1,0:T(8,128)(2,1)S(1)} collective-permute-done((bf16[16,8192]{1,0:T(8,128)(2,1)S(1)}, bf16[16,8192]{1,0:T(8,128)(2,1)S(1)}, u32[]{:S(2)}, u32[]{:S(2)}) %collective-permute-start) | collective-permute-done | bytes 262176 | tf_op jit(solution)/shard_map/ppermute | solution.py:85
  113.8 1.1 bitcast_dynamic-update-slice_fusion.6
  114.9 3.3 collective-permute-start.2
  118.3 2.5 collective-permute-start.1
  120.8 1.2 slice.31
  121.9 3.0 reshape.186
  124.9 3.9 %reshape.152 = bf16[2048,320]{1,0:T(8,128)(2,1)} reshape(bf16[655360]{0:T(1024)(128)(2,1)} %reshape.186) | data formatting | bytes 2621440 | tf_op jit(solution)/shard_map/reshape | solution.py:135
  128.9 1.4 collective-permute-done.2
  130.3 3.4 collective-permute-start.3
  133.7 1.9 bitcast_dynamic-update-slice_fusion.2
  135.6 9.4 %collective-permute-done.3 = bf16[2,16,8192]{2,1,0:T(8,128)(2,1)S(1)} collective-permute-done((bf16[2,16,8192]{2,1,0:T(8,128)(2,1)S(1)}, bf16[2,16,8192]{2,1,0:T(8,128)(2,1)S(1)}, u32[]{:S(2)}, u32[]{:S(2)}) %collective-permute-start.3) | collective-permute-done | bytes 524320 | tf_op jit(solution)/shard_map/ppermute | solution.py:85
  147.5 1.9 bitcast_dynamic-update-slice_fusion.3
  151.1 3.3 constant_dynamic-slice_fusion.3
  154.3 1.9 collective-permute-start.4
  156.9 1.2 multiply_cosine_fusion
  158.2 47.9 %all-gather.5.cloned.1.call-done = bf16[8192,320]{1,0:T(8,128)(2,1)} async-done(((bf16[2048,320]{1,0:T(8,128)(2,1)}), bf16[8192,320]{1,0:T(8,128)(2,1)}) %all-gather.5.cloned.1.call-update) | async-done | bytes 5242896 | tf_op jit(solution)/shard_map/all_gather | solution.py:137
  206.1 1.3 copy.72
  207.4 1.9 fusion.46
  209.3 5.2 %fusion.2 = bf16[2,4,2,16,8192]{4,3,0,1,2:T(8,128)(2,1)S(1)} fusion(s32[]{:T(128)S(6)} %select_n.138, bf16[1,4,2,16,8192]{4,3,0,1,2:T(8,128)(2,1)S(1)} %fusion.46, bf16[1,4,2,16,8192]{4,3,0,1,2:T(8,128)(2,1)} %bitcast.11), kind=kLoop, calls=%fused_computation.9 | loop fusion | flops 6291456 | bytes 8388612 | tf_op jit(solution)/shard_map/jit(_roll_dynamic)/concatenate | solution.py:91
  214.6 2.5 fusion.40
  217.1 11.9 %collective-permute-start.5 = (bf16[64,256]{1,0:T(8,128)(2,1)S(1)}, bf16[64,256]{1,0:T(8,128)(2,1)S(1)}, u32[]{:S(2)}, u32[]{:S(2)}) collective-permute-start(bf16[64,256]{1,0:T(8,128)(2,1)S(1)} %get-tuple-element.34), channel_id=1, source_target_pairs={{0,8},{8,0},{1,9},{9,1},{2,10},{10,2},{3,11},{11,3},{4,12},{12,4},... | collective-permute-start | bytes 98312 | tf_op jit(solution)/shard_map/ppermute | solution.py:85
  229.0 2.6 collective-permute-done.5
  231.6 2.4 collective-permute-start.6
  234.1 3.4 collective-permute-start.7
  237.8 3.2 collective-permute-done.7
  241.0 2.7 collective-permute-start.8
  243.7 4.7 %collective-permute-done.8 = bf16[2,64,256]{2,1,0:T(8,128)(2,1)S(1)} collective-permute-done((bf16[2,64,256]{2,1,0:T(8,128)(2,1)S(1)}, bf16[2,64,256]{2,1,0:T(8,128)(2,1)S(1)}, u32[]{:S(2)}, u32[]{:S(2)}) %collective-permute-start.8) | collective-permute-done | bytes 65568 | tf_op jit(solution)/shard_map/ppermute | solution.py:85
  248.4 2.1 collective-permute-start.9
  255.6 9.3 %all-gather.7.cloned.1.call-done = bf16[256,8192]{1,0:T(8,128)(2,1)} async-done(((bf16[256,2048]{1,0:T(8,128)(2,1)}), bf16[256,8192]{1,0:T(8,128)(2,1)}) %all-gather.7.cloned.1.call-update) | async-done | bytes 4194320 | tf_op jit(solution)/shard_map/all_gather | solution.py:140
  264.9 3.4 convolution_convert_fusion
  268.7 1.5 copy.87
  270.2 1.9 collective-permute-start.10
  272.2 4.4 %collective-permute-done.10 = bf16[2,4,16,8192]{3,2,0,1:T(8,128)(2,1)} collective-permute-done((bf16[2,4,16,8192]{3,2,0,1:T(8,128)(2,1)}, bf16[2,4,16,8192]{3,2,0,1:T(8,128)(2,1)}, u32[]{:S(2)}, u32[]{:S(2)}) %collective-permute-start.10) | collective-permute-done | bytes 2097184 | tf_op jit(solution)/shard_map/ppermute | solution.py:115
  276.6 2.1 convert_add_fusion
  278.7 2.0 copy-done
  280.9 3.4 collective-permute-start.11
  284.3 3.0 collective-permute-start.12
  287.3 4.0 %collective-permute-start.13 = (bf16[2,16,8192]{2,1,0:T(8,128)(2,1)S(1)}, bf16[2,16,8192]{2,1,0:T(8,128)(2,1)S(1)}, u32[]{:S(2)}, u32[]{:S(2)}) collective-permute-start(bf16[2,16,8192]{2,1,0:T(8,128)(2,1)S(1)} %get-tuple-element.23), channel_id=1, source_target_pairs={{0,6},{2,0},{4,2},{6,4},{1,7},{3,1},{5,3},{7,5},{8,14},{10,8},{12,... | collective-permute-start | bytes 1572872 | tf_op jit(solution)/shard_map/ppermute | solution.py:120
  291.3 6.2 %collective-permute-done.11 = bf16[2,16,8192]{2,1,0:T(8,128)(2,1)S(1)} collective-permute-done((bf16[2,16,8192]{2,1,0:T(8,128)(2,1)S(1)}, bf16[2,16,8192]{2,1,0:T(8,128)(2,1)S(1)}, u32[]{:S(2)}, u32[]{:S(2)}) %collective-permute-start.11) | collective-permute-done | bytes 524320 | tf_op jit(solution)/shard_map/ppermute | solution.py:120
  297.5 5.0 %collective-permute-done.12 = bf16[2,16,8192]{2,1,0:T(8,128)(2,1)S(1)} collective-permute-done((bf16[2,16,8192]{2,1,0:T(8,128)(2,1)S(1)}, bf16[2,16,8192]{2,1,0:T(8,128)(2,1)S(1)}, u32[]{:S(2)}, u32[]{:S(2)}) %collective-permute-start.12) | collective-permute-done | bytes 524320 | tf_op jit(solution)/shard_map/ppermute | solution.py:120
  302.5 10.1 %collective-permute-done.13 = bf16[2,16,8192]{2,1,0:T(8,128)(2,1)S(1)} collective-permute-done((bf16[2,16,8192]{2,1,0:T(8,128)(2,1)S(1)}, bf16[2,16,8192]{2,1,0:T(8,128)(2,1)S(1)}, u32[]{:S(2)}, u32[]{:S(2)}) %collective-permute-start.13) | collective-permute-done | bytes 524320 | tf_op jit(solution)/shard_map/ppermute | solution.py:120
  312.6 1.4 fusion.7
  314.1 11.9 %collective-permute-start.14 = (bf16[16,8192]{1,0:T(8,128)(2,1)S(1)}, bf16[16,8192]{1,0:T(8,128)(2,1)S(1)}, u32[]{:S(2)}, u32[]{:S(2)}) collective-permute-start(bf16[16,8192]{1,0:T(8,128)(2,1)S(1)} %fusion.22), channel_id=1, source_target_pairs={{0,8},{8,0},{1,9},{9,1},{2,10},{10,2},{3,11},{11,3},{4,12},{12,4},... | collective-permute-start | bytes 786440 | tf_op jit(solution)/shard_map/ppermute | solution.py:121
  326.0 22.0 %collective-permute-done.14 = bf16[16,8192]{1,0:T(8,128)(2,1)S(1)} collective-permute-done((bf16[16,8192]{1,0:T(8,128)(2,1)S(1)}, bf16[16,8192]{1,0:T(8,128)(2,1)S(1)}, u32[]{:S(2)}, u32[]{:S(2)}) %collective-permute-start.14) | collective-permute-done | bytes 262176 | tf_op jit(solution)/shard_map/ppermute | solution.py:121
  (76 shorter events, 17.5 us)
Async XLA Ops:
  6.5 79.0 %all-gather.9.cloned.1.call-start = ((), (), s32[]{:S(2)}) async-start(), calls=%async_computation.2 | async-start | bytes 2654208 | tf_op jit(solution)/shard_map/all_gather | solution.py:133
  13.5 192.6 %all-gather.5.cloned.1.call-start = ((), (), s32[]{:S(2)}) async-start(), calls=%async_computation | async-start | bytes 7864320 | tf_op jit(solution)/shard_map/all_gather | solution.py:137
  88.2 25.6 %collective-permute-start = (bf16[16,8192]{1,0:T(8,128)(2,1)S(1)}, bf16[16,8192]{1,0:T(8,128)(2,1)S(1)}, u32[]{:S(2)}, u32[]{:S(2)}) collective-permute-start(bf16[16,8192]{1,0:T(8,128)(2,1)S(1)} %fusion.10), channel_id=1, source_target_pairs={{0,8},{8,0},{1,9},{9,1},{2,10},{10,2},{3,11},{11,3},{4,12},{12,4},... | collective-permute-start | bytes 786440 | tf_op jit(solution)/shard_map/ppermute | solution.py:85
  114.9 15.4 %collective-permute-start.2 = (bf16[2,16,8192]{2,1,0:T(8,128)(2,1)S(1)}, bf16[2,16,8192]{2,1,0:T(8,128)(2,1)S(1)}, u32[]{:S(2)}, u32[]{:S(2)}) collective-permute-start(bf16[2,16,8192]{2,1,0:T(8,128)(2,1)S(1)} %get-tuple-element.21), channel_id=1, source_target_pairs={{0,2},{2,4},{4,6},{6,0},{1,3},{3,5},{5,7},{7,1},{8,10},{10,12},{12... | collective-permute-start | bytes 1572872 | tf_op jit(solution)/shard_map/ppermute | solution.py:85
  118.3 15.5 %collective-permute-start.1 = (bf16[2,16,8192]{2,1,0:T(8,128)(2,1)S(1)}, bf16[2,16,8192]{2,1,0:T(8,128)(2,1)}, u32[]{:S(2)}, u32[]{:S(2)}) collective-permute-start(bf16[2,16,8192]{2,1,0:T(8,128)(2,1)S(1)} %get-tuple-element.21), channel_id=1, source_target_pairs={{0,6},{2,0},{4,2},{6,4},{1,7},{3,1},{5,3},{7,5},{8,14},{10,8},{12,... | collective-permute-start | bytes 1572872 | tf_op jit(solution)/shard_map/ppermute | solution.py:88
  128.9 136.0 %all-gather.7.cloned.1.call-start = ((), (), s32[]{:S(2)}) async-start(), calls=%async_computation.1 | async-start | bytes 5242880 | tf_op jit(solution)/shard_map/all_gather | solution.py:140
  130.3 14.6 %collective-permute-start.3 = (bf16[2,16,8192]{2,1,0:T(8,128)(2,1)S(1)}, bf16[2,16,8192]{2,1,0:T(8,128)(2,1)S(1)}, u32[]{:S(2)}, u32[]{:S(2)}) collective-permute-start(bf16[2,16,8192]{2,1,0:T(8,128)(2,1)S(1)} %collective-permute-done.2), channel_id=1, source_target_pairs={{0,2},{2,4},{4,6},{6,0},{1,3},{3,5},{5,7},{7,1},{8,10},{10,12},{12... | collective-permute-start | bytes 1572872 | tf_op jit(solution)/shard_map/ppermute | solution.py:85
  154.3 55.0 %collective-permute-start.4 = (bf16[4,2,16,8192]{3,2,0,1:T(8,128)(2,1)}, bf16[4,2,16,8192]{3,2,0,1:T(8,128)(2,1)}, u32[]{:S(2)}, u32[]{:S(2)}) collective-permute-start(bf16[4,2,16,8192]{3,2,0,1:T(8,128)(2,1)} %constant_dynamic-slice_fusion.3), channel_id=1, source_target_pairs={{0,1},{1,0},{2,3},{3,2},{4,5},{5,4},{6,7},{7,6},{8,9},{9,8},{10,11... | collective-permute-start | bytes 6291464 | tf_op jit(solution)/shard_map/ppermute | solution.py:85
  207.4 7.1 %slice-start = ((s8[6291456]{0:T(1024)(128)(4,1)}), s8[4194304]{0:T(1024)(128)(4,1)S(1)}, s32[]{:S(2)}) async-start(s8[6291456]{0:T(1024)(128)(4,1)} %bitcast.121), calls=%async_computation.3 | async-start | bytes 8388608
  209.3 5.2 %slice-start.1 = ((s8[6291456]{0:T(1024)(128)(4,1)}), s8[2097152]{0:T(1024)(128)(4,1)S(1)}, s32[]{:S(2)}) async-start(s8[6291456]{0:T(1024)(128)(4,1)} %bitcast.121), calls=%async_computation.4 | async-start | bytes 4194304
  214.6 36.0 %copy-start.2 = (f32[256,64]{1,0:T(8,128)S(1)}, f32[256,64]{1,0:T(8,128)}, u32[]{:S(2)}) copy-start(f32[256,64]{1,0:T(8,128)} %get-tuple-element.38) | copy-start | bytes 196612
  217.1 14.5 %collective-permute-start.5 = (bf16[64,256]{1,0:T(8,128)(2,1)S(1)}, bf16[64,256]{1,0:T(8,128)(2,1)S(1)}, u32[]{:S(2)}, u32[]{:S(2)}) collective-permute-start(bf16[64,256]{1,0:T(8,128)(2,1)S(1)} %get-tuple-element.34), channel_id=1, source_target_pairs={{0,8},{8,0},{1,9},{9,1},{2,10},{10,2},{3,11},{11,3},{4,12},{12,4},... | collective-permute-start | bytes 98312 | tf_op jit(solution)/shard_map/ppermute | solution.py:85
  231.6 12.0 %collective-permute-start.6 = (bf16[2,64,256]{2,1,0:T(8,128)(2,1)S(1)}, bf16[2,64,256]{2,1,0:T(8,128)(2,1)S(1)}, u32[]{:S(2)}, u32[]{:S(2)}) collective-permute-start(bf16[2,64,256]{2,1,0:T(8,128)(2,1)S(1)} %get-tuple-element.19), channel_id=1, source_target_pairs={{0,6},{2,0},{4,2},{6,4},{1,7},{3,1},{5,3},{7,5},{8,14},{10,8},{12,... | collective-permute-start | bytes 196616 | tf_op jit(solution)/shard_map/ppermute | solution.py:88
  234.1 6.9 %collective-permute-start.7 = (bf16[2,64,256]{2,1,0:T(8,128)(2,1)S(1)}, bf16[2,64,256]{2,1,0:T(8,128)(2,1)S(1)}, u32[]{:S(2)}, u32[]{:S(2)}) collective-permute-start(bf16[2,64,256]{2,1,0:T(8,128)(2,1)S(1)} %get-tuple-element.19), channel_id=1, source_target_pairs={{0,2},{2,4},{4,6},{6,0},{1,3},{3,5},{5,7},{7,1},{8,10},{10,12},{12... | collective-permute-start | bytes 196616 | tf_op jit(solution)/shard_map/ppermute | solution.py:85
  241.0 7.4 %collective-permute-start.8 = (bf16[2,64,256]{2,1,0:T(8,128)(2,1)S(1)}, bf16[2,64,256]{2,1,0:T(8,128)(2,1)S(1)}, u32[]{:S(2)}, u32[]{:S(2)}) collective-permute-start(bf16[2,64,256]{2,1,0:T(8,128)(2,1)S(1)} %collective-permute-done.7), channel_id=1, source_target_pairs={{0,2},{2,4},{4,6},{6,0},{1,3},{3,5},{5,7},{7,1},{8,10},{10,12},{12... | collective-permute-start | bytes 196616 | tf_op jit(solution)/shard_map/ppermute | solution.py:85
  248.4 3.4 collective-permute-start.9
  270.2 6.4 %collective-permute-start.10 = (bf16[2,4,16,8192]{3,2,0,1:T(8,128)(2,1)}, bf16[2,4,16,8192]{3,2,0,1:T(8,128)(2,1)}, u32[]{:S(2)}, u32[]{:S(2)}) collective-permute-start(bf16[2,4,16,8192]{3,2,0,1:T(8,128)(2,1)} %bitcast.118), channel_id=1, source_target_pairs={{0,1},{1,0},{2,3},{3,2},{4,5},{5,4},{6,7},{7,6},{8,9},{9,8},{10,11... | collective-permute-start | bytes 6291464 | tf_op jit(solution)/shard_map/ppermute | solution.py:115
  278.7 2.0 copy-start
  280.7 67.3 %copy-start.1 = (bf16[16,8192]{1,0:T(8,128)(2,1)S(1)}, bf16[16,8192]{1,0:T(8,128)(2,1)}, u32[]{:S(2)}) copy-start(bf16[16,8192]{1,0:T(8,128)(2,1)} %param.8) | copy-start | bytes 786436
  280.9 16.7 %collective-permute-start.11 = (bf16[2,16,8192]{2,1,0:T(8,128)(2,1)S(1)}, bf16[2,16,8192]{2,1,0:T(8,128)(2,1)S(1)}, u32[]{:S(2)}, u32[]{:S(2)}) collective-permute-start(bf16[2,16,8192]{2,1,0:T(8,128)(2,1)S(1)} %get-tuple-element.22), channel_id=1, source_target_pairs={{0,2},{2,4},{4,6},{6,0},{1,3},{3,5},{5,7},{7,1},{8,10},{10,12},{12... | collective-permute-start | bytes 1572872 | tf_op jit(solution)/shard_map/ppermute | solution.py:120
  284.3 18.3 %collective-permute-start.12 = (bf16[2,16,8192]{2,1,0:T(8,128)(2,1)S(1)}, bf16[2,16,8192]{2,1,0:T(8,128)(2,1)S(1)}, u32[]{:S(2)}, u32[]{:S(2)}) collective-permute-start(bf16[2,16,8192]{2,1,0:T(8,128)(2,1)S(1)} %get-tuple-element.24), channel_id=1, source_target_pairs={{0,4},{2,6},{4,0},{6,2},{1,5},{3,7},{5,1},{7,3},{8,12},{10,14},{12... | collective-permute-start | bytes 1572872 | tf_op jit(solution)/shard_map/ppermute | solution.py:120
  287.3 25.3 %collective-permute-start.13 = (bf16[2,16,8192]{2,1,0:T(8,128)(2,1)S(1)}, bf16[2,16,8192]{2,1,0:T(8,128)(2,1)S(1)}, u32[]{:S(2)}, u32[]{:S(2)}) collective-permute-start(bf16[2,16,8192]{2,1,0:T(8,128)(2,1)S(1)} %get-tuple-element.23), channel_id=1, source_target_pairs={{0,6},{2,0},{4,2},{6,4},{1,7},{3,1},{5,3},{7,5},{8,14},{10,8},{12,... | collective-permute-start | bytes 1572872 | tf_op jit(solution)/shard_map/ppermute | solution.py:120
  314.1 33.9 %collective-permute-start.14 = (bf16[16,8192]{1,0:T(8,128)(2,1)S(1)}, bf16[16,8192]{1,0:T(8,128)(2,1)S(1)}, u32[]{:S(2)}, u32[]{:S(2)}) collective-permute-start(bf16[16,8192]{1,0:T(8,128)(2,1)S(1)} %fusion.22), channel_id=1, source_target_pairs={{0,8},{8,0},{1,9},{9,1},{2,10},{10,2},{3,11},{11,3},{4,12},{12,4},... | collective-permute-start | bytes 786440 | tf_op jit(solution)/shard_map/ppermute | solution.py:121
Sparse Core Ops, SparseCore 0:
  13.6 71.8 all-gather.8
  129.0 77.0 all-gather.4
  208.2 56.6 all-gather.6

commit v7 on v5

--- a/solution.py
+++ b/solution.py
@@ -129,13 +129,13 @@
     stacked = jnp.concatenate([w_query, w_key, w_value], axis=1)
     normed = normalize(tokens, norm_gain)
     stacked, normed = lax.optimization_barrier((stacked, normed))
-    payload = jnp.concatenate([stacked.reshape(-1), w_out.reshape(-1)])
-    along_zl = lax.all_gather(payload, "zl", axis=0)
-    in_part = along_zl[:, : stacked.size].reshape(-1, stacked.shape[1])
-    out_part = along_zl[:, stacked.size :].reshape((-1,) + w_out.shape)
-    weights = lax.all_gather(in_part, "x", axis=0, tiled=True)
-    weights, out_part = lax.optimization_barrier((weights, out_part))
+    payload = jnp.concatenate([stacked, w_out], axis=1)
+    along_zl = lax.all_gather(payload, "zl", axis=0, tiled=True)
+    in_part = along_zl[:, : stacked.shape[1]]
+    out_part = along_zl[:, stacked.shape[1] :].reshape((-1,) + w_out.shape)
     out_part = jnp.transpose(out_part, (1, 0, 2)).reshape(w_out.shape[0], -1)
+    in_part, out_part, normed = lax.optimization_barrier((in_part, out_part, normed))
+    weights = ring_gather(in_part, "x", 4).reshape(-1, in_part.shape[1])
     out_weights = lax.all_gather(out_part, "x", axis=1, tiled=True)
     gathered = group_gather(normed)
     row_count = gathered.shape[0]

time: 363 us -> 360 us (level)
  the two profiles are of different devices: /device:TPU:40 before, /device:TPU:1 now
where the time goes in v7:
time: 360 us; the launch traced here: 359 us
  waiting for transfers between devices  212 us (59%)
  starting transfers between devices  68.5 us (19%)
  local copies, waits for them, and re-layouts  41.8 us (12%)
  other arithmetic  16.5 us (5%)
  between operations  14.1 us (4%)
  matrix products  6.47 us (2%)
    ppermute x10, waiting for transfers between devices, ring_gather(): ahead = lax.ppermute(ahead, axis_name, forward)  81.3 us
    all_gather x1, waiting for transfers between devices, body(): along_zl = lax.all_gather(payload, 'zl', axis=0, tiled=True)  79.6 us
    ppermute x10, starting transfers between devices, ring_gather(): ahead = lax.ppermute(ahead, axis_name, forward)  37.3 us
    ppermute x1, waiting for transfers between devices, group_reduce_scatter(): lax.ppermute(take(mine, 1 - zh_index, 0).astype(jnp.bfloat16), 'zh', swap)  25.2 us
    ppermute x3, waiting for transfers between devices, group_reduce_scatter(): lax.ppermute(outgoing, 'y', [(s, (s + shift) % 4) for s in range(4)])  21.3 us
    unnamed x33, local copies, waits for them, and re-layouts  16.4 us
    ppermute x3, starting transfers between devices, ring_gather(): behind = lax.ppermute(behind, axis_name, backward)  13.1 us
    ppermute x3, starting transfers between devices, group_reduce_scatter(): lax.ppermute(outgoing, 'y', [(s, (s + shift) % 4) for s in range(4)])  8.41 us
  transfers between devices with their start and end apart: 20, of which 13 were waited for; matrix products, arithmetic and copies ran while one was open for 12% of the time, Pallas kernels for 0%

profile of v7, /device:TPU:1, one launch (start us, length us, event | category | flops | bytes accessed | tf_op | source)
XLA Modules:
  0.0 359.0 jit_solution(6259827226247867304)
XLA Ops:
  11.4 1.8 pad_maximum_fusion
  13.3 79.6 %all-gather.3.cloned.1.call-done = bf16[2048,576]{1,0:T(8,128)(2,1)} async-done(((bf16[256,576]{1,0:T(8,128)(2,1)}), bf16[2048,576]{1,0:T(8,128)(2,1)}) %all-gather.3.cloned.1.call-update) | async-done | bytes 2359312 | tf_op jit(solution)/shard_map/all_gather | solution.py:133
  93.0 1.8 slice.46
  96.2 1.6 slice.45
  97.7 6.6 %collective-permute-start = (bf16[16,8192]{1,0:T(8,128)(2,1)S(1)}, bf16[16,8192]{1,0:T(8,128)(2,1)S(1)}, u32[]{:S(2)}, u32[]{:S(2)}) collective-permute-start(bf16[16,8192]{1,0:T(8,128)(2,1)S(1)} %fusion.10), channel_id=1, source_target_pairs={{0,8},{8,0},{1,9},{9,1},{2,10},{10,2},{3,11},{11,3},{4,12},{12,4},... | collective-permute-start | bytes 786440 | tf_op jit(solution)/shard_map/ppermute | solution.py:85
  105.0 1.6 copy.54
  106.6 4.3 %collective-permute-start.5 = (bf16[2048,320]{0,1:T(8,128)(2,1)}, bf16[2048,320]{0,1:T(8,128)(2,1)}, u32[]{:S(2)}, u32[]{:S(2)}) collective-permute-start(bf16[2048,320]{0,1:T(8,128)(2,1)} %copy.54), channel_id=1, source_target_pairs={{0,384},{128,0},{256,128},{384,256},{1,385},{129,1},{257,129},{385... | collective-permute-start | bytes 3932168 | tf_op jit(solution)/shard_map/ppermute | solution.py:88
  110.9 1.9 collective-permute-start.6
  112.8 17.9 %collective-permute-done = bf16[16,8192]{1,0:T(8,128)(2,1)S(1)} collective-permute-done((bf16[16,8192]{1,0:T(8,128)(2,1)S(1)}, bf16[16,8192]{1,0:T(8,128)(2,1)S(1)}, u32[]{:S(2)}, u32[]{:S(2)}) %collective-permute-start) | collective-permute-done | bytes 262176 | tf_op jit(solution)/shard_map/ppermute | solution.py:85
  131.1 4.4 %collective-permute-start.1 = (bf16[2,16,8192]{2,1,0:T(8,128)(2,1)S(1)}, bf16[2,16,8192]{2,1,0:T(8,128)(2,1)S(1)}, u32[]{:S(2)}, u32[]{:S(2)}) collective-permute-start(bf16[2,16,8192]{2,1,0:T(8,128)(2,1)S(1)} %get-tuple-element.19), channel_id=1, source_target_pairs={{0,6},{2,0},{4,2},{6,4},{1,7},{3,1},{5,3},{7,5},{8,14},{10,8},{12,... | collective-permute-start | bytes 1572872 | tf_op jit(solution)/shard_map/ppermute | solution.py:88
  135.4 1.9 collective-permute-start.2
  138.7 12.6 %collective-permute-done.2 = bf16[2,16,8192]{2,1,0:T(8,128)(2,1)S(1)} collective-permute-done((bf16[2,16,8192]{2,1,0:T(8,128)(2,1)S(1)}, bf16[2,16,8192]{2,1,0:T(8,128)(2,1)S(1)}, u32[]{:S(2)}, u32[]{:S(2)}) %collective-permute-start.2) | collective-permute-done | bytes 524320 | tf_op jit(solution)/shard_map/ppermute | solution.py:85
  151.3 1.9 collective-permute-start.3
  153.3 13.1 %collective-permute-done.3 = bf16[2,16,8192]{2,1,0:T(8,128)(2,1)S(1)} collective-permute-done((bf16[2,16,8192]{2,1,0:T(8,128)(2,1)S(1)}, bf16[2,16,8192]{2,1,0:T(8,128)(2,1)S(1)}, u32[]{:S(2)}, u32[]{:S(2)}) %collective-permute-start.3) | collective-permute-done | bytes 524320 | tf_op jit(solution)/shard_map/ppermute | solution.py:85
  166.6 1.5 constant_dynamic-slice_fusion.4
  168.1 4.3 %collective-permute-start.4 = (bf16[4,2,16,8192]{3,2,0,1:T(8,128)(2,1)}, bf16[4,2,16,8192]{3,2,0,1:T(8,128)(2,1)}, u32[]{:S(2)}, u32[]{:S(2)}) collective-permute-start(bf16[4,2,16,8192]{3,2,0,1:T(8,128)(2,1)} %constant_dynamic-slice_fusion.4), channel_id=1, source_target_pairs={{0,1},{1,0},{2,3},{3,2},{4,5},{5,4},{6,7},{7,6},{8,9},{9,8},{10,11... | collective-permute-start | bytes 6291464 | tf_op jit(solution)/shard_map/ppermute | solution.py:85
  172.4 3.0 collective-permute-start.7
  175.4 1.5 fusion.46
  176.9 1.8 copy.58
  178.8 2.6 copy.55
  181.3 2.7 bitcast_dynamic-update-slice_fusion.4
  184.1 22.6 %collective-permute-done.7 = bf16[2048,320]{0,1:T(8,128)(2,1)} collective-permute-done((bf16[2048,320]{0,1:T(8,128)(2,1)}, bf16[2048,320]{0,1:T(8,128)(2,1)}, u32[]{:S(2)}, u32[]{:S(2)}) %collective-permute-start.7) | collective-permute-done | bytes 1310752 | tf_op jit(solution)/shard_map/ppermute | solution.py:85
  206.7 2.6 copy.57
  209.3 2.8 bitcast_dynamic-update-slice_fusion.2
  218.9 3.6 constant_dynamic-slice_fusion.3
  222.4 5.2 %fusion.2 = bf16[2,4,2,16,8192]{4,3,0,1,2:T(8,128)(2,1)S(1)} fusion(s32[]{:T(128)S(6)} %select_n.148, bf16[1,4,2,16,8192]{4,3,0,1,2:T(8,128)(2,1)S(1)} %copy-done.3, bf16[1,4,2,16,8192]{4,3,0,1,2:T(8,128)(2,1)} %bitcast.14), kind=kLoop, calls=%fused_computation.9 | loop fusion | flops 6291456 | bytes 8388612 | tf_op jit(solution)/shard_map/jit(_roll_dynamic)/concatenate | solution.py:91
  227.6 2.5 fusion.40
  230.2 7.4 %collective-permute-start.8 = (bf16[64,256]{1,0:T(8,128)(2,1)S(1)}, bf16[64,256]{1,0:T(8,128)(2,1)S(1)}, u32[]{:S(2)}, u32[]{:S(2)}) collective-permute-start(bf16[64,256]{1,0:T(8,128)(2,1)S(1)} %get-tuple-element.32), channel_id=1, source_target_pairs={{0,8},{8,0},{1,9},{9,1},{2,10},{10,2},{3,11},{11,3},{4,12},{12,4},... | collective-permute-start | bytes 98312 | tf_op jit(solution)/shard_map/ppermute | solution.py:85
  237.7 5.9 %collective-permute-done.8 = bf16[64,256]{1,0:T(8,128)(2,1)S(1)} collective-permute-done((bf16[64,256]{1,0:T(8,128)(2,1)S(1)}, bf16[64,256]{1,0:T(8,128)(2,1)S(1)}, u32[]{:S(2)}, u32[]{:S(2)}) %collective-permute-start.8) | collective-permute-done | bytes 32800 | tf_op jit(solution)/shard_map/ppermute | solution.py:85
  243.6 4.4 %collective-permute-start.9 = (bf16[2,64,256]{2,1,0:T(8,128)(2,1)S(1)}, bf16[2,64,256]{2,1,0:T(8,128)(2,1)S(1)}, u32[]{:S(2)}, u32[]{:S(2)}) collective-permute-start(bf16[2,64,256]{2,1,0:T(8,128)(2,1)S(1)} %get-tuple-element.17), channel_id=1, source_target_pairs={{0,6},{2,0},{4,2},{6,4},{1,7},{3,1},{5,3},{7,5},{8,14},{10,8},{12,... | collective-permute-start | bytes 196616 | tf_op jit(solution)/shard_map/ppermute | solution.py:88
  248.1 1.9 collective-permute-start.10
  250.3 4.0 %collective-permute-done.10 = bf16[2,64,256]{2,1,0:T(8,128)(2,1)S(1)} collective-permute-done((bf16[2,64,256]{2,1,0:T(8,128)(2,1)S(1)}, bf16[2,64,256]{2,1,0:T(8,128)(2,1)S(1)}, u32[]{:S(2)}, u32[]{:S(2)}) %collective-permute-start.10) | collective-permute-done | bytes 65568 | tf_op jit(solution)/shard_map/ppermute | solution.py:85
  254.3 1.9 collective-permute-start.11
  256.2 4.3 %collective-permute-done.11 = bf16[2,64,256]{2,1,0:T(8,128)(2,1)S(1)} collective-permute-done((bf16[2,64,256]{2,1,0:T(8,128)(2,1)S(1)}, bf16[2,64,256]{2,1,0:T(8,128)(2,1)S(1)}, u32[]{:S(2)}, u32[]{:S(2)}) %collective-permute-start.11) | collective-permute-done | bytes 65568 | tf_op jit(solution)/shard_map/ppermute | solution.py:85
  260.6 6.4 %collective-permute-start.12 = (bf16[4,2,64,256]{3,2,1,0:T(8,128)(2,1)S(1)}, bf16[4,2,64,256]{3,2,1,0:T(8,128)(2,1)S(1)}, u32[]{:S(2)}, u32[]{:S(2)}) collective-permute-start(bf16[4,2,64,256]{3,2,1,0:T(8,128)(2,1)S(1)} %constant_dynamic-slice_fusion.2), channel_id=1, source_target_pairs={{0,1},{1,0},{2,3},{3,2},{4,5},{5,4},{6,7},{7,6},{8,9},{9,8},{10,11... | collective-permute-start | bytes 786440 | tf_op jit(solution)/shard_map/ppermute | solution.py:85
  271.6 3.5 convolution_convert_fusion
  275.4 1.5 copy.92
  276.9 2.3 collective-permute-start.13
  279.2 4.1 %collective-permute-done.13 = bf16[2,4,16,8192]{3,2,0,1:T(8,128)(2,1)} collective-permute-done((bf16[2,4,16,8192]{3,2,0,1:T(8,128)(2,1)}, bf16[2,4,16,8192]{3,2,0,1:T(8,128)(2,1)}, u32[]{:S(2)}, u32[]{:S(2)}) %collective-permute-start.13) | collective-permute-done | bytes 2097184 | tf_op jit(solution)/shard_map/ppermute | solution.py:115
  283.3 2.1 convert_add_fusion
  285.4 1.9 copy-done.2
  287.5 1.9 collective-permute-start.14
  289.5 2.5 collective-permute-start.15
  291.9 4.0 %collective-permute-start.16 = (bf16[2,16,8192]{2,1,0:T(8,128)(2,1)S(1)}, bf16[2,16,8192]{2,1,0:T(8,128)(2,1)S(1)}, u32[]{:S(2)}, u32[]{:S(2)}) collective-permute-start(bf16[2,16,8192]{2,1,0:T(8,128)(2,1)S(1)} %get-tuple-element.21), channel_id=1, source_target_pairs={{0,6},{2,0},{4,2},{6,4},{1,7},{3,1},{5,3},{7,5},{8,14},{10,8},{12,... | collective-permute-start | bytes 1572872 | tf_op jit(solution)/shard_map/ppermute | solution.py:120
  296.0 19.0 %collective-permute-done.14 = bf16[2,16,8192]{2,1,0:T(8,128)(2,1)S(1)} collective-permute-done((bf16[2,16,8192]{2,1,0:T(8,128)(2,1)S(1)}, bf16[2,16,8192]{2,1,0:T(8,128)(2,1)S(1)}, u32[]{:S(2)}, u32[]{:S(2)}) %collective-permute-start.14) | collective-permute-done | bytes 524320 | tf_op jit(solution)/shard_map/ppermute | solution.py:120
  315.0 2.2 collective-permute-done.16
  318.7 7.4 %collective-permute-start.17 = (bf16[16,8192]{1,0:T(8,128)(2,1)S(1)}, bf16[16,8192]{1,0:T(8,128)(2,1)S(1)}, u32[]{:S(2)}, u32[]{:S(2)}) collective-permute-start(bf16[16,8192]{1,0:T(8,128)(2,1)S(1)} %fusion.22), channel_id=1, source_target_pairs={{0,8},{8,0},{1,9},{9,1},{2,10},{10,2},{3,11},{11,3},{4,12},{12,4},... | collective-permute-start | bytes 786440 | tf_op jit(solution)/shard_map/ppermute | solution.py:121
  326.1 25.2 %collective-permute-done.17 = bf16[16,8192]{1,0:T(8,128)(2,1)S(1)} collective-permute-done((bf16[16,8192]{1,0:T(8,128)(2,1)S(1)}, bf16[16,8192]{1,0:T(8,128)(2,1)S(1)}, u32[]{:S(2)}, u32[]{:S(2)}) %collective-permute-start.17) | collective-permute-done | bytes 262176 | tf_op jit(solution)/shard_map/ppermute | solution.py:121
  (86 shorter events, 23.2 us)
Async XLA Ops:
  6.5 86.4 %all-gather.3.cloned.1.call-start = ((), (), s32[]{:S(2)}) async-start(), calls=%async_computation | async-start | bytes 2949120 | tf_op jit(solution)/shard_map/all_gather | solution.py:133
  13.2 258.4 %all-gather.5.cloned.1.call-start = ((), (), s32[]{:S(2)}) async-start(), calls=%async_computation.1 | async-start | bytes 5242880 | tf_op jit(solution)/shard_map/all_gather | solution.py:139
  97.7 33.0 %collective-permute-start = (bf16[16,8192]{1,0:T(8,128)(2,1)S(1)}, bf16[16,8192]{1,0:T(8,128)(2,1)S(1)}, u32[]{:S(2)}, u32[]{:S(2)}) collective-permute-start(bf16[16,8192]{1,0:T(8,128)(2,1)S(1)} %fusion.10), channel_id=1, source_target_pairs={{0,8},{8,0},{1,9},{9,1},{2,10},{10,2},{3,11},{11,3},{4,12},{12,4},... | collective-permute-start | bytes 786440 | tf_op jit(solution)/shard_map/ppermute | solution.py:85
  106.6 72.2 %collective-permute-start.5 = (bf16[2048,320]{0,1:T(8,128)(2,1)}, bf16[2048,320]{0,1:T(8,128)(2,1)}, u32[]{:S(2)}, u32[]{:S(2)}) collective-permute-start(bf16[2048,320]{0,1:T(8,128)(2,1)} %copy.54), channel_id=1, source_target_pairs={{0,384},{128,0},{256,128},{384,256},{1,385},{129,1},{257,129},{385... | collective-permute-start | bytes 3932168 | tf_op jit(solution)/shard_map/ppermute | solution.py:88
  110.9 61.5 %collective-permute-start.6 = (bf16[2048,320]{0,1:T(8,128)(2,1)}, bf16[2048,320]{0,1:T(8,128)(2,1)}, u32[]{:S(2)}, u32[]{:S(2)}) collective-permute-start(bf16[2048,320]{0,1:T(8,128)(2,1)} %copy.54), channel_id=1, source_target_pairs={{0,128},{128,256},{256,384},{384,0},{1,129},{129,257},{257,385},{3... | collective-permute-start | bytes 3932168 | tf_op jit(solution)/shard_map/ppermute | solution.py:85
  131.1 22.2 %collective-permute-start.1 = (bf16[2,16,8192]{2,1,0:T(8,128)(2,1)S(1)}, bf16[2,16,8192]{2,1,0:T(8,128)(2,1)S(1)}, u32[]{:S(2)}, u32[]{:S(2)}) collective-permute-start(bf16[2,16,8192]{2,1,0:T(8,128)(2,1)S(1)} %get-tuple-element.19), channel_id=1, source_target_pairs={{0,6},{2,0},{4,2},{6,4},{1,7},{3,1},{5,3},{7,5},{8,14},{10,8},{12,... | collective-permute-start | bytes 1572872 | tf_op jit(solution)/shard_map/ppermute | solution.py:88
  135.4 15.9 %collective-permute-start.2 = (bf16[2,16,8192]{2,1,0:T(8,128)(2,1)S(1)}, bf16[2,16,8192]{2,1,0:T(8,128)(2,1)S(1)}, u32[]{:S(2)}, u32[]{:S(2)}) collective-permute-start(bf16[2,16,8192]{2,1,0:T(8,128)(2,1)S(1)} %get-tuple-element.19), channel_id=1, source_target_pairs={{0,2},{2,4},{4,6},{6,0},{1,3},{3,5},{5,7},{7,1},{8,10},{10,12},{12... | collective-permute-start | bytes 1572872 | tf_op jit(solution)/shard_map/ppermute | solution.py:85
  151.3 15.1 %collective-permute-start.3 = (bf16[2,16,8192]{2,1,0:T(8,128)(2,1)S(1)}, bf16[2,16,8192]{2,1,0:T(8,128)(2,1)S(1)}, u32[]{:S(2)}, u32[]{:S(2)}) collective-permute-start(bf16[2,16,8192]{2,1,0:T(8,128)(2,1)S(1)} %collective-permute-done.2), channel_id=1, source_target_pairs={{0,2},{2,4},{4,6},{6,0},{1,3},{3,5},{5,7},{7,1},{8,10},{10,12},{12... | collective-permute-start | bytes 1572872 | tf_op jit(solution)/shard_map/ppermute | solution.py:85
  168.1 54.3 %collective-permute-start.4 = (bf16[4,2,16,8192]{3,2,0,1:T(8,128)(2,1)}, bf16[4,2,16,8192]{3,2,0,1:T(8,128)(2,1)}, u32[]{:S(2)}, u32[]{:S(2)}) collective-permute-start(bf16[4,2,16,8192]{3,2,0,1:T(8,128)(2,1)} %constant_dynamic-slice_fusion.4), channel_id=1, source_target_pairs={{0,1},{1,0},{2,3},{3,2},{4,5},{5,4},{6,7},{7,6},{8,9},{9,8},{10,11... | collective-permute-start | bytes 6291464 | tf_op jit(solution)/shard_map/ppermute | solution.py:85
  172.4 34.3 %collective-permute-start.7 = (bf16[2048,320]{0,1:T(8,128)(2,1)}, bf16[2048,320]{0,1:T(8,128)(2,1)}, u32[]{:S(2)}, u32[]{:S(2)}) collective-permute-start(bf16[2048,320]{0,1:T(8,128)(2,1)} %collective-permute-done.6), channel_id=1, source_target_pairs={{0,128},{128,256},{256,384},{384,0},{1,129},{129,257},{257,385},{3... | collective-permute-start | bytes 3932168 | tf_op jit(solution)/shard_map/ppermute | solution.py:85
  209.3 5.5 %copy-start = (bf16[2048,320]{1,0:T(8,128)(2,1)S(1)}, bf16[2048,320]{1,0:T(8,128)(2,1)}, u32[]{:S(2)}) copy-start(bf16[2048,320]{1,0:T(8,128)(2,1)} %copy.55) | copy-start | bytes 3932164
  212.1 4.1 %copy-start.1 = (bf16[2048,320]{1,0:T(8,128)(2,1)S(1)}, bf16[2048,320]{1,0:T(8,128)(2,1)}, u32[]{:S(2)}) copy-start(bf16[2048,320]{1,0:T(8,128)(2,1)} %copy.57) | copy-start | bytes 3932164
  218.9 3.6 copy-start.3
  230.2 13.4 %collective-permute-start.8 = (bf16[64,256]{1,0:T(8,128)(2,1)S(1)}, bf16[64,256]{1,0:T(8,128)(2,1)S(1)}, u32[]{:S(2)}, u32[]{:S(2)}) collective-permute-start(bf16[64,256]{1,0:T(8,128)(2,1)S(1)} %get-tuple-element.32), channel_id=1, source_target_pairs={{0,8},{8,0},{1,9},{9,1},{2,10},{10,2},{3,11},{11,3},{4,12},{12,4},... | collective-permute-start | bytes 98312 | tf_op jit(solution)/shard_map/ppermute | solution.py:85
  243.6 12.6 %collective-permute-start.9 = (bf16[2,64,256]{2,1,0:T(8,128)(2,1)S(1)}, bf16[2,64,256]{2,1,0:T(8,128)(2,1)S(1)}, u32[]{:S(2)}, u32[]{:S(2)}) collective-permute-start(bf16[2,64,256]{2,1,0:T(8,128)(2,1)S(1)} %get-tuple-element.17), channel_id=1, source_target_pairs={{0,6},{2,0},{4,2},{6,4},{1,7},{3,1},{5,3},{7,5},{8,14},{10,8},{12,... | collective-permute-start | bytes 196616 | tf_op jit(solution)/shard_map/ppermute | solution.py:88
  248.1 6.2 %collective-permute-start.10 = (bf16[2,64,256]{2,1,0:T(8,128)(2,1)S(1)}, bf16[2,64,256]{2,1,0:T(8,128)(2,1)S(1)}, u32[]{:S(2)}, u32[]{:S(2)}) collective-permute-start(bf16[2,64,256]{2,1,0:T(8,128)(2,1)S(1)} %get-tuple-element.17), channel_id=1, source_target_pairs={{0,2},{2,4},{4,6},{6,0},{1,3},{3,5},{5,7},{7,1},{8,10},{10,12},{12... | collective-permute-start | bytes 196616 | tf_op jit(solution)/shard_map/ppermute | solution.py:85
  254.3 6.2 %collective-permute-start.11 = (bf16[2,64,256]{2,1,0:T(8,128)(2,1)S(1)}, bf16[2,64,256]{2,1,0:T(8,128)(2,1)S(1)}, u32[]{:S(2)}, u32[]{:S(2)}) collective-permute-start(bf16[2,64,256]{2,1,0:T(8,128)(2,1)S(1)} %collective-permute-done.10), channel_id=1, source_target_pairs={{0,2},{2,4},{4,6},{6,0},{1,3},{3,5},{5,7},{7,1},{8,10},{10,12},{12... | collective-permute-start | bytes 196616 | tf_op jit(solution)/shard_map/ppermute | solution.py:85
  260.6 7.5 %collective-permute-start.12 = (bf16[4,2,64,256]{3,2,1,0:T(8,128)(2,1)S(1)}, bf16[4,2,64,256]{3,2,1,0:T(8,128)(2,1)S(1)}, u32[]{:S(2)}, u32[]{:S(2)}) collective-permute-start(bf16[4,2,64,256]{3,2,1,0:T(8,128)(2,1)S(1)} %constant_dynamic-slice_fusion.2), channel_id=1, source_target_pairs={{0,1},{1,0},{2,3},{3,2},{4,5},{5,4},{6,7},{7,6},{8,9},{9,8},{10,11... | collective-permute-start | bytes 786440 | tf_op jit(solution)/shard_map/ppermute | solution.py:85
  276.9 6.4 %collective-permute-start.13 = (bf16[2,4,16,8192]{3,2,0,1:T(8,128)(2,1)}, bf16[2,4,16,8192]{3,2,0,1:T(8,128)(2,1)}, u32[]{:S(2)}, u32[]{:S(2)}) collective-permute-start(bf16[2,4,16,8192]{3,2,0,1:T(8,128)(2,1)} %bitcast.129), channel_id=1, source_target_pairs={{0,1},{1,0},{2,3},{3,2},{4,5},{5,4},{6,7},{7,6},{8,9},{9,8},{10,11... | collective-permute-start | bytes 6291464 | tf_op jit(solution)/shard_map/ppermute | solution.py:115
  285.4 2.0 copy-start.2
  287.3 64.0 %copy-start.4 = (bf16[16,8192]{1,0:T(8,128)(2,1)S(1)}, bf16[16,8192]{1,0:T(8,128)(2,1)}, u32[]{:S(2)}) copy-start(bf16[16,8192]{1,0:T(8,128)(2,1)} %param.8) | copy-start | bytes 786436
  287.5 27.5 %collective-permute-start.14 = (bf16[2,16,8192]{2,1,0:T(8,128)(2,1)S(1)}, bf16[2,16,8192]{2,1,0:T(8,128)(2,1)S(1)}, u32[]{:S(2)}, u32[]{:S(2)}) collective-permute-start(bf16[2,16,8192]{2,1,0:T(8,128)(2,1)S(1)} %get-tuple-element.20), channel_id=1, source_target_pairs={{0,2},{2,4},{4,6},{6,0},{1,3},{3,5},{5,7},{7,1},{8,10},{10,12},{12... | collective-permute-start | bytes 1572872 | tf_op jit(solution)/shard_map/ppermute | solution.py:120
  289.5 25.6 %collective-permute-start.15 = (bf16[2,16,8192]{2,1,0:T(8,128)(2,1)S(1)}, bf16[2,16,8192]{2,1,0:T(8,128)(2,1)S(1)}, u32[]{:S(2)}, u32[]{:S(2)}) collective-permute-start(bf16[2,16,8192]{2,1,0:T(8,128)(2,1)S(1)} %get-tuple-element.22), channel_id=1, source_target_pairs={{0,4},{2,6},{4,0},{6,2},{1,5},{3,7},{5,1},{7,3},{8,12},{10,14},{12... | collective-permute-start | bytes 1572872 | tf_op jit(solution)/shard_map/ppermute | solution.py:120
  291.9 25.3 %collective-permute-start.16 = (bf16[2,16,8192]{2,1,0:T(8,128)(2,1)S(1)}, bf16[2,16,8192]{2,1,0:T(8,128)(2,1)S(1)}, u32[]{:S(2)}, u32[]{:S(2)}) collective-permute-start(bf16[2,16,8192]{2,1,0:T(8,128)(2,1)S(1)} %get-tuple-element.21), channel_id=1, source_target_pairs={{0,6},{2,0},{4,2},{6,4},{1,7},{3,1},{5,3},{7,5},{8,14},{10,8},{12,... | collective-permute-start | bytes 1572872 | tf_op jit(solution)/shard_map/ppermute | solution.py:120
  318.7 32.6 %collective-permute-start.17 = (bf16[16,8192]{1,0:T(8,128)(2,1)S(1)}, bf16[16,8192]{1,0:T(8,128)(2,1)S(1)}, u32[]{:S(2)}, u32[]{:S(2)}) collective-permute-start(bf16[16,8192]{1,0:T(8,128)(2,1)S(1)} %fusion.22), channel_id=1, source_target_pairs={{0,8},{8,0},{1,9},{9,1},{2,10},{10,2},{3,11},{11,3},{4,12},{12,4},... | collective-permute-start | bytes 786440 | tf_op jit(solution)/shard_map/ppermute | solution.py:121
Sparse Core Ops, SparseCore 0:
  13.3 79.5 all-gather.2
  113.0 66.1 all-gather.4

commit v8 on v7

--- a/solution.py
+++ b/solution.py
@@ -135,7 +135,8 @@
     out_part = along_zl[:, stacked.shape[1] :].reshape((-1,) + w_out.shape)
     out_part = jnp.transpose(out_part, (1, 0, 2)).reshape(w_out.shape[0], -1)
     in_part, out_part, normed = lax.optimization_barrier((in_part, out_part, normed))
-    weights = ring_gather(in_part, "x", 4).reshape(-1, in_part.shape[1])
+    weights = lax.all_gather(in_part, "x", axis=0, tiled=True)
+    weights, out_part = lax.optimization_barrier((weights, out_part))
     out_weights = lax.all_gather(out_part, "x", axis=1, tiled=True)
     gathered = group_gather(normed)
     row_count = gathered.shape[0]

time: 360 us -> 356 us (0.989)
  the two profiles are of different devices: /device:TPU:1 before, /device:TPU:40 now
where the time goes in v8:
time: 356 us; the launch traced here: 355 us
  waiting for transfers between devices  228 us (64%)
  starting transfers between devices  66.8 us (19%)
  local copies, waits for them, and re-layouts  23.4 us (7%)
  other arithmetic  17.3 us (5%)
  between operations  13.7 us (4%)
  matrix products  6.37 us (2%)
    all_gather x1, waiting for transfers between devices, body(): along_zl = lax.all_gather(payload, 'zl', axis=0, tiled=True)  74.4 us
    ppermute x8, waiting for transfers between devices, ring_gather(): ahead = lax.ppermute(ahead, axis_name, forward)  51.4 us
    all_gather x1, waiting for transfers between devices, body(): weights = lax.all_gather(in_part, 'x', axis=0, tiled=True)  43.5 us
    ppermute x8, starting transfers between devices, ring_gather(): ahead = lax.ppermute(ahead, axis_name, forward)  37.5 us
    ppermute x1, waiting for transfers between devices, group_reduce_scatter(): lax.ppermute(take(mine, 1 - zh_index, 0).astype(jnp.bfloat16), 'zh', swap)  22 us
    ppermute x3, waiting for transfers between devices, group_reduce_scatter(): lax.ppermute(outgoing, 'y', [(s, (s + shift) % 4) for s in range(4)])  21.2 us
    ppermute x1, starting transfers between devices, group_reduce_scatter(): lax.ppermute(take(mine, 1 - zh_index, 0).astype(jnp.bfloat16), 'zh', swap)  11.9 us
    all_gather x1, waiting for transfers between devices, body(): out_weights = lax.all_gather(out_part, 'x', axis=1, tiled=True)  10.9 us
  transfers between devices with their start and end apart: 18, of which 15 were waited for; matrix products, arithmetic and copies ran while one was open for 6% of the time, Pallas kernels for 0%

profile of v8, /device:TPU:40, one launch (start us, length us, event | category | flops | bytes accessed | tf_op | source)
XLA Modules:
  0.0 355.4 jit_solution(5901169383294656176)
XLA Ops:
  8.2 1.1 fusion.8
  9.4 1.1 fusion.10
  10.4 1.0 pad_maximum_fusion.2
  11.4 1.8 pad_maximum_fusion
  13.3 74.4 %all-gather.4.cloned.1.call-done = bf16[2048,576]{1,0:T(8,128)(2,1)} async-done(((bf16[256,576]{1,0:T(8,128)(2,1)}), bf16[2048,576]{1,0:T(8,128)(2,1)}) %all-gather.4.cloned.1.call-update) | async-done | bytes 2359312 | tf_op jit(solution)/shard_map/all_gather | solution.py:133
  87.7 1.8 slice.46
  89.5 1.3 copy.30
  90.9 2.7 slice.45
  93.6 8.8 %collective-permute-start = (bf16[16,8192]{1,0:T(8,128)(2,1)S(1)}, bf16[16,8192]{1,0:T(8,128)(2,1)S(1)}, u32[]{:S(2)}, u32[]{:S(2)}) collective-permute-start(bf16[16,8192]{1,0:T(8,128)(2,1)S(1)} %fusion.10), channel_id=1, source_target_pairs={{0,8},{8,0},{1,9},{9,1},{2,10},{10,2},{3,11},{11,3},{4,12},{12,4},... | collective-permute-start | bytes 786440 | tf_op jit(solution)/shard_map/ppermute | solution.py:85
  102.4 19.5 %collective-permute-done = bf16[16,8192]{1,0:T(8,128)(2,1)S(1)} collective-permute-done((bf16[16,8192]{1,0:T(8,128)(2,1)S(1)}, bf16[16,8192]{1,0:T(8,128)(2,1)S(1)}, u32[]{:S(2)}, u32[]{:S(2)}) %collective-permute-start) | collective-permute-done | bytes 262176 | tf_op jit(solution)/shard_map/ppermute | solution.py:85
  121.9 1.1 bitcast_dynamic-update-slice_fusion.6
  123.0 3.4 collective-permute-start.2
  126.4 2.4 collective-permute-start.1
  128.9 9.7 %collective-permute-done.2 = bf16[2,16,8192]{2,1,0:T(8,128)(2,1)S(1)} collective-permute-done((bf16[2,16,8192]{2,1,0:T(8,128)(2,1)S(1)}, bf16[2,16,8192]{2,1,0:T(8,128)(2,1)S(1)}, u32[]{:S(2)}, u32[]{:S(2)}) %collective-permute-start.2) | collective-permute-done | bytes 524320 | tf_op jit(solution)/shard_map/ppermute | solution.py:85
  138.7 3.4 collective-permute-start.3
  142.9 10.6 %collective-permute-done.3 = bf16[2,16,8192]{2,1,0:T(8,128)(2,1)S(1)} collective-permute-done((bf16[2,16,8192]{2,1,0:T(8,128)(2,1)S(1)}, bf16[2,16,8192]{2,1,0:T(8,128)(2,1)S(1)}, u32[]{:S(2)}, u32[]{:S(2)}) %collective-permute-start.3) | collective-permute-done | bytes 524320 | tf_op jit(solution)/shard_map/ppermute | solution.py:85
  156.8 0.9 bitcast_dynamic-update-slice_fusion.1
  158.5 1.7 constant_dynamic-slice_fusion.3
  160.3 1.9 collective-permute-start.4
  162.8 43.5 %all-gather.6.cloned.1.call-done = bf16[8192,320]{1,0:T(8,128)(2,1)} async-done(((bf16[2048,320]{1,0:T(8,128)(2,1)}), bf16[8192,320]{1,0:T(8,128)(2,1)}) %all-gather.6.cloned.1.call-update) | async-done | bytes 5242896 | tf_op jit(solution)/shard_map/all_gather | solution.py:138
  206.3 1.9 fusion.46
  208.3 5.2 %fusion.2 = bf16[2,4,2,16,8192]{4,3,0,1,2:T(8,128)(2,1)S(1)} fusion(s32[]{:T(128)S(6)} %select_n.138, bf16[1,4,2,16,8192]{4,3,0,1,2:T(8,128)(2,1)S(1)} %fusion.46, bf16[1,4,2,16,8192]{4,3,0,1,2:T(8,128)(2,1)} %bitcast.14), kind=kLoop, calls=%fused_computation.9 | loop fusion | flops 6291456 | bytes 8388612 | tf_op jit(solution)/shard_map/jit(_roll_dynamic)/concatenate | solution.py:91
  213.5 2.5 fusion.40
  215.9 11.9 %collective-permute-start.5 = (bf16[64,256]{1,0:T(8,128)(2,1)S(1)}, bf16[64,256]{1,0:T(8,128)(2,1)S(1)}, u32[]{:S(2)}, u32[]{:S(2)}) collective-permute-start(bf16[64,256]{1,0:T(8,128)(2,1)S(1)} %get-tuple-element.36), channel_id=1, source_target_pairs={{0,8},{8,0},{1,9},{9,1},{2,10},{10,2},{3,11},{11,3},{4,12},{12,4},... | collective-permute-start | bytes 98312 | tf_op jit(solution)/shard_map/ppermute | solution.py:85
  227.9 2.6 collective-permute-done.5
  230.5 2.4 collective-permute-start.6
  233.0 3.4 collective-permute-start.7
  236.7 3.2 collective-permute-done.7
  239.9 2.7 collective-permute-start.8
  242.6 4.7 %collective-permute-done.8 = bf16[2,64,256]{2,1,0:T(8,128)(2,1)S(1)} collective-permute-done((bf16[2,64,256]{2,1,0:T(8,128)(2,1)S(1)}, bf16[2,64,256]{2,1,0:T(8,128)(2,1)S(1)}, u32[]{:S(2)}, u32[]{:S(2)}) %collective-permute-start.8) | collective-permute-done | bytes 65568 | tf_op jit(solution)/shard_map/ppermute | solution.py:85
  247.3 2.1 collective-permute-start.9
  249.7 1.1 collective-permute-done.9
  254.2 10.9 %all-gather.8.cloned.1.call-done = bf16[256,8192]{0,1:T(8,128)(2,1)} async-done(((bf16[256,2048]{0,1:T(8,128)(2,1)}), bf16[256,8192]{0,1:T(8,128)(2,1)}) %all-gather.8.cloned.1.call-update) | async-done | bytes 4194320 | tf_op jit(solution)/shard_map/all_gather | solution.py:140
  265.1 3.5 convolution_convert_fusion
  268.9 1.5 copy.68
  270.4 1.9 collective-permute-start.10
  272.4 4.4 %collective-permute-done.10 = bf16[2,4,16,8192]{3,2,0,1:T(8,128)(2,1)} collective-permute-done((bf16[2,4,16,8192]{3,2,0,1:T(8,128)(2,1)}, bf16[2,4,16,8192]{3,2,0,1:T(8,128)(2,1)}, u32[]{:S(2)}, u32[]{:S(2)}) %collective-permute-start.10) | collective-permute-done | bytes 2097184 | tf_op jit(solution)/shard_map/ppermute | solution.py:115
  276.8 2.1 convert_add_fusion
  278.9 2.0 copy-done
  281.0 3.4 collective-permute-start.11
  284.4 3.0 collective-permute-start.12
  287.5 4.0 %collective-permute-start.13 = (bf16[2,16,8192]{2,1,0:T(8,128)(2,1)S(1)}, bf16[2,16,8192]{2,1,0:T(8,128)(2,1)S(1)}, u32[]{:S(2)}, u32[]{:S(2)}) collective-permute-start(bf16[2,16,8192]{2,1,0:T(8,128)(2,1)S(1)} %get-tuple-element.25), channel_id=1, source_target_pairs={{0,6},{2,0},{4,2},{6,4},{1,7},{3,1},{5,3},{7,5},{8,14},{10,8},{12,... | collective-permute-start | bytes 1572872 | tf_op jit(solution)/shard_map/ppermute | solution.py:120
  291.5 6.2 %collective-permute-done.11 = bf16[2,16,8192]{2,1,0:T(8,128)(2,1)S(1)} collective-permute-done((bf16[2,16,8192]{2,1,0:T(8,128)(2,1)S(1)}, bf16[2,16,8192]{2,1,0:T(8,128)(2,1)S(1)}, u32[]{:S(2)}, u32[]{:S(2)}) %collective-permute-start.11) | collective-permute-done | bytes 524320 | tf_op jit(solution)/shard_map/ppermute | solution.py:120
  297.7 5.0 %collective-permute-done.12 = bf16[2,16,8192]{2,1,0:T(8,128)(2,1)S(1)} collective-permute-done((bf16[2,16,8192]{2,1,0:T(8,128)(2,1)S(1)}, bf16[2,16,8192]{2,1,0:T(8,128)(2,1)S(1)}, u32[]{:S(2)}, u32[]{:S(2)}) %collective-permute-start.12) | collective-permute-done | bytes 524320 | tf_op jit(solution)/shard_map/ppermute | solution.py:120
  302.7 10.1 %collective-permute-done.13 = bf16[2,16,8192]{2,1,0:T(8,128)(2,1)S(1)} collective-permute-done((bf16[2,16,8192]{2,1,0:T(8,128)(2,1)S(1)}, bf16[2,16,8192]{2,1,0:T(8,128)(2,1)S(1)}, u32[]{:S(2)}, u32[]{:S(2)}) %collective-permute-start.13) | collective-permute-done | bytes 524320 | tf_op jit(solution)/shard_map/ppermute | solution.py:120
  312.8 1.4 fusion.7
  314.2 11.9 %collective-permute-start.14 = (bf16[16,8192]{1,0:T(8,128)(2,1)S(1)}, bf16[16,8192]{1,0:T(8,128)(2,1)S(1)}, u32[]{:S(2)}, u32[]{:S(2)}) collective-permute-start(bf16[16,8192]{1,0:T(8,128)(2,1)S(1)} %fusion.22), channel_id=1, source_target_pairs={{0,8},{8,0},{1,9},{9,1},{2,10},{10,2},{3,11},{11,3},{4,12},{12,4},... | collective-permute-start | bytes 786440 | tf_op jit(solution)/shard_map/ppermute | solution.py:121
  326.2 22.0 %collective-permute-done.14 = bf16[16,8192]{1,0:T(8,128)(2,1)S(1)} collective-permute-done((bf16[16,8192]{1,0:T(8,128)(2,1)S(1)}, bf16[16,8192]{1,0:T(8,128)(2,1)S(1)}, u32[]{:S(2)}, u32[]{:S(2)}) %collective-permute-start.14) | collective-permute-done | bytes 262176 | tf_op jit(solution)/shard_map/ppermute | solution.py:121
  (69 shorter events, 12.6 us)
Async XLA Ops:
  6.5 81.2 %all-gather.4.cloned.1.call-start = ((), (), s32[]{:S(2)}) async-start(), calls=%async_computation | async-start | bytes 2949120 | tf_op jit(solution)/shard_map/all_gather | solution.py:133
  13.2 193.1 %all-gather.6.cloned.1.call-start = ((), (), s32[]{:S(2)}) async-start(), calls=%async_computation.1 | async-start | bytes 7864320 | tf_op jit(solution)/shard_map/all_gather | solution.py:138
  93.6 28.3 %collective-permute-start = (bf16[16,8192]{1,0:T(8,128)(2,1)S(1)}, bf16[16,8192]{1,0:T(8,128)(2,1)S(1)}, u32[]{:S(2)}, u32[]{:S(2)}) collective-permute-start(bf16[16,8192]{1,0:T(8,128)(2,1)S(1)} %fusion.10), channel_id=1, source_target_pairs={{0,8},{8,0},{1,9},{9,1},{2,10},{10,2},{3,11},{11,3},{4,12},{12,4},... | collective-permute-start | bytes 786440 | tf_op jit(solution)/shard_map/ppermute | solution.py:85
  123.0 15.7 %collective-permute-start.2 = (bf16[2,16,8192]{2,1,0:T(8,128)(2,1)S(1)}, bf16[2,16,8192]{2,1,0:T(8,128)(2,1)S(1)}, u32[]{:S(2)}, u32[]{:S(2)}) collective-permute-start(bf16[2,16,8192]{2,1,0:T(8,128)(2,1)S(1)} %get-tuple-element.23), channel_id=1, source_target_pairs={{0,2},{2,4},{4,6},{6,0},{1,3},{3,5},{5,7},{7,1},{8,10},{10,12},{12... | collective-permute-start | bytes 1572872 | tf_op jit(solution)/shard_map/ppermute | solution.py:85
  126.4 15.7 %collective-permute-start.1 = (bf16[2,16,8192]{2,1,0:T(8,128)(2,1)S(1)}, bf16[2,16,8192]{2,1,0:T(8,128)(2,1)S(1)}, u32[]{:S(2)}, u32[]{:S(2)}) collective-permute-start(bf16[2,16,8192]{2,1,0:T(8,128)(2,1)S(1)} %get-tuple-element.23), channel_id=1, source_target_pairs={{0,6},{2,0},{4,2},{6,4},{1,7},{3,1},{5,3},{7,5},{8,14},{10,8},{12,... | collective-permute-start | bytes 1572872 | tf_op jit(solution)/shard_map/ppermute | solution.py:88
  128.9 136.2 %all-gather.8.cloned.1.call-start = ((), (), s32[]{:S(2)}) async-start(), calls=%async_computation.2 | async-start | bytes 5242880 | tf_op jit(solution)/shard_map/all_gather | solution.py:140
  138.7 14.8 %collective-permute-start.3 = (bf16[2,16,8192]{2,1,0:T(8,128)(2,1)S(1)}, bf16[2,16,8192]{2,1,0:T(8,128)(2,1)S(1)}, u32[]{:S(2)}, u32[]{:S(2)}) collective-permute-start(bf16[2,16,8192]{2,1,0:T(8,128)(2,1)S(1)} %collective-permute-done.2), channel_id=1, source_target_pairs={{0,2},{2,4},{4,6},{6,0},{1,3},{3,5},{5,7},{7,1},{8,10},{10,12},{12... | collective-permute-start | bytes 1572872 | tf_op jit(solution)/shard_map/ppermute | solution.py:85
  160.3 48.0 %collective-permute-start.4 = (bf16[4,2,16,8192]{3,2,0,1:T(8,128)(2,1)S(1)}, bf16[4,2,16,8192]{3,2,0,1:T(8,128)(2,1)}, u32[]{:S(2)}, u32[]{:S(2)}) collective-permute-start(bf16[4,2,16,8192]{3,2,0,1:T(8,128)(2,1)S(1)} %constant_dynamic-slice_fusion.3), channel_id=1, source_target_pairs={{0,1},{1,0},{2,3},{3,2},{4,5},{5,4},{6,7},{7,6},{8,9},{9,8},{10,11... | collective-permute-start | bytes 6291464 | tf_op jit(solution)/shard_map/ppermute | solution.py:85
  206.3 7.1 %slice-start = ((s8[6291456]{0:T(1024)(128)(4,1)}), s8[4194304]{0:T(1024)(128)(4,1)S(1)}, s32[]{:S(2)}) async-start(s8[6291456]{0:T(1024)(128)(4,1)} %bitcast.119), calls=%async_computation.3 | async-start | bytes 8388608
  208.2 5.2 %slice-start.1 = ((s8[6291456]{0:T(1024)(128)(4,1)}), s8[2097152]{0:T(1024)(128)(4,1)S(1)}, s32[]{:S(2)}) async-start(s8[6291456]{0:T(1024)(128)(4,1)} %bitcast.119), calls=%async_computation.4 | async-start | bytes 4194304
  215.9 14.5 %collective-permute-start.5 = (bf16[64,256]{1,0:T(8,128)(2,1)S(1)}, bf16[64,256]{1,0:T(8,128)(2,1)S(1)}, u32[]{:S(2)}, u32[]{:S(2)}) collective-permute-start(bf16[64,256]{1,0:T(8,128)(2,1)S(1)} %get-tuple-element.36), channel_id=1, source_target_pairs={{0,8},{8,0},{1,9},{9,1},{2,10},{10,2},{3,11},{11,3},{4,12},{12,4},... | collective-permute-start | bytes 98312 | tf_op jit(solution)/shard_map/ppermute | solution.py:85
  230.5 12.0 %collective-permute-start.6 = (bf16[2,64,256]{2,1,0:T(8,128)(2,1)S(1)}, bf16[2,64,256]{2,1,0:T(8,128)(2,1)S(1)}, u32[]{:S(2)}, u32[]{:S(2)}) collective-permute-start(bf16[2,64,256]{2,1,0:T(8,128)(2,1)S(1)} %get-tuple-element.21), channel_id=1, source_target_pairs={{0,6},{2,0},{4,2},{6,4},{1,7},{3,1},{5,3},{7,5},{8,14},{10,8},{12,... | collective-permute-start | bytes 196616 | tf_op jit(solution)/shard_map/ppermute | solution.py:88
  233.0 6.9 %collective-permute-start.7 = (bf16[2,64,256]{2,1,0:T(8,128)(2,1)S(1)}, bf16[2,64,256]{2,1,0:T(8,128)(2,1)S(1)}, u32[]{:S(2)}, u32[]{:S(2)}) collective-permute-start(bf16[2,64,256]{2,1,0:T(8,128)(2,1)S(1)} %get-tuple-element.21), channel_id=1, source_target_pairs={{0,2},{2,4},{4,6},{6,0},{1,3},{3,5},{5,7},{7,1},{8,10},{10,12},{12... | collective-permute-start | bytes 196616 | tf_op jit(solution)/shard_map/ppermute | solution.py:85
  239.9 7.4 %collective-permute-start.8 = (bf16[2,64,256]{2,1,0:T(8,128)(2,1)S(1)}, bf16[2,64,256]{2,1,0:T(8,128)(2,1)S(1)}, u32[]{:S(2)}, u32[]{:S(2)}) collective-permute-start(bf16[2,64,256]{2,1,0:T(8,128)(2,1)S(1)} %collective-permute-done.7), channel_id=1, source_target_pairs={{0,2},{2,4},{4,6},{6,0},{1,3},{3,5},{5,7},{7,1},{8,10},{10,12},{12... | collective-permute-start | bytes 196616 | tf_op jit(solution)/shard_map/ppermute | solution.py:85
  247.3 3.4 collective-permute-start.9
  270.4 6.4 %collective-permute-start.10 = (bf16[2,4,16,8192]{3,2,0,1:T(8,128)(2,1)}, bf16[2,4,16,8192]{3,2,0,1:T(8,128)(2,1)}, u32[]{:S(2)}, u32[]{:S(2)}) collective-permute-start(bf16[2,4,16,8192]{3,2,0,1:T(8,128)(2,1)} %bitcast.116), channel_id=1, source_target_pairs={{0,1},{1,0},{2,3},{3,2},{4,5},{5,4},{6,7},{7,6},{8,9},{9,8},{10,11... | collective-permute-start | bytes 6291464 | tf_op jit(solution)/shard_map/ppermute | solution.py:115
  278.9 2.0 copy-start
  280.9 67.3 %copy-start.1 = (bf16[16,8192]{1,0:T(8,128)(2,1)S(1)}, bf16[16,8192]{1,0:T(8,128)(2,1)}, u32[]{:S(2)}) copy-start(bf16[16,8192]{1,0:T(8,128)(2,1)} %param.8) | copy-start | bytes 786436
  281.0 16.7 %collective-permute-start.11 = (bf16[2,16,8192]{2,1,0:T(8,128)(2,1)S(1)}, bf16[2,16,8192]{2,1,0:T(8,128)(2,1)S(1)}, u32[]{:S(2)}, u32[]{:S(2)}) collective-permute-start(bf16[2,16,8192]{2,1,0:T(8,128)(2,1)S(1)} %get-tuple-element.24), channel_id=1, source_target_pairs={{0,2},{2,4},{4,6},{6,0},{1,3},{3,5},{5,7},{7,1},{8,10},{10,12},{12... | collective-permute-start | bytes 1572872 | tf_op jit(solution)/shard_map/ppermute | solution.py:120
  284.4 18.3 %collective-permute-start.12 = (bf16[2,16,8192]{2,1,0:T(8,128)(2,1)S(1)}, bf16[2,16,8192]{2,1,0:T(8,128)(2,1)S(1)}, u32[]{:S(2)}, u32[]{:S(2)}) collective-permute-start(bf16[2,16,8192]{2,1,0:T(8,128)(2,1)S(1)} %get-tuple-element.26), channel_id=1, source_target_pairs={{0,4},{2,6},{4,0},{6,2},{1,5},{3,7},{5,1},{7,3},{8,12},{10,14},{12... | collective-permute-start | bytes 1572872 | tf_op jit(solution)/shard_map/ppermute | solution.py:120
  287.5 25.3 %collective-permute-start.13 = (bf16[2,16,8192]{2,1,0:T(8,128)(2,1)S(1)}, bf16[2,16,8192]{2,1,0:T(8,128)(2,1)S(1)}, u32[]{:S(2)}, u32[]{:S(2)}) collective-permute-start(bf16[2,16,8192]{2,1,0:T(8,128)(2,1)S(1)} %get-tuple-element.25), channel_id=1, source_target_pairs={{0,6},{2,0},{4,2},{6,4},{1,7},{3,1},{5,3},{7,5},{8,14},{10,8},{12,... | collective-permute-start | bytes 1572872 | tf_op jit(solution)/shard_map/ppermute | solution.py:120
  314.2 33.9 %collective-permute-start.14 = (bf16[16,8192]{1,0:T(8,128)(2,1)S(1)}, bf16[16,8192]{1,0:T(8,128)(2,1)S(1)}, u32[]{:S(2)}, u32[]{:S(2)}) collective-permute-start(bf16[16,8192]{1,0:T(8,128)(2,1)S(1)} %fusion.22), channel_id=1, source_target_pairs={{0,8},{8,0},{1,9},{9,1},{2,10},{10,2},{3,11},{11,3},{4,12},{12,4},... | collective-permute-start | bytes 786440 | tf_op jit(solution)/shard_map/ppermute | solution.py:121
Sparse Core Ops, SparseCore 0:
  13.3 74.3 all-gather.3
  129.0 77.2 all-gather.5
  208.4 56.6 all-gather.7

commit v9 on v8

--- a/solution.py
+++ b/solution.py
@@ -167,7 +167,11 @@
         mixed, out_weights, preferred_element_type=jnp.float32
     ).astype(jnp.bfloat16)
     width = partial_out.shape[1]
-    summed = group_reduce_scatter(partial_out.reshape(2, 4, 2, row_count // 16, width))
+    blocks = partial_out.reshape(2, 4, 2, row_count // 16, width)
+    half = width // 2
+    summed = jnp.concatenate(
+        [group_reduce_scatter(blocks[..., :half]), group_reduce_scatter(blocks[..., half:])], axis=-1
+    )
     return (tokens.astype(jnp.float32) + summed).astype(jnp.bfloat16)
 
 

time: 356 us -> 346 us (0.972)
  the two profiles are of different devices: /device:TPU:40 before, /device:TPU:1 now
where the time goes in v9:
time: 346 us; the launch traced here: 342 us
  waiting for transfers between devices  192 us (55%)
  starting transfers between devices  91.9 us (27%)
  local copies, waits for them, and re-layouts  21.5 us (6%)
  other arithmetic  15.8 us (5%)
  between operations  13.9 us (4%)
  matrix products  6.37 us (2%)
    all_gather x1, waiting for transfers between devices, body(): along_zl = lax.all_gather(payload, 'zl', axis=0, tiled=True)  79.7 us
    ppermute x8, waiting for transfers between devices, ring_gather(): ahead = lax.ppermute(ahead, axis_name, forward)  59.6 us
    ppermute x8, starting transfers between devices, ring_gather(): ahead = lax.ppermute(ahead, axis_name, forward)  38 us
    all_gather x1, waiting for transfers between devices, body(): weights = lax.all_gather(in_part, 'x', axis=0, tiled=True)  31.7 us
    ppermute x2, starting transfers between devices, group_reduce_scatter(): lax.ppermute(take(mine, 1 - zh_index, 0).astype(jnp.bfloat16), 'zh', swap)  22.6 us
    ppermute x6, starting transfers between devices, group_reduce_scatter(): lax.ppermute(outgoing, 'y', [(s, (s + shift) % 4) for s in range(4)])  19 us
    ppermute x2, waiting for transfers between devices, group_reduce_scatter(): lax.ppermute(take(mine, 1 - zh_index, 0).astype(jnp.bfloat16), 'zh', swap)  13.6 us
    unnamed x24, local copies, waits for them, and re-layouts  8.13 us
  transfers between devices with their start and end apart: 23, of which 12 were waited for; matrix products, arithmetic and copies ran while one was open for 7% of the time, Pallas kernels for 0%

profile of v9, /device:TPU:1, one launch (start us, length us, event | category | flops | bytes accessed | tf_op | source)
XLA Modules:
  0.0 341.7 jit_solution(8837595858517672727)
XLA Ops:
  7.4 0.8 copy.29
  8.2 1.1 fusion.6
  9.4 1.1 fusion.8
  10.4 1.0 pad_maximum_fusion.2
  11.4 1.8 pad_maximum_fusion
  13.3 79.7 %all-gather.4.cloned.1.call-done = bf16[2048,576]{1,0:T(8,128)(2,1)} async-done(((bf16[256,576]{1,0:T(8,128)(2,1)}), bf16[2048,576]{1,0:T(8,128)(2,1)}) %all-gather.4.cloned.1.call-update) | async-done | bytes 2359312 | tf_op jit(solution)/shard_map/all_gather | solution.py:133
  93.0 1.8 slice.54
  94.8 1.3 copy.30
  96.2 2.7 slice.53
  98.9 6.6 %collective-permute-start = (bf16[16,8192]{1,0:T(8,128)(2,1)S(1)}, bf16[16,8192]{1,0:T(8,128)(2,1)S(1)}, u32[]{:S(2)}, u32[]{:S(2)}) collective-permute-start(bf16[16,8192]{1,0:T(8,128)(2,1)S(1)} %fusion.8), channel_id=1, source_target_pairs={{0,8},{8,0},{1,9},{9,1},{2,10},{10,2},{3,11},{11,3},{4,12},{12,4},... | collective-permute-start | bytes 786440 | tf_op jit(solution)/shard_map/ppermute | solution.py:85
  105.5 26.4 %collective-permute-done = bf16[16,8192]{1,0:T(8,128)(2,1)S(1)} collective-permute-done((bf16[16,8192]{1,0:T(8,128)(2,1)S(1)}, bf16[16,8192]{1,0:T(8,128)(2,1)S(1)}, u32[]{:S(2)}, u32[]{:S(2)}) %collective-permute-start) | collective-permute-done | bytes 262176 | tf_op jit(solution)/shard_map/ppermute | solution.py:85
  131.9 1.1 bitcast_dynamic-update-slice_fusion.6
  133.0 3.1 collective-permute-start.2
  136.1 3.4 collective-permute-start.1
  139.6 9.5 %collective-permute-done.2 = bf16[2,16,8192]{2,1,0:T(8,128)(2,1)S(1)} collective-permute-done((bf16[2,16,8192]{2,1,0:T(8,128)(2,1)S(1)}, bf16[2,16,8192]{2,1,0:T(8,128)(2,1)S(1)}, u32[]{:S(2)}, u32[]{:S(2)}) %collective-permute-start.2) | collective-permute-done | bytes 524320 | tf_op jit(solution)/shard_map/ppermute | solution.py:85
  149.1 1.9 collective-permute-start.3
  151.9 12.5 %collective-permute-done.3 = bf16[2,16,8192]{2,1,0:T(8,128)(2,1)S(1)} collective-permute-done((bf16[2,16,8192]{2,1,0:T(8,128)(2,1)S(1)}, bf16[2,16,8192]{2,1,0:T(8,128)(2,1)S(1)}, u32[]{:S(2)}, u32[]{:S(2)}) %collective-permute-start.3) | collective-permute-done | bytes 524320 | tf_op jit(solution)/shard_map/ppermute | solution.py:85
  166.8 0.8 bitcast_dynamic-update-slice_fusion.3
  167.7 0.8 bitcast_dynamic-update-slice_fusion.1
  169.4 1.7 constant_dynamic-slice_fusion.5
  171.1 4.1 %collective-permute-start.4 = (bf16[4,2,16,8192]{3,2,0,1:T(8,128)(2,1)S(1)}, bf16[4,2,16,8192]{3,2,0,1:T(8,128)(2,1)}, u32[]{:S(2)}, u32[]{:S(2)}) collective-permute-start(bf16[4,2,16,8192]{3,2,0,1:T(8,128)(2,1)S(1)} %constant_dynamic-slice_fusion.5), channel_id=1, source_target_pairs={{0,1},{1,0},{2,3},{3,2},{4,5},{5,4},{6,7},{7,6},{8,9},{9,8},{10,11... | collective-permute-start | bytes 6291464 | tf_op jit(solution)/shard_map/ppermute | solution.py:85
  175.9 31.7 %all-gather.6.cloned.1.call-done = bf16[8192,320]{1,0:T(8,128)(2,1)} async-done(((bf16[2048,320]{1,0:T(8,128)(2,1)}), bf16[8192,320]{1,0:T(8,128)(2,1)}) %all-gather.6.cloned.1.call-update) | async-done | bytes 5242896 | tf_op jit(solution)/shard_map/all_gather | solution.py:138
  207.6 1.9 fusion.53
  209.5 5.2 %fusion.2 = bf16[2,4,2,16,8192]{4,3,0,1,2:T(8,128)(2,1)S(1)} fusion(s32[]{:T(128)S(6)} %select_n.152, bf16[1,4,2,16,8192]{4,3,0,1,2:T(8,128)(2,1)S(1)} %fusion.53, bf16[1,4,2,16,8192]{4,3,0,1,2:T(8,128)(2,1)} %bitcast.14), kind=kLoop, calls=%fused_computation.9 | loop fusion | flops 6291456 | bytes 8388612 | tf_op jit(solution)/shard_map/jit(_roll_dynamic)/concatenate | solution.py:91
  214.8 2.5 fusion.47
  217.2 12.6 %collective-permute-start.5 = (bf16[64,256]{1,0:T(8,128)(2,1)S(1)}, bf16[64,256]{1,0:T(8,128)(2,1)S(1)}, u32[]{:S(2)}, u32[]{:S(2)}) collective-permute-start(bf16[64,256]{1,0:T(8,128)(2,1)S(1)} %get-tuple-element.43), channel_id=1, source_target_pairs={{0,8},{8,0},{1,9},{9,1},{2,10},{10,2},{3,11},{11,3},{4,12},{12,4},... | collective-permute-start | bytes 98312 | tf_op jit(solution)/shard_map/ppermute | solution.py:85
  229.9 1.4 collective-permute-done.5
  231.3 4.4 %collective-permute-start.6 = (bf16[2,64,256]{2,1,0:T(8,128)(2,1)S(1)}, bf16[2,64,256]{2,1,0:T(8,128)(2,1)S(1)}, u32[]{:S(2)}, u32[]{:S(2)}) collective-permute-start(bf16[2,64,256]{2,1,0:T(8,128)(2,1)S(1)} %get-tuple-element.21), channel_id=1, source_target_pairs={{0,6},{2,0},{4,2},{6,4},{1,7},{3,1},{5,3},{7,5},{8,14},{10,8},{12,... | collective-permute-start | bytes 196616 | tf_op jit(solution)/shard_map/ppermute | solution.py:88
  235.7 1.9 collective-permute-start.7
  237.9 4.4 %collective-permute-done.7 = bf16[2,64,256]{2,1,0:T(8,128)(2,1)S(1)} collective-permute-done((bf16[2,64,256]{2,1,0:T(8,128)(2,1)S(1)}, bf16[2,64,256]{2,1,0:T(8,128)(2,1)S(1)}, u32[]{:S(2)}, u32[]{:S(2)}) %collective-permute-start.7) | collective-permute-done | bytes 65568 | tf_op jit(solution)/shard_map/ppermute | solution.py:85
  242.3 1.9 collective-permute-start.8
  244.3 4.7 %collective-permute-done.8 = bf16[2,64,256]{2,1,0:T(8,128)(2,1)S(1)} collective-permute-done((bf16[2,64,256]{2,1,0:T(8,128)(2,1)S(1)}, bf16[2,64,256]{2,1,0:T(8,128)(2,1)S(1)}, u32[]{:S(2)}, u32[]{:S(2)}) %collective-permute-start.8) | collective-permute-done | bytes 65568 | tf_op jit(solution)/shard_map/ppermute | solution.py:85
  249.0 5.9 %collective-permute-start.9 = (bf16[4,2,64,256]{3,2,1,0:T(8,128)(2,1)S(1)}, bf16[4,2,64,256]{3,2,1,0:T(8,128)(2,1)S(1)}, u32[]{:S(2)}, u32[]{:S(2)}) collective-permute-start(bf16[4,2,64,256]{3,2,1,0:T(8,128)(2,1)S(1)} %constant_dynamic-slice_fusion.4), channel_id=1, source_target_pairs={{0,1},{1,0},{2,3},{3,2},{4,5},{5,4},{6,7},{7,6},{8,9},{9,8},{10,11... | collective-permute-start | bytes 786440 | tf_op jit(solution)/shard_map/ppermute | solution.py:85
  259.4 7.0 %all-gather.8.cloned.1.call-done = bf16[256,8192]{0,1:T(8,128)(2,1)} async-done(((bf16[256,2048]{0,1:T(8,128)(2,1)}), bf16[256,8192]{0,1:T(8,128)(2,1)}) %all-gather.8.cloned.1.call-update) | async-done | bytes 4194320 | tf_op jit(solution)/shard_map/all_gather | solution.py:140
  266.4 3.5 %convolution_convert_fusion = bf16[256,8192]{1,0:T(8,128)(2,1)S(1)} fusion(bf16[256,8192]{0,1:T(8,128)(2,1)} %all-gather.8.cloned.1.call-done, bf16[32,8,2,128]{3,2,1,0:T(2,128)(2,1)S(1)} %bitcast.151), kind=kOutput, calls=%fused_computation.2 | convolution fusion | flops 1075838976 | bytes 8519680 | tf_op jit(solution)/shard_map/dot_general | solution.py:166
  270.5 1.1 copy.78
  271.6 2.6 collective-permute-start.10
  274.3 1.9 collective-permute-start.15
  276.8 1.5 convert_add_fusion.1
  278.4 3.1 collective-permute-start.11
  281.5 4.3 %collective-permute-start.12 = (bf16[2,16,4096]{2,1,0:T(8,128)(2,1)S(1)}, bf16[2,16,4096]{2,1,0:T(8,128)(2,1)S(1)}, u32[]{:S(2)}, u32[]{:S(2)}) collective-permute-start(bf16[2,16,4096]{2,1,0:T(8,128)(2,1)S(1)} %get-tuple-element.28), channel_id=1, source_target_pairs={{0,4},{2,6},{4,0},{6,2},{1,5},{3,7},{5,1},{7,3},{8,12},{10,14},{12... | collective-permute-start | bytes 786440 | tf_op jit(solution)/shard_map/ppermute | solution.py:120
  285.9 3.1 collective-permute-start.13
  289.3 2.2 collective-permute-start.16
  291.5 2.8 collective-permute-start.17
  294.4 3.4 %collective-permute-start.18 = (bf16[2,16,4096]{2,1,0:T(8,128)(2,1)S(1)}, bf16[2,16,4096]{2,1,0:T(8,128)(2,1)S(1)}, u32[]{:S(2)}, u32[]{:S(2)}) collective-permute-start(bf16[2,16,4096]{2,1,0:T(8,128)(2,1)S(1)} %get-tuple-element.32), channel_id=1, source_target_pairs={{0,6},{2,0},{4,2},{6,4},{1,7},{3,1},{5,3},{7,5},{8,14},{10,8},{12,... | collective-permute-start | bytes 786440 | tf_op jit(solution)/shard_map/ppermute | solution.py:120
  298.0 12.5 %collective-permute-start.14 = (bf16[16,4096]{1,0:T(8,128)(2,1)S(1)}, bf16[16,4096]{1,0:T(8,128)(2,1)S(1)}, u32[]{:S(2)}, u32[]{:S(2)}) collective-permute-start(bf16[16,4096]{1,0:T(8,128)(2,1)S(1)} %fusion.27), channel_id=1, source_target_pairs={{0,8},{8,0},{1,9},{9,1},{2,10},{10,2},{3,11},{11,3},{4,12},{12,4},... | collective-permute-start | bytes 393224 | tf_op jit(solution)/shard_map/ppermute | solution.py:121
  310.7 10.0 %collective-permute-start.19 = (bf16[16,4096]{1,0:T(8,128)(2,1)S(1)}, bf16[16,4096]{1,0:T(8,128)(2,1)S(1)}, u32[]{:S(2)}, u32[]{:S(2)}) collective-permute-start(bf16[16,4096]{1,0:T(8,128)(2,1)S(1)} %fusion.28), channel_id=1, source_target_pairs={{0,8},{8,0},{1,9},{9,1},{2,10},{10,2},{3,11},{11,3},{4,12},{12,4},... | collective-permute-start | bytes 393224 | tf_op jit(solution)/shard_map/ppermute | solution.py:121
  320.8 13.6 %collective-permute-done.19 = bf16[16,4096]{1,0:T(8,128)(2,1)S(1)} collective-permute-done((bf16[16,4096]{1,0:T(8,128)(2,1)S(1)}, bf16[16,4096]{1,0:T(8,128)(2,1)S(1)}, u32[]{:S(2)}, u32[]{:S(2)}) %collective-permute-start.19) | collective-permute-done | bytes 131104 | tf_op jit(solution)/shard_map/ppermute | solution.py:121
  (85 shorter events, 13.2 us)
Async XLA Ops:
  6.5 86.4 %all-gather.4.cloned.1.call-start = ((), (), s32[]{:S(2)}) async-start(), calls=%async_computation | async-start | bytes 2949120 | tf_op jit(solution)/shard_map/all_gather | solution.py:133
  13.2 194.3 %all-gather.6.cloned.1.call-start = ((), (), s32[]{:S(2)}) async-start(), calls=%async_computation.1 | async-start | bytes 7864320 | tf_op jit(solution)/shard_map/all_gather | solution.py:138
  98.9 33.0 %collective-permute-start = (bf16[16,8192]{1,0:T(8,128)(2,1)S(1)}, bf16[16,8192]{1,0:T(8,128)(2,1)S(1)}, u32[]{:S(2)}, u32[]{:S(2)}) collective-permute-start(bf16[16,8192]{1,0:T(8,128)(2,1)S(1)} %fusion.8), channel_id=1, source_target_pairs={{0,8},{8,0},{1,9},{9,1},{2,10},{10,2},{3,11},{11,3},{4,12},{12,4},... | collective-permute-start | bytes 786440 | tf_op jit(solution)/shard_map/ppermute | solution.py:85
  133.0 16.1 %collective-permute-start.2 = (bf16[2,16,8192]{2,1,0:T(8,128)(2,1)S(1)}, bf16[2,16,8192]{2,1,0:T(8,128)(2,1)S(1)}, u32[]{:S(2)}, u32[]{:S(2)}) collective-permute-start(bf16[2,16,8192]{2,1,0:T(8,128)(2,1)S(1)} %get-tuple-element.23), channel_id=1, source_target_pairs={{0,2},{2,4},{4,6},{6,0},{1,3},{3,5},{5,7},{7,1},{8,10},{10,12},{12... | collective-permute-start | bytes 1572872 | tf_op jit(solution)/shard_map/ppermute | solution.py:85
  136.1 14.9 %collective-permute-start.1 = (bf16[2,16,8192]{2,1,0:T(8,128)(2,1)S(1)}, bf16[2,16,8192]{2,1,0:T(8,128)(2,1)S(1)}, u32[]{:S(2)}, u32[]{:S(2)}) collective-permute-start(bf16[2,16,8192]{2,1,0:T(8,128)(2,1)S(1)} %get-tuple-element.23), channel_id=1, source_target_pairs={{0,6},{2,0},{4,2},{6,4},{1,7},{3,1},{5,3},{7,5},{8,14},{10,8},{12,... | collective-permute-start | bytes 1572872 | tf_op jit(solution)/shard_map/ppermute | solution.py:88
  139.5 126.9 %all-gather.8.cloned.1.call-start = ((), (), s32[]{:S(2)}) async-start(), calls=%async_computation.2 | async-start | bytes 5242880 | tf_op jit(solution)/shard_map/all_gather | solution.py:140
  149.1 15.3 %collective-permute-start.3 = (bf16[2,16,8192]{2,1,0:T(8,128)(2,1)S(1)}, bf16[2,16,8192]{2,1,0:T(8,128)(2,1)S(1)}, u32[]{:S(2)}, u32[]{:S(2)}) collective-permute-start(bf16[2,16,8192]{2,1,0:T(8,128)(2,1)S(1)} %collective-permute-done.2), channel_id=1, source_target_pairs={{0,2},{2,4},{4,6},{6,0},{1,3},{3,5},{5,7},{7,1},{8,10},{10,12},{12... | collective-permute-start | bytes 1572872 | tf_op jit(solution)/shard_map/ppermute | solution.py:85
  171.1 38.4 %collective-permute-start.4 = (bf16[4,2,16,8192]{3,2,0,1:T(8,128)(2,1)S(1)}, bf16[4,2,16,8192]{3,2,0,1:T(8,128)(2,1)}, u32[]{:S(2)}, u32[]{:S(2)}) collective-permute-start(bf16[4,2,16,8192]{3,2,0,1:T(8,128)(2,1)S(1)} %constant_dynamic-slice_fusion.5), channel_id=1, source_target_pairs={{0,1},{1,0},{2,3},{3,2},{4,5},{5,4},{6,7},{7,6},{8,9},{9,8},{10,11... | collective-permute-start | bytes 6291464 | tf_op jit(solution)/shard_map/ppermute | solution.py:85
  207.6 7.1 %slice-start = ((s8[6291456]{0:T(1024)(128)(4,1)}), s8[4194304]{0:T(1024)(128)(4,1)S(1)}, s32[]{:S(2)}) async-start(s8[6291456]{0:T(1024)(128)(4,1)} %bitcast.141), calls=%async_computation.3 | async-start | bytes 8388608
  209.5 5.2 %slice-start.1 = ((s8[6291456]{0:T(1024)(128)(4,1)}), s8[2097152]{0:T(1024)(128)(4,1)S(1)}, s32[]{:S(2)}) async-start(s8[6291456]{0:T(1024)(128)(4,1)} %bitcast.141), calls=%async_computation.4 | async-start | bytes 4194304
  217.2 14.0 %collective-permute-start.5 = (bf16[64,256]{1,0:T(8,128)(2,1)S(1)}, bf16[64,256]{1,0:T(8,128)(2,1)S(1)}, u32[]{:S(2)}, u32[]{:S(2)}) collective-permute-start(bf16[64,256]{1,0:T(8,128)(2,1)S(1)} %get-tuple-element.43), channel_id=1, source_target_pairs={{0,8},{8,0},{1,9},{9,1},{2,10},{10,2},{3,11},{11,3},{4,12},{12,4},... | collective-permute-start | bytes 98312 | tf_op jit(solution)/shard_map/ppermute | solution.py:85
  231.3 12.9 %collective-permute-start.6 = (bf16[2,64,256]{2,1,0:T(8,128)(2,1)S(1)}, bf16[2,64,256]{2,1,0:T(8,128)(2,1)S(1)}, u32[]{:S(2)}, u32[]{:S(2)}) collective-permute-start(bf16[2,64,256]{2,1,0:T(8,128)(2,1)S(1)} %get-tuple-element.21), channel_id=1, source_target_pairs={{0,6},{2,0},{4,2},{6,4},{1,7},{3,1},{5,3},{7,5},{8,14},{10,8},{12,... | collective-permute-start | bytes 196616 | tf_op jit(solution)/shard_map/ppermute | solution.py:88
  235.7 6.6 %collective-permute-start.7 = (bf16[2,64,256]{2,1,0:T(8,128)(2,1)S(1)}, bf16[2,64,256]{2,1,0:T(8,128)(2,1)S(1)}, u32[]{:S(2)}, u32[]{:S(2)}) collective-permute-start(bf16[2,64,256]{2,1,0:T(8,128)(2,1)S(1)} %get-tuple-element.21), channel_id=1, source_target_pairs={{0,2},{2,4},{4,6},{6,0},{1,3},{3,5},{5,7},{7,1},{8,10},{10,12},{12... | collective-permute-start | bytes 196616 | tf_op jit(solution)/shard_map/ppermute | solution.py:85
  242.3 6.6 %collective-permute-start.8 = (bf16[2,64,256]{2,1,0:T(8,128)(2,1)S(1)}, bf16[2,64,256]{2,1,0:T(8,128)(2,1)S(1)}, u32[]{:S(2)}, u32[]{:S(2)}) collective-permute-start(bf16[2,64,256]{2,1,0:T(8,128)(2,1)S(1)} %collective-permute-done.7), channel_id=1, source_target_pairs={{0,2},{2,4},{4,6},{6,0},{1,3},{3,5},{5,7},{7,1},{8,10},{10,12},{12... | collective-permute-start | bytes 196616 | tf_op jit(solution)/shard_map/ppermute | solution.py:85
  249.0 6.9 %collective-permute-start.9 = (bf16[4,2,64,256]{3,2,1,0:T(8,128)(2,1)S(1)}, bf16[4,2,64,256]{3,2,1,0:T(8,128)(2,1)S(1)}, u32[]{:S(2)}, u32[]{:S(2)}) collective-permute-start(bf16[4,2,64,256]{3,2,1,0:T(8,128)(2,1)S(1)} %constant_dynamic-slice_fusion.4), channel_id=1, source_target_pairs={{0,1},{1,0},{2,3},{3,2},{4,5},{5,4},{6,7},{7,6},{8,9},{9,8},{10,11... | collective-permute-start | bytes 786440 | tf_op jit(solution)/shard_map/ppermute | solution.py:85
  271.6 5.2 %collective-permute-start.10 = (bf16[2,4,16,4096]{3,2,0,1:T(8,128)(2,1)}, bf16[2,4,16,4096]{3,2,0,1:T(8,128)(2,1)}, u32[]{:S(2)}, u32[]{:S(2)}) collective-permute-start(bf16[2,4,16,4096]{3,2,0,1:T(8,128)(2,1)} %bitcast.138), channel_id=1, source_target_pairs={{0,1},{1,0},{2,3},{3,2},{4,5},{5,4},{6,7},{7,6},{8,9},{9,8},{10,11... | collective-permute-start | bytes 3145736 | tf_op jit(solution)/shard_map/ppermute | solution.py:115
  274.3 14.6 %collective-permute-start.15 = (bf16[2,4,16,4096]{3,2,0,1:T(8,128)(2,1)S(1)}, bf16[2,4,16,4096]{3,2,0,1:T(8,128)(2,1)S(1)}, u32[]{:S(2)}, u32[]{:S(2)}) collective-permute-start(bf16[2,4,16,4096]{3,2,0,1:T(8,128)(2,1)S(1)} %bitcast.147), channel_id=1, source_target_pairs={{0,1},{1,0},{2,3},{3,2},{4,5},{5,4},{6,7},{7,6},{8,9},{9,8},{10,11... | collective-permute-start | bytes 3145736 | tf_op jit(solution)/shard_map/ppermute | solution.py:115
  278.4 16.0 %collective-permute-start.11 = (bf16[2,16,4096]{2,1,0:T(8,128)(2,1)S(1)}, bf16[2,16,4096]{2,1,0:T(8,128)(2,1)S(1)}, u32[]{:S(2)}, u32[]{:S(2)}) collective-permute-start(bf16[2,16,4096]{2,1,0:T(8,128)(2,1)S(1)} %get-tuple-element.26), channel_id=1, source_target_pairs={{0,2},{2,4},{4,6},{6,0},{1,3},{3,5},{5,7},{7,1},{8,10},{10,12},{12... | collective-permute-start | bytes 786440 | tf_op jit(solution)/shard_map/ppermute | solution.py:120
  281.5 16.3 %collective-permute-start.12 = (bf16[2,16,4096]{2,1,0:T(8,128)(2,1)S(1)}, bf16[2,16,4096]{2,1,0:T(8,128)(2,1)S(1)}, u32[]{:S(2)}, u32[]{:S(2)}) collective-permute-start(bf16[2,16,4096]{2,1,0:T(8,128)(2,1)S(1)} %get-tuple-element.28), channel_id=1, source_target_pairs={{0,4},{2,6},{4,0},{6,2},{1,5},{3,7},{5,1},{7,3},{8,12},{10,14},{12... | collective-permute-start | bytes 786440 | tf_op jit(solution)/shard_map/ppermute | solution.py:120
  285.9 11.9 %collective-permute-start.13 = (bf16[2,16,4096]{2,1,0:T(8,128)(2,1)S(1)}, bf16[2,16,4096]{2,1,0:T(8,128)(2,1)S(1)}, u32[]{:S(2)}, u32[]{:S(2)}) collective-permute-start(bf16[2,16,4096]{2,1,0:T(8,128)(2,1)S(1)} %get-tuple-element.27), channel_id=1, source_target_pairs={{0,6},{2,0},{4,2},{6,4},{1,7},{3,1},{5,3},{7,5},{8,14},{10,8},{12,... | collective-permute-start | bytes 786440 | tf_op jit(solution)/shard_map/ppermute | solution.py:120
  289.2 45.2 %copy-start = (bf16[16,8192]{1,0:T(8,128)(2,1)S(1)}, bf16[16,8192]{1,0:T(8,128)(2,1)}, u32[]{:S(2)}) copy-start(bf16[16,8192]{1,0:T(8,128)(2,1)} %param.8) | copy-start | bytes 786436
  289.3 21.2 %collective-permute-start.16 = (bf16[2,16,4096]{2,1,0:T(8,128)(2,1)S(1)}, bf16[2,16,4096]{2,1,0:T(8,128)(2,1)S(1)}, u32[]{:S(2)}, u32[]{:S(2)}) collective-permute-start(bf16[2,16,4096]{2,1,0:T(8,128)(2,1)S(1)} %get-tuple-element.31), channel_id=1, source_target_pairs={{0,2},{2,4},{4,6},{6,0},{1,3},{3,5},{5,7},{7,1},{8,10},{10,12},{12... | collective-permute-start | bytes 786440 | tf_op jit(solution)/shard_map/ppermute | solution.py:120
  291.5 19.0 %collective-permute-start.17 = (bf16[2,16,4096]{2,1,0:T(8,128)(2,1)S(1)}, bf16[2,16,4096]{2,1,0:T(8,128)(2,1)S(1)}, u32[]{:S(2)}, u32[]{:S(2)}) collective-permute-start(bf16[2,16,4096]{2,1,0:T(8,128)(2,1)S(1)} %get-tuple-element.33), channel_id=1, source_target_pairs={{0,4},{2,6},{4,0},{6,2},{1,5},{3,7},{5,1},{7,3},{8,12},{10,14},{12... | collective-permute-start | bytes 786440 | tf_op jit(solution)/shard_map/ppermute | solution.py:120
  294.4 16.2 %collective-permute-start.18 = (bf16[2,16,4096]{2,1,0:T(8,128)(2,1)S(1)}, bf16[2,16,4096]{2,1,0:T(8,128)(2,1)S(1)}, u32[]{:S(2)}, u32[]{:S(2)}) collective-permute-start(bf16[2,16,4096]{2,1,0:T(8,128)(2,1)S(1)} %get-tuple-element.32), channel_id=1, source_target_pairs={{0,6},{2,0},{4,2},{6,4},{1,7},{3,1},{5,3},{7,5},{8,14},{10,8},{12,... | collective-permute-start | bytes 786440 | tf_op jit(solution)/shard_map/ppermute | solution.py:120
  298.0 22.8 %collective-permute-start.14 = (bf16[16,4096]{1,0:T(8,128)(2,1)S(1)}, bf16[16,4096]{1,0:T(8,128)(2,1)S(1)}, u32[]{:S(2)}, u32[]{:S(2)}) collective-permute-start(bf16[16,4096]{1,0:T(8,128)(2,1)S(1)} %fusion.27), channel_id=1, source_target_pairs={{0,8},{8,0},{1,9},{9,1},{2,10},{10,2},{3,11},{11,3},{4,12},{12,4},... | collective-permute-start | bytes 393224 | tf_op jit(solution)/shard_map/ppermute | solution.py:121
  310.7 23.7 %collective-permute-start.19 = (bf16[16,4096]{1,0:T(8,128)(2,1)S(1)}, bf16[16,4096]{1,0:T(8,128)(2,1)S(1)}, u32[]{:S(2)}, u32[]{:S(2)}) collective-permute-start(bf16[16,4096]{1,0:T(8,128)(2,1)S(1)} %fusion.28), channel_id=1, source_target_pairs={{0,8},{8,0},{1,9},{9,1},{2,10},{10,2},{3,11},{11,3},{4,12},{12,4},... | collective-permute-start | bytes 393224 | tf_op jit(solution)/shard_map/ppermute | solution.py:121
Sparse Core Ops, SparseCore 0:
  13.3 79.5 all-gather.3
  139.7 67.8 all-gather.5
  209.7 56.6 all-gather.7

commit v10 on v9

--- a/solution.py
+++ b/solution.py
@@ -168,9 +168,9 @@
     ).astype(jnp.bfloat16)
     width = partial_out.shape[1]
     blocks = partial_out.reshape(2, 4, 2, row_count // 16, width)
-    half = width // 2
+    quarter = width // 4
     summed = jnp.concatenate(
-        [group_reduce_scatter(blocks[..., :half]), group_reduce_scatter(blocks[..., half:])], axis=-1
+        [group_reduce_scatter(blocks[..., k * quarter : (k + 1) * quarter]) for k in range(4)], axis=-1
     )
     return (tokens.astype(jnp.float32) + summed).astype(jnp.bfloat16)
 

time: 346 us -> 376 us (1.087)
  starting transfers between devices: 91.9 us -> 121 us
    ppermute x6 -> x12, starting transfers between devices: 19 us -> 37.5 us  [group_reduce_scatter(): lax.ppermute(outgoing, 'y', [(s, (s + shift) % 4) for s in range(4)])]
    ppermute x2 -> x4, starting transfers between devices: 22.6 us -> 28.5 us  [group_reduce_scatter(): lax.ppermute(take(mine, 1 - zh_index, 0).astype(jnp.bfloat16), 'zh', swap)]
    ppermute x2 -> x4, starting transfers between devices: 4.49 us -> 8.95 us  [group_reduce_scatter(): sent = lax.ppermute(take(partial, 1 - c_index, 2), 'c', swap)]
    ppermute x2 -> x4, waiting for transfers between devices: 13.6 us -> 12 us  [group_reduce_scatter(): lax.ppermute(take(mine, 1 - zh_index, 0).astype(jnp.bfloat16), 'zh', swap)]
    unnamed x24 -> x28, local copies, waits for them, and re-layouts: 8.13 us -> 7.9 us
  transfers between devices with their start and end apart: 23 -> 33, of which waited for: 12 -> 11; matrix products, arithmetic and copies ran while one was open for 7% -> 6% of each run, Pallas kernels for 0% -> 0%
where the time goes in v10:
time: 376 us; the launch traced here: 369 us
  waiting for transfers between devices  190 us (51%)
  starting transfers between devices  121 us (32%)
  local copies, waits for them, and re-layouts  22.3 us (6%)
  other arithmetic  15.5 us (4%)
  between operations  14.2 us (4%)
  matrix products  6.37 us (2%)
    all_gather x1, waiting for transfers between devices, body(): along_zl = lax.all_gather(payload, 'zl', axis=0, tiled=True)  79.7 us
    ppermute x8, waiting for transfers between devices, ring_gather(): ahead = lax.ppermute(ahead, axis_name, forward)  59.6 us
    ppermute x8, starting transfers between devices, ring_gather(): ahead = lax.ppermute(ahead, axis_name, forward)  38 us
    ppermute x12, starting transfers between devices, group_reduce_scatter(): lax.ppermute(outgoing, 'y', [(s, (s + shift) % 4) for s in range(4)])  37.5 us
    all_gather x1, waiting for transfers between devices, body(): weights = lax.all_gather(in_part, 'x', axis=0, tiled=True)  31.7 us
    ppermute x4, starting transfers between devices, group_reduce_scatter(): lax.ppermute(take(mine, 1 - zh_index, 0).astype(jnp.bfloat16), 'zh', swap)  28.5 us
    ppermute x4, waiting for transfers between devices, group_reduce_scatter(): lax.ppermute(take(mine, 1 - zh_index, 0).astype(jnp.bfloat16), 'zh', swap)  12 us
    ppermute x4, starting transfers between devices, group_reduce_scatter(): sent = lax.ppermute(take(partial, 1 - c_index, 2), 'c', swap)  8.95 us
  transfers between devices with their start and end apart: 33, of which 11 were waited for; matrix products, arithmetic and copies ran while one was open for 6% of the time, Pallas kernels for 0%

profile of v10, /device:TPU:1, one launch (start us, length us, event | category | flops | bytes accessed | tf_op | source)
XLA Modules:
  0.0 369.5 jit_solution(7019168677101966138)
XLA Ops:
  11.4 1.8 pad_maximum_fusion
  13.3 79.7 %all-gather.4.cloned.1.call-done = bf16[2048,576]{1,0:T(8,128)(2,1)} async-done(((bf16[256,576]{1,0:T(8,128)(2,1)}), bf16[2048,576]{1,0:T(8,128)(2,1)}) %all-gather.4.cloned.1.call-update) | async-done | bytes 2359312 | tf_op jit(solution)/shard_map/all_gather | solution.py:133
  93.0 1.8 slice.62
  96.2 2.8 slice.61
  98.9 6.6 %collective-permute-start = (bf16[16,8192]{1,0:T(8,128)(2,1)S(1)}, bf16[16,8192]{1,0:T(8,128)(2,1)S(1)}, u32[]{:S(2)}, u32[]{:S(2)}) collective-permute-start(bf16[16,8192]{1,0:T(8,128)(2,1)S(1)} %fusion.8), channel_id=1, source_target_pairs={{0,8},{8,0},{1,9},{9,1},{2,10},{10,2},{3,11},{11,3},{4,12},{12,4},... | collective-permute-start | bytes 786440 | tf_op jit(solution)/shard_map/ppermute | solution.py:85
  105.6 26.4 %collective-permute-done = bf16[16,8192]{1,0:T(8,128)(2,1)S(1)} collective-permute-done((bf16[16,8192]{1,0:T(8,128)(2,1)S(1)}, bf16[16,8192]{1,0:T(8,128)(2,1)S(1)}, u32[]{:S(2)}, u32[]{:S(2)}) %collective-permute-start) | collective-permute-done | bytes 262176 | tf_op jit(solution)/shard_map/ppermute | solution.py:85
  133.1 3.1 collective-permute-start.2
  136.2 3.4 collective-permute-start.1
  139.6 9.5 %collective-permute-done.2 = bf16[2,16,8192]{2,1,0:T(8,128)(2,1)S(1)} collective-permute-done((bf16[2,16,8192]{2,1,0:T(8,128)(2,1)S(1)}, bf16[2,16,8192]{2,1,0:T(8,128)(2,1)S(1)}, u32[]{:S(2)}, u32[]{:S(2)}) %collective-permute-start.2) | collective-permute-done | bytes 524320 | tf_op jit(solution)/shard_map/ppermute | solution.py:85
  149.1 1.9 collective-permute-start.3
  151.9 12.5 %collective-permute-done.3 = bf16[2,16,8192]{2,1,0:T(8,128)(2,1)S(1)} collective-permute-done((bf16[2,16,8192]{2,1,0:T(8,128)(2,1)S(1)}, bf16[2,16,8192]{2,1,0:T(8,128)(2,1)S(1)}, u32[]{:S(2)}, u32[]{:S(2)}) %collective-permute-start.3) | collective-permute-done | bytes 524320 | tf_op jit(solution)/shard_map/ppermute | solution.py:85
  169.4 1.7 constant_dynamic-slice_fusion.9
  171.2 4.1 %collective-permute-start.4 = (bf16[4,2,16,8192]{3,2,0,1:T(8,128)(2,1)S(1)}, bf16[4,2,16,8192]{3,2,0,1:T(8,128)(2,1)}, u32[]{:S(2)}, u32[]{:S(2)}) collective-permute-start(bf16[4,2,16,8192]{3,2,0,1:T(8,128)(2,1)S(1)} %constant_dynamic-slice_fusion.9), channel_id=1, source_target_pairs={{0,1},{1,0},{2,3},{3,2},{4,5},{5,4},{6,7},{7,6},{8,9},{9,8},{10,11... | collective-permute-start | bytes 6291464 | tf_op jit(solution)/shard_map/ppermute | solution.py:85
  175.9 31.7 %all-gather.6.cloned.1.call-done = bf16[8192,320]{1,0:T(8,128)(2,1)} async-done(((bf16[2048,320]{1,0:T(8,128)(2,1)}), bf16[8192,320]{1,0:T(8,128)(2,1)}) %all-gather.6.cloned.1.call-update) | async-done | bytes 5242896 | tf_op jit(solution)/shard_map/all_gather | solution.py:138
  207.7 1.9 fusion.65
  209.6 5.0 %fusion.2 = bf16[2,4,2,16,8192]{4,3,0,1,2:T(8,128)(2,1)S(1)} fusion(s32[]{:T(128)S(6)} %select_n.180, bf16[1,4,2,16,8192]{4,3,0,1,2:T(8,128)(2,1)S(1)} %fusion.65, bf16[1,4,2,16,8192]{4,3,0,1,2:T(8,128)(2,1)} %bitcast.14), kind=kLoop, calls=%fused_computation.9 | loop fusion | flops 6291456 | bytes 8388612 | tf_op jit(solution)/shard_map/jit(_roll_dynamic)/concatenate | solution.py:91
  214.6 2.5 fusion.59
  217.1 12.6 %collective-permute-start.5 = (bf16[64,256]{1,0:T(8,128)(2,1)S(1)}, bf16[64,256]{1,0:T(8,128)(2,1)S(1)}, u32[]{:S(2)}, u32[]{:S(2)}) collective-permute-start(bf16[64,256]{1,0:T(8,128)(2,1)S(1)} %get-tuple-element.55), channel_id=1, source_target_pairs={{0,8},{8,0},{1,9},{9,1},{2,10},{10,2},{3,11},{11,3},{4,12},{12,4},... | collective-permute-start | bytes 98312 | tf_op jit(solution)/shard_map/ppermute | solution.py:85
  229.7 1.4 collective-permute-done.5
  231.2 4.4 %collective-permute-start.6 = (bf16[2,64,256]{2,1,0:T(8,128)(2,1)S(1)}, bf16[2,64,256]{2,1,0:T(8,128)(2,1)S(1)}, u32[]{:S(2)}, u32[]{:S(2)}) collective-permute-start(bf16[2,64,256]{2,1,0:T(8,128)(2,1)S(1)} %get-tuple-element.21), channel_id=1, source_target_pairs={{0,6},{2,0},{4,2},{6,4},{1,7},{3,1},{5,3},{7,5},{8,14},{10,8},{12,... | collective-permute-start | bytes 196616 | tf_op jit(solution)/shard_map/ppermute | solution.py:88
  235.6 1.9 collective-permute-start.7
  237.8 4.4 %collective-permute-done.7 = bf16[2,64,256]{2,1,0:T(8,128)(2,1)S(1)} collective-permute-done((bf16[2,64,256]{2,1,0:T(8,128)(2,1)S(1)}, bf16[2,64,256]{2,1,0:T(8,128)(2,1)S(1)}, u32[]{:S(2)}, u32[]{:S(2)}) %collective-permute-start.7) | collective-permute-done | bytes 65568 | tf_op jit(solution)/shard_map/ppermute | solution.py:85
  242.2 1.9 collective-permute-start.8
  244.1 4.7 %collective-permute-done.8 = bf16[2,64,256]{2,1,0:T(8,128)(2,1)S(1)} collective-permute-done((bf16[2,64,256]{2,1,0:T(8,128)(2,1)S(1)}, bf16[2,64,256]{2,1,0:T(8,128)(2,1)S(1)}, u32[]{:S(2)}, u32[]{:S(2)}) %collective-permute-start.8) | collective-permute-done | bytes 65568 | tf_op jit(solution)/shard_map/ppermute | solution.py:85
  248.9 5.9 %collective-permute-start.9 = (bf16[4,2,64,256]{3,2,1,0:T(8,128)(2,1)S(1)}, bf16[4,2,64,256]{3,2,1,0:T(8,128)(2,1)S(1)}, u32[]{:S(2)}, u32[]{:S(2)}) collective-permute-start(bf16[4,2,64,256]{3,2,1,0:T(8,128)(2,1)S(1)} %constant_dynamic-slice_fusion.8), channel_id=1, source_target_pairs={{0,1},{1,0},{2,3},{3,2},{4,5},{5,4},{6,7},{7,6},{8,9},{9,8},{10,11... | collective-permute-start | bytes 786440 | tf_op jit(solution)/shard_map/ppermute | solution.py:85
  259.2 7.2 %all-gather.8.cloned.1.call-done = bf16[256,8192]{0,1:T(8,128)(2,1)} async-done(((bf16[256,2048]{0,1:T(8,128)(2,1)}), bf16[256,8192]{0,1:T(8,128)(2,1)}) %all-gather.8.cloned.1.call-update) | async-done | bytes 4194320 | tf_op jit(solution)/shard_map/all_gather | solution.py:140
  266.5 3.5 convolution_convert_fusion
  272.2 2.6 collective-permute-start.10
  274.8 2.1 collective-permute-start.15
  277.2 2.4 collective-permute-start.20
  279.7 1.9 collective-permute-start.25
  282.8 3.1 collective-permute-start.11
  286.0 4.3 %collective-permute-start.12 = (bf16[2,16,2048]{2,1,0:T(8,128)(2,1)S(1)}, bf16[2,16,2048]{2,1,0:T(8,128)(2,1)S(1)}, u32[]{:S(2)}, u32[]{:S(2)}) collective-permute-start(bf16[2,16,2048]{2,1,0:T(8,128)(2,1)S(1)} %get-tuple-element.30), channel_id=1, source_target_pairs={{0,4},{2,6},{4,0},{6,2},{1,5},{3,7},{5,1},{7,3},{8,12},{10,14},{12... | collective-permute-start | bytes 393224 | tf_op jit(solution)/shard_map/ppermute | solution.py:120
  290.3 3.1 collective-permute-start.13
  293.6 2.2 collective-permute-start.16
  296.0 2.8 collective-permute-start.17
  299.1 3.4 collective-permute-start.18
  302.5 2.5 collective-permute-start.21
  305.0 3.7 %collective-permute-start.22 = (bf16[2,16,2048]{2,1,0:T(8,128)(2,1)S(1)}, bf16[2,16,2048]{2,1,0:T(8,128)(2,1)S(1)}, u32[]{:S(2)}, u32[]{:S(2)}) collective-permute-start(bf16[2,16,2048]{2,1,0:T(8,128)(2,1)S(1)} %get-tuple-element.40), channel_id=1, source_target_pairs={{0,4},{2,6},{4,0},{6,2},{1,5},{3,7},{5,1},{7,3},{8,12},{10,14},{12... | collective-permute-start | bytes 393224 | tf_op jit(solution)/shard_map/ppermute | solution.py:120
  308.8 4.0 %collective-permute-start.23 = (bf16[2,16,2048]{2,1,0:T(8,128)(2,1)S(1)}, bf16[2,16,2048]{2,1,0:T(8,128)(2,1)S(1)}, u32[]{:S(2)}, u32[]{:S(2)}) collective-permute-start(bf16[2,16,2048]{2,1,0:T(8,128)(2,1)S(1)} %get-tuple-element.39), channel_id=1, source_target_pairs={{0,6},{2,0},{4,2},{6,4},{1,7},{3,1},{5,3},{7,5},{8,14},{10,8},{12,... | collective-permute-start | bytes 393224 | tf_op jit(solution)/shard_map/ppermute | solution.py:120
  312.8 1.9 collective-permute-start.26
  314.7 3.1 collective-permute-start.27
  317.9 3.4 collective-permute-start.28
  321.4 12.5 %collective-permute-start.14 = (bf16[16,2048]{1,0:T(8,128)(2,1)S(1)}, bf16[16,2048]{1,0:T(8,128)(2,1)S(1)}, u32[]{:S(2)}, u32[]{:S(2)}) collective-permute-start(bf16[16,2048]{1,0:T(8,128)(2,1)S(1)} %fusion.44), channel_id=1, source_target_pairs={{0,8},{8,0},{1,9},{9,1},{2,10},{10,2},{3,11},{11,3},{4,12},{12,4},... | collective-permute-start | bytes 196616 | tf_op jit(solution)/shard_map/ppermute | solution.py:121
  333.9 1.9 collective-permute-start.19
  336.0 12.1 %collective-permute-start.24 = (bf16[16,2048]{1,0:T(8,128)(2,1)S(1)}, bf16[16,2048]{1,0:T(8,128)(2,1)S(1)}, u32[]{:S(2)}, u32[]{:S(2)}) collective-permute-start(bf16[16,2048]{1,0:T(8,128)(2,1)S(1)} %fusion.46), channel_id=1, source_target_pairs={{0,8},{8,0},{1,9},{9,1},{2,10},{10,2},{3,11},{11,3},{4,12},{12,4},... | collective-permute-start | bytes 196616 | tf_op jit(solution)/shard_map/ppermute | solution.py:121
  348.2 1.9 collective-permute-start.29
  350.2 12.0 %collective-permute-done.29 = bf16[16,2048]{1,0:T(8,128)(2,1)S(1)} collective-permute-done((bf16[16,2048]{1,0:T(8,128)(2,1)S(1)}, bf16[16,2048]{1,0:T(8,128)(2,1)S(1)}, u32[]{:S(2)}, u32[]{:S(2)}) %collective-permute-start.29) | collective-permute-done | bytes 65568 | tf_op jit(solution)/shard_map/ppermute | solution.py:121
  (120 shorter events, 24.1 us)
Async XLA Ops:
  6.5 86.5 %all-gather.4.cloned.1.call-start = ((), (), s32[]{:S(2)}) async-start(), calls=%async_computation | async-start | bytes 2949120 | tf_op jit(solution)/shard_map/all_gather | solution.py:133
  13.2 194.4 %all-gather.6.cloned.1.call-start = ((), (), s32[]{:S(2)}) async-start(), calls=%async_computation.1 | async-start | bytes 7864320 | tf_op jit(solution)/shard_map/all_gather | solution.py:138
  98.9 33.0 %collective-permute-start = (bf16[16,8192]{1,0:T(8,128)(2,1)S(1)}, bf16[16,8192]{1,0:T(8,128)(2,1)S(1)}, u32[]{:S(2)}, u32[]{:S(2)}) collective-permute-start(bf16[16,8192]{1,0:T(8,128)(2,1)S(1)} %fusion.8), channel_id=1, source_target_pairs={{0,8},{8,0},{1,9},{9,1},{2,10},{10,2},{3,11},{11,3},{4,12},{12,4},... | collective-permute-start | bytes 786440 | tf_op jit(solution)/shard_map/ppermute | solution.py:85
  133.1 16.1 %collective-permute-start.2 = (bf16[2,16,8192]{2,1,0:T(8,128)(2,1)S(1)}, bf16[2,16,8192]{2,1,0:T(8,128)(2,1)S(1)}, u32[]{:S(2)}, u32[]{:S(2)}) collective-permute-start(bf16[2,16,8192]{2,1,0:T(8,128)(2,1)S(1)} %get-tuple-element.23), channel_id=1, source_target_pairs={{0,2},{2,4},{4,6},{6,0},{1,3},{3,5},{5,7},{7,1},{8,10},{10,12},{12... | collective-permute-start | bytes 1572872 | tf_op jit(solution)/shard_map/ppermute | solution.py:85
  136.2 14.9 %collective-permute-start.1 = (bf16[2,16,8192]{2,1,0:T(8,128)(2,1)S(1)}, bf16[2,16,8192]{2,1,0:T(8,128)(2,1)S(1)}, u32[]{:S(2)}, u32[]{:S(2)}) collective-permute-start(bf16[2,16,8192]{2,1,0:T(8,128)(2,1)S(1)} %get-tuple-element.23), channel_id=1, source_target_pairs={{0,6},{2,0},{4,2},{6,4},{1,7},{3,1},{5,3},{7,5},{8,14},{10,8},{12,... | collective-permute-start | bytes 1572872 | tf_op jit(solution)/shard_map/ppermute | solution.py:88
  139.6 126.9 %all-gather.8.cloned.1.call-start = ((), (), s32[]{:S(2)}) async-start(), calls=%async_computation.2 | async-start | bytes 5242880 | tf_op jit(solution)/shard_map/all_gather | solution.py:140
  149.1 15.3 %collective-permute-start.3 = (bf16[2,16,8192]{2,1,0:T(8,128)(2,1)S(1)}, bf16[2,16,8192]{2,1,0:T(8,128)(2,1)S(1)}, u32[]{:S(2)}, u32[]{:S(2)}) collective-permute-start(bf16[2,16,8192]{2,1,0:T(8,128)(2,1)S(1)} %collective-permute-done.2), channel_id=1, source_target_pairs={{0,2},{2,4},{4,6},{6,0},{1,3},{3,5},{5,7},{7,1},{8,10},{10,12},{12... | collective-permute-start | bytes 1572872 | tf_op jit(solution)/shard_map/ppermute | solution.py:85
  171.2 38.4 %collective-permute-start.4 = (bf16[4,2,16,8192]{3,2,0,1:T(8,128)(2,1)S(1)}, bf16[4,2,16,8192]{3,2,0,1:T(8,128)(2,1)}, u32[]{:S(2)}, u32[]{:S(2)}) collective-permute-start(bf16[4,2,16,8192]{3,2,0,1:T(8,128)(2,1)S(1)} %constant_dynamic-slice_fusion.9), channel_id=1, source_target_pairs={{0,1},{1,0},{2,3},{3,2},{4,5},{5,4},{6,7},{7,6},{8,9},{9,8},{10,11... | collective-permute-start | bytes 6291464 | tf_op jit(solution)/shard_map/ppermute | solution.py:85
  207.6 6.9 %slice-start = ((s8[6291456]{0:T(1024)(128)(4,1)}), s8[4194304]{0:T(1024)(128)(4,1)S(1)}, s32[]{:S(2)}) async-start(s8[6291456]{0:T(1024)(128)(4,1)} %bitcast.189), calls=%async_computation.3 | async-start | bytes 8388608
  209.6 5.0 %slice-start.1 = ((s8[6291456]{0:T(1024)(128)(4,1)}), s8[2097152]{0:T(1024)(128)(4,1)S(1)}, s32[]{:S(2)}) async-start(s8[6291456]{0:T(1024)(128)(4,1)} %bitcast.189), calls=%async_computation.4 | async-start | bytes 4194304
  217.1 14.0 %collective-permute-start.5 = (bf16[64,256]{1,0:T(8,128)(2,1)S(1)}, bf16[64,256]{1,0:T(8,128)(2,1)S(1)}, u32[]{:S(2)}, u32[]{:S(2)}) collective-permute-start(bf16[64,256]{1,0:T(8,128)(2,1)S(1)} %get-tuple-element.55), channel_id=1, source_target_pairs={{0,8},{8,0},{1,9},{9,1},{2,10},{10,2},{3,11},{11,3},{4,12},{12,4},... | collective-permute-start | bytes 98312 | tf_op jit(solution)/shard_map/ppermute | solution.py:85
  231.2 12.9 %collective-permute-start.6 = (bf16[2,64,256]{2,1,0:T(8,128)(2,1)S(1)}, bf16[2,64,256]{2,1,0:T(8,128)(2,1)S(1)}, u32[]{:S(2)}, u32[]{:S(2)}) collective-permute-start(bf16[2,64,256]{2,1,0:T(8,128)(2,1)S(1)} %get-tuple-element.21), channel_id=1, source_target_pairs={{0,6},{2,0},{4,2},{6,4},{1,7},{3,1},{5,3},{7,5},{8,14},{10,8},{12,... | collective-permute-start | bytes 196616 | tf_op jit(solution)/shard_map/ppermute | solution.py:88
  235.6 6.6 %collective-permute-start.7 = (bf16[2,64,256]{2,1,0:T(8,128)(2,1)S(1)}, bf16[2,64,256]{2,1,0:T(8,128)(2,1)S(1)}, u32[]{:S(2)}, u32[]{:S(2)}) collective-permute-start(bf16[2,64,256]{2,1,0:T(8,128)(2,1)S(1)} %get-tuple-element.21), channel_id=1, source_target_pairs={{0,2},{2,4},{4,6},{6,0},{1,3},{3,5},{5,7},{7,1},{8,10},{10,12},{12... | collective-permute-start | bytes 196616 | tf_op jit(solution)/shard_map/ppermute | solution.py:85
  242.2 6.6 %collective-permute-start.8 = (bf16[2,64,256]{2,1,0:T(8,128)(2,1)S(1)}, bf16[2,64,256]{2,1,0:T(8,128)(2,1)S(1)}, u32[]{:S(2)}, u32[]{:S(2)}) collective-permute-start(bf16[2,64,256]{2,1,0:T(8,128)(2,1)S(1)} %collective-permute-done.7), channel_id=1, source_target_pairs={{0,2},{2,4},{4,6},{6,0},{1,3},{3,5},{5,7},{7,1},{8,10},{10,12},{12... | collective-permute-start | bytes 196616 | tf_op jit(solution)/shard_map/ppermute | solution.py:85
  248.9 6.9 %collective-permute-start.9 = (bf16[4,2,64,256]{3,2,1,0:T(8,128)(2,1)S(1)}, bf16[4,2,64,256]{3,2,1,0:T(8,128)(2,1)S(1)}, u32[]{:S(2)}, u32[]{:S(2)}) collective-permute-start(bf16[4,2,64,256]{3,2,1,0:T(8,128)(2,1)S(1)} %constant_dynamic-slice_fusion.8), channel_id=1, source_target_pairs={{0,1},{1,0},{2,3},{3,2},{4,5},{5,4},{6,7},{7,6},{8,9},{9,8},{10,11... | collective-permute-start | bytes 786440 | tf_op jit(solution)/shard_map/ppermute | solution.py:85
  272.2 9.4 %collective-permute-start.10 = (bf16[2,4,16,2048]{3,2,0,1:T(8,128)(2,1)}, bf16[2,4,16,2048]{3,2,0,1:T(8,128)(2,1)}, u32[]{:S(2)}, u32[]{:S(2)}) collective-permute-start(bf16[2,4,16,2048]{3,2,0,1:T(8,128)(2,1)} %bitcast.186), channel_id=1, source_target_pairs={{0,1},{1,0},{2,3},{3,2},{4,5},{5,4},{6,7},{7,6},{8,9},{9,8},{10,11... | collective-permute-start | bytes 1572872 | tf_op jit(solution)/shard_map/ppermute | solution.py:115
  274.8 6.8 %copy-start.1 = (bf16[2,4,1,16,2048]{4,3,2,1,0:T(8,128)(2,1)S(1)}, bf16[2,4,1,16,2048]{4,3,2,1,0:T(8,128)(2,1)}, u32[]{:S(2)}) copy-start(bf16[2,4,1,16,2048]{4,3,2,1,0:T(8,128)(2,1)} %get-tuple-element.65) | copy-start | bytes 1572868
  274.8 15.5 %collective-permute-start.15 = (bf16[2,4,16,2048]{3,2,0,1:T(8,128)(2,1)S(1)}, bf16[2,4,16,2048]{3,2,0,1:T(8,128)(2,1)S(1)}, u32[]{:S(2)}, u32[]{:S(2)}) collective-permute-start(bf16[2,4,16,2048]{3,2,0,1:T(8,128)(2,1)S(1)} %bitcast.201), channel_id=1, source_target_pairs={{0,1},{1,0},{2,3},{3,2},{4,5},{5,4},{6,7},{7,6},{8,9},{9,8},{10,11... | collective-permute-start | bytes 1572872 | tf_op jit(solution)/shard_map/ppermute | solution.py:115
  277.2 16.4 %collective-permute-start.20 = (bf16[2,4,16,2048]{3,2,0,1:T(8,128)(2,1)S(1)}, bf16[2,4,16,2048]{3,2,0,1:T(8,128)(2,1)S(1)}, u32[]{:S(2)}, u32[]{:S(2)}) collective-permute-start(bf16[2,4,16,2048]{3,2,0,1:T(8,128)(2,1)S(1)} %bitcast.200), channel_id=1, source_target_pairs={{0,1},{1,0},{2,3},{3,2},{4,5},{5,4},{6,7},{7,6},{8,9},{9,8},{10,11... | collective-permute-start | bytes 1572872 | tf_op jit(solution)/shard_map/ppermute | solution.py:115
  279.7 16.4 %collective-permute-start.25 = (bf16[2,4,16,2048]{3,2,0,1:T(8,128)(2,1)S(1)}, bf16[2,4,16,2048]{3,2,0,1:T(8,128)(2,1)S(1)}, u32[]{:S(2)}, u32[]{:S(2)}) collective-permute-start(bf16[2,4,16,2048]{3,2,0,1:T(8,128)(2,1)S(1)} %bitcast.199), channel_id=1, source_target_pairs={{0,1},{1,0},{2,3},{3,2},{4,5},{5,4},{6,7},{7,6},{8,9},{9,8},{10,11... | collective-permute-start | bytes 1572872 | tf_op jit(solution)/shard_map/ppermute | solution.py:115
  282.8 16.2 %collective-permute-start.11 = (bf16[2,16,2048]{2,1,0:T(8,128)(2,1)S(1)}, bf16[2,16,2048]{2,1,0:T(8,128)(2,1)S(1)}, u32[]{:S(2)}, u32[]{:S(2)}) collective-permute-start(bf16[2,16,2048]{2,1,0:T(8,128)(2,1)S(1)} %get-tuple-element.28), channel_id=1, source_target_pairs={{0,2},{2,4},{4,6},{6,0},{1,3},{3,5},{5,7},{7,1},{8,10},{10,12},{12... | collective-permute-start | bytes 393224 | tf_op jit(solution)/shard_map/ppermute | solution.py:120
  286.0 16.5 %collective-permute-start.12 = (bf16[2,16,2048]{2,1,0:T(8,128)(2,1)S(1)}, bf16[2,16,2048]{2,1,0:T(8,128)(2,1)S(1)}, u32[]{:S(2)}, u32[]{:S(2)}) collective-permute-start(bf16[2,16,2048]{2,1,0:T(8,128)(2,1)S(1)} %get-tuple-element.30), channel_id=1, source_target_pairs={{0,4},{2,6},{4,0},{6,2},{1,5},{3,7},{5,1},{7,3},{8,12},{10,14},{12... | collective-permute-start | bytes 393224 | tf_op jit(solution)/shard_map/ppermute | solution.py:120
  290.3 14.6 %collective-permute-start.13 = (bf16[2,16,2048]{2,1,0:T(8,128)(2,1)S(1)}, bf16[2,16,2048]{2,1,0:T(8,128)(2,1)S(1)}, u32[]{:S(2)}, u32[]{:S(2)}) collective-permute-start(bf16[2,16,2048]{2,1,0:T(8,128)(2,1)S(1)} %get-tuple-element.29), channel_id=1, source_target_pairs={{0,6},{2,0},{4,2},{6,4},{1,7},{3,1},{5,3},{7,5},{8,14},{10,8},{12,... | collective-permute-start | bytes 393224 | tf_op jit(solution)/shard_map/ppermute | solution.py:120
  293.6 15.2 %collective-permute-start.16 = (bf16[2,16,2048]{2,1,0:T(8,128)(2,1)S(1)}, bf16[2,16,2048]{2,1,0:T(8,128)(2,1)S(1)}, u32[]{:S(2)}, u32[]{:S(2)}) collective-permute-start(bf16[2,16,2048]{2,1,0:T(8,128)(2,1)S(1)} %get-tuple-element.33), channel_id=1, source_target_pairs={{0,2},{2,4},{4,6},{6,0},{1,3},{3,5},{5,7},{7,1},{8,10},{10,12},{12... | collective-permute-start | bytes 393224 | tf_op jit(solution)/shard_map/ppermute | solution.py:120
  296.0 16.7 %collective-permute-start.17 = (bf16[2,16,2048]{2,1,0:T(8,128)(2,1)S(1)}, bf16[2,16,2048]{2,1,0:T(8,128)(2,1)S(1)}, u32[]{:S(2)}, u32[]{:S(2)}) collective-permute-start(bf16[2,16,2048]{2,1,0:T(8,128)(2,1)S(1)} %get-tuple-element.35), channel_id=1, source_target_pairs={{0,4},{2,6},{4,0},{6,2},{1,5},{3,7},{5,1},{7,3},{8,12},{10,14},{12... | collective-permute-start | bytes 393224 | tf_op jit(solution)/shard_map/ppermute | solution.py:120
  298.8 63.3 %copy-start = (bf16[16,8192]{1,0:T(8,128)(2,1)S(1)}, bf16[16,8192]{1,0:T(8,128)(2,1)}, u32[]{:S(2)}) copy-start(bf16[16,8192]{1,0:T(8,128)(2,1)} %param.8) | copy-start | bytes 786436
  299.1 15.7 %collective-permute-start.18 = (bf16[2,16,2048]{2,1,0:T(8,128)(2,1)S(1)}, bf16[2,16,2048]{2,1,0:T(8,128)(2,1)S(1)}, u32[]{:S(2)}, u32[]{:S(2)}) collective-permute-start(bf16[2,16,2048]{2,1,0:T(8,128)(2,1)S(1)} %get-tuple-element.34), channel_id=1, source_target_pairs={{0,6},{2,0},{4,2},{6,4},{1,7},{3,1},{5,3},{7,5},{8,14},{10,8},{12,... | collective-permute-start | bytes 393224 | tf_op jit(solution)/shard_map/ppermute | solution.py:120
  302.5 15.4 %collective-permute-start.21 = (bf16[2,16,2048]{2,1,0:T(8,128)(2,1)S(1)}, bf16[2,16,2048]{2,1,0:T(8,128)(2,1)S(1)}, u32[]{:S(2)}, u32[]{:S(2)}) collective-permute-start(bf16[2,16,2048]{2,1,0:T(8,128)(2,1)S(1)} %get-tuple-element.38), channel_id=1, source_target_pairs={{0,2},{2,4},{4,6},{6,0},{1,3},{3,5},{5,7},{7,1},{8,10},{10,12},{12... | collective-permute-start | bytes 393224 | tf_op jit(solution)/shard_map/ppermute | solution.py:120
  305.0 16.4 %collective-permute-start.22 = (bf16[2,16,2048]{2,1,0:T(8,128)(2,1)S(1)}, bf16[2,16,2048]{2,1,0:T(8,128)(2,1)S(1)}, u32[]{:S(2)}, u32[]{:S(2)}) collective-permute-start(bf16[2,16,2048]{2,1,0:T(8,128)(2,1)S(1)} %get-tuple-element.40), channel_id=1, source_target_pairs={{0,4},{2,6},{4,0},{6,2},{1,5},{3,7},{5,1},{7,3},{8,12},{10,14},{12... | collective-permute-start | bytes 393224 | tf_op jit(solution)/shard_map/ppermute | solution.py:120
  308.8 25.1 %collective-permute-start.23 = (bf16[2,16,2048]{2,1,0:T(8,128)(2,1)S(1)}, bf16[2,16,2048]{2,1,0:T(8,128)(2,1)S(1)}, u32[]{:S(2)}, u32[]{:S(2)}) collective-permute-start(bf16[2,16,2048]{2,1,0:T(8,128)(2,1)S(1)} %get-tuple-element.39), channel_id=1, source_target_pairs={{0,6},{2,0},{4,2},{6,4},{1,7},{3,1},{5,3},{7,5},{8,14},{10,8},{12,... | collective-permute-start | bytes 393224 | tf_op jit(solution)/shard_map/ppermute | solution.py:120
  312.8 23.2 %collective-permute-start.26 = (bf16[2,16,2048]{2,1,0:T(8,128)(2,1)S(1)}, bf16[2,16,2048]{2,1,0:T(8,128)(2,1)S(1)}, u32[]{:S(2)}, u32[]{:S(2)}) collective-permute-start(bf16[2,16,2048]{2,1,0:T(8,128)(2,1)S(1)} %get-tuple-element.43), channel_id=1, source_target_pairs={{0,2},{2,4},{4,6},{6,0},{1,3},{3,5},{5,7},{7,1},{8,10},{10,12},{12... | collective-permute-start | bytes 393224 | tf_op jit(solution)/shard_map/ppermute | solution.py:120
  314.7 33.3 %collective-permute-start.27 = (bf16[2,16,2048]{2,1,0:T(8,128)(2,1)S(1)}, bf16[2,16,2048]{2,1,0:T(8,128)(2,1)S(1)}, u32[]{:S(2)}, u32[]{:S(2)}) collective-permute-start(bf16[2,16,2048]{2,1,0:T(8,128)(2,1)S(1)} %get-tuple-element.45), channel_id=1, source_target_pairs={{0,4},{2,6},{4,0},{6,2},{1,5},{3,7},{5,1},{7,3},{8,12},{10,14},{12... | collective-permute-start | bytes 393224 | tf_op jit(solution)/shard_map/ppermute | solution.py:120
  317.9 30.1 %collective-permute-start.28 = (bf16[2,16,2048]{2,1,0:T(8,128)(2,1)S(1)}, bf16[2,16,2048]{2,1,0:T(8,128)(2,1)S(1)}, u32[]{:S(2)}, u32[]{:S(2)}) collective-permute-start(bf16[2,16,2048]{2,1,0:T(8,128)(2,1)S(1)} %get-tuple-element.44), channel_id=1, source_target_pairs={{0,6},{2,0},{4,2},{6,4},{1,7},{3,1},{5,3},{7,5},{8,14},{10,8},{12,... | collective-permute-start | bytes 393224 | tf_op jit(solution)/shard_map/ppermute | solution.py:120
  321.4 28.7 %collective-permute-start.14 = (bf16[16,2048]{1,0:T(8,128)(2,1)S(1)}, bf16[16,2048]{1,0:T(8,128)(2,1)S(1)}, u32[]{:S(2)}, u32[]{:S(2)}) collective-permute-start(bf16[16,2048]{1,0:T(8,128)(2,1)S(1)} %fusion.44), channel_id=1, source_target_pairs={{0,8},{8,0},{1,9},{9,1},{2,10},{10,2},{3,11},{11,3},{4,12},{12,4},... | collective-permute-start | bytes 196616 | tf_op jit(solution)/shard_map/ppermute | solution.py:121
  333.9 16.2 %collective-permute-start.19 = (bf16[16,2048]{1,0:T(8,128)(2,1)S(1)}, bf16[16,2048]{1,0:T(8,128)(2,1)S(1)}, u32[]{:S(2)}, u32[]{:S(2)}) collective-permute-start(bf16[16,2048]{1,0:T(8,128)(2,1)S(1)} %fusion.45), channel_id=1, source_target_pairs={{0,8},{8,0},{1,9},{9,1},{2,10},{10,2},{3,11},{11,3},{4,12},{12,4},... | collective-permute-start | bytes 196616 | tf_op jit(solution)/shard_map/ppermute | solution.py:121
  336.0 14.2 %collective-permute-start.24 = (bf16[16,2048]{1,0:T(8,128)(2,1)S(1)}, bf16[16,2048]{1,0:T(8,128)(2,1)S(1)}, u32[]{:S(2)}, u32[]{:S(2)}) collective-permute-start(bf16[16,2048]{1,0:T(8,128)(2,1)S(1)} %fusion.46), channel_id=1, source_target_pairs={{0,8},{8,0},{1,9},{9,1},{2,10},{10,2},{3,11},{11,3},{4,12},{12,4},... | collective-permute-start | bytes 196616 | tf_op jit(solution)/shard_map/ppermute | solution.py:121
  348.2 14.0 %collective-permute-start.29 = (bf16[16,2048]{1,0:T(8,128)(2,1)S(1)}, bf16[16,2048]{1,0:T(8,128)(2,1)S(1)}, u32[]{:S(2)}, u32[]{:S(2)}) collective-permute-start(bf16[16,2048]{1,0:T(8,128)(2,1)S(1)} %fusion.47), channel_id=1, source_target_pairs={{0,8},{8,0},{1,9},{9,1},{2,10},{10,2},{3,11},{11,3},{4,12},{12,4},... | collective-permute-start | bytes 196616 | tf_op jit(solution)/shard_map/ppermute | solution.py:121
Sparse Core Ops, SparseCore 0:
  13.4 79.5 all-gather.3
  139.7 67.8 all-gather.5
  209.7 56.6 all-gather.7

commit v11 on v9

--- a/solution.py
+++ b/solution.py
@@ -91,12 +91,12 @@
     return jnp.roll(stacked, index, axis=0)
 
 
-def group_gather(block):
-    along_zh = ring_gather(block, "zh", 2)
+def group_gather(block, crossed=False):
+    along_zh = block if crossed else ring_gather(block, "zh", 2)
     along_y = ring_gather(along_zh, "y", 4)
     along_c = ring_gather(along_y, "c", 2)
     ordered = jnp.transpose(along_c, (2, 1, 0) + tuple(range(3, along_c.ndim)))
-    return ordered.reshape((-1,) + block.shape[1:])
+    return ordered.reshape((-1,) + along_c.shape[3 + int(crossed):])
 
 
 def dp_gather(block, axis):
@@ -134,11 +134,12 @@
     in_part = along_zl[:, : stacked.shape[1]]
     out_part = along_zl[:, stacked.shape[1] :].reshape((-1,) + w_out.shape)
     out_part = jnp.transpose(out_part, (1, 0, 2)).reshape(w_out.shape[0], -1)
+    normed = ring_gather(normed, "zh", 2)
     in_part, out_part, normed = lax.optimization_barrier((in_part, out_part, normed))
     weights = lax.all_gather(in_part, "x", axis=0, tiled=True)
     weights, out_part = lax.optimization_barrier((weights, out_part))
     out_weights = lax.all_gather(out_part, "x", axis=1, tiled=True)
-    gathered = group_gather(normed)
+    gathered = group_gather(normed, crossed=True)
     row_count = gathered.shape[0]
     projected = jnp.dot(gathered, weights, preferred_element_type=jnp.float32)
     query_part = projected[:, :q_cols]

time: 346 us -> 328 us (0.948)
  waiting for transfers between devices: 192 us -> 163 us
  starting transfers between devices: 91.9 us -> 103 us
    ppermute x8, waiting for transfers between devices: 59.6 us -> 40.4 us  [ring_gather(): ahead = lax.ppermute(ahead, axis_name, forward)]
    all_gather x1, waiting for transfers between devices: 79.7 us -> 68 us  [body(): along_zl = lax.all_gather(payload, 'zl', axis=0, tiled=True)]
    ppermute x8, starting transfers between devices: 38 us -> 47.4 us  [ring_gather(): ahead = lax.ppermute(ahead, axis_name, forward)]
    unnamed x24 -> x25, local copies, waits for them, and re-layouts: 8.13 us -> 8.98 us
  transfers between devices with their start and end apart: 23 -> 23, of which waited for: 12 -> 12; matrix products, arithmetic and copies ran while one was open for 7% -> 8% of each run, Pallas kernels for 0% -> 0%
where the time goes in v11:
time: 328 us; the launch traced here: 323 us
  waiting for transfers between devices  163 us (50%)
  starting transfers between devices  103 us (31%)
  local copies, waits for them, and re-layouts  22.3 us (7%)
  other arithmetic  15 us (5%)
  between operations  13.9 us (4%)
  matrix products  6.38 us (2%)
    all_gather x1, waiting for transfers between devices, body(): along_zl = lax.all_gather(payload, 'zl', axis=0, tiled=True)  68 us
    ppermute x8, starting transfers between devices, ring_gather(): ahead = lax.ppermute(ahead, axis_name, forward)  47.4 us
    ppermute x8, waiting for transfers between devices, ring_gather(): ahead = lax.ppermute(ahead, axis_name, forward)  40.4 us
    all_gather x1, waiting for transfers between devices, body(): weights = lax.all_gather(in_part, 'x', axis=0, tiled=True)  33.3 us
    ppermute x2, starting transfers between devices, group_reduce_scatter(): lax.ppermute(take(mine, 1 - zh_index, 0).astype(jnp.bfloat16), 'zh', swap)  22.6 us
    ppermute x6, starting transfers between devices, group_reduce_scatter(): lax.ppermute(outgoing, 'y', [(s, (s + shift) % 4) for s in range(4)])  19 us
    ppermute x2, waiting for transfers between devices, group_reduce_scatter(): lax.ppermute(take(mine, 1 - zh_index, 0).astype(jnp.bfloat16), 'zh', swap)  13.6 us
    ppermute x2, starting transfers between devices, ring_gather(): behind = lax.ppermute(behind, axis_name, backward)  9.02 us
  transfers between devices with their start and end apart: 23, of which 12 were waited for; matrix products, arithmetic and copies ran while one was open for 8% of the time, Pallas kernels for 0%

profile of v11, /device:TPU:1, one launch (start us, length us, event | category | flops | bytes accessed | tf_op | source)
XLA Modules:
  0.0 323.2 jit_solution(2730249385328685725)
XLA Ops:
  8.2 1.1 fusion.6
  9.4 1.1 fusion.8
  10.4 1.0 pad_maximum_fusion.2
  11.4 1.8 pad_maximum_fusion
  13.3 16.3 %collective-permute-start = (bf16[16,8192]{1,0:T(8,128)(2,1)S(1)}, bf16[16,8192]{1,0:T(8,128)(2,1)S(1)}, u32[]{:S(2)}, u32[]{:S(2)}) collective-permute-start(bf16[16,8192]{1,0:T(8,128)(2,1)S(1)} %fusion.8), channel_id=1, source_target_pairs={{0,8},{8,0},{1,9},{9,1},{2,10},{10,2},{3,11},{11,3},{4,12},{12,4},... | collective-permute-start | bytes 786440 | tf_op jit(solution)/shard_map/ppermute | solution.py:85
  29.6 5.2 %collective-permute-done = bf16[16,8192]{1,0:T(8,128)(2,1)S(1)} collective-permute-done((bf16[16,8192]{1,0:T(8,128)(2,1)S(1)}, bf16[16,8192]{1,0:T(8,128)(2,1)S(1)}, u32[]{:S(2)}, u32[]{:S(2)}) %collective-permute-start) | collective-permute-done | bytes 262176 | tf_op jit(solution)/shard_map/ppermute | solution.py:85
  35.2 68.0 %all-gather.4.cloned.1.call-done = bf16[2048,576]{1,0:T(8,128)(2,1)} async-done(((bf16[256,576]{1,0:T(8,128)(2,1)}), bf16[2048,576]{1,0:T(8,128)(2,1)}) %all-gather.4.cloned.1.call-update) | async-done | bytes 2359312 | tf_op jit(solution)/shard_map/all_gather | solution.py:133
  103.2 1.8 slice.54
  105.1 1.3 copy.32
  106.4 2.7 slice.53
  109.1 4.7 %collective-permute-start.1 = (bf16[2,16,8192]{2,1,0:T(8,128)(2,1)S(1)}, bf16[2,16,8192]{2,1,0:T(8,128)(2,1)S(1)}, u32[]{:S(2)}, u32[]{:S(2)}) collective-permute-start(bf16[2,16,8192]{2,1,0:T(8,128)(2,1)S(1)} %fusion.16), channel_id=1, source_target_pairs={{0,6},{2,0},{4,2},{6,4},{1,7},{3,1},{5,3},{7,5},{8,14},{10,8},{12,... | collective-permute-start | bytes 1572872 | tf_op jit(solution)/shard_map/ppermute | solution.py:88
  113.8 1.9 collective-permute-start.2
  116.6 12.4 %collective-permute-done.2 = bf16[2,16,8192]{2,1,0:T(8,128)(2,1)S(1)} collective-permute-done((bf16[2,16,8192]{2,1,0:T(8,128)(2,1)S(1)}, bf16[2,16,8192]{2,1,0:T(8,128)(2,1)S(1)}, u32[]{:S(2)}, u32[]{:S(2)}) %collective-permute-start.2) | collective-permute-done | bytes 524320 | tf_op jit(solution)/shard_map/ppermute | solution.py:85
  129.0 1.9 collective-permute-start.3
  130.9 0.8 bitcast_dynamic-update-slice_fusion.2
  131.7 11.6 %collective-permute-done.3 = bf16[2,16,8192]{2,1,0:T(8,128)(2,1)S(1)} collective-permute-done((bf16[2,16,8192]{2,1,0:T(8,128)(2,1)S(1)}, bf16[2,16,8192]{2,1,0:T(8,128)(2,1)S(1)}, u32[]{:S(2)}, u32[]{:S(2)}) %collective-permute-start.3) | collective-permute-done | bytes 524320 | tf_op jit(solution)/shard_map/ppermute | solution.py:85
  145.8 0.8 bitcast_dynamic-update-slice_fusion.3
  146.7 0.9 bitcast_dynamic-update-slice_fusion.1
  147.5 0.8 bitcast_dynamic-update-slice_fusion.7
  148.4 1.8 constant_dynamic-slice_fusion.5
  150.1 4.9 %collective-permute-start.4 = (bf16[4,2,16,8192]{3,2,0,1:T(8,128)(2,1)S(1)}, bf16[4,2,16,8192]{3,2,0,1:T(8,128)(2,1)}, u32[]{:S(2)}, u32[]{:S(2)}) collective-permute-start(bf16[4,2,16,8192]{3,2,0,1:T(8,128)(2,1)S(1)} %constant_dynamic-slice_fusion.5), channel_id=1, source_target_pairs={{0,1},{1,0},{2,3},{3,2},{4,5},{5,4},{6,7},{7,6},{8,9},{9,8},{10,11... | collective-permute-start | bytes 6291464 | tf_op jit(solution)/shard_map/ppermute | solution.py:85
  155.7 33.3 %all-gather.6.cloned.1.call-done = bf16[8192,320]{1,0:T(8,128)(2,1)} async-done(((bf16[2048,320]{1,0:T(8,128)(2,1)}), bf16[8192,320]{1,0:T(8,128)(2,1)}) %all-gather.6.cloned.1.call-update) | async-done | bytes 5242896 | tf_op jit(solution)/shard_map/all_gather | solution.py:139
  189.1 1.9 fusion.52
  191.0 5.2 %fusion.2 = bf16[2,4,2,16,8192]{4,3,0,1,2:T(8,128)(2,1)S(1)} fusion(s32[]{:T(128)S(6)} %select_n.152, bf16[1,4,2,16,8192]{4,3,0,1,2:T(8,128)(2,1)S(1)} %fusion.52, bf16[1,4,2,16,8192]{4,3,0,1,2:T(8,128)(2,1)} %bitcast.16), kind=kLoop, calls=%fused_computation.9 | loop fusion | flops 6291456 | bytes 8388612 | tf_op jit(solution)/shard_map/jit(_roll_dynamic)/concatenate | solution.py:91
  196.2 2.5 fusion.46
  198.7 12.6 %collective-permute-start.5 = (bf16[64,256]{1,0:T(8,128)(2,1)S(1)}, bf16[64,256]{1,0:T(8,128)(2,1)S(1)}, u32[]{:S(2)}, u32[]{:S(2)}) collective-permute-start(bf16[64,256]{1,0:T(8,128)(2,1)S(1)} %get-tuple-element.41), channel_id=1, source_target_pairs={{0,8},{8,0},{1,9},{9,1},{2,10},{10,2},{3,11},{11,3},{4,12},{12,4},... | collective-permute-start | bytes 98312 | tf_op jit(solution)/shard_map/ppermute | solution.py:85
  211.3 1.4 collective-permute-done.5
  212.8 4.4 %collective-permute-start.6 = (bf16[2,64,256]{2,1,0:T(8,128)(2,1)S(1)}, bf16[2,64,256]{2,1,0:T(8,128)(2,1)S(1)}, u32[]{:S(2)}, u32[]{:S(2)}) collective-permute-start(bf16[2,64,256]{2,1,0:T(8,128)(2,1)S(1)} %get-tuple-element.21), channel_id=1, source_target_pairs={{0,6},{2,0},{4,2},{6,4},{1,7},{3,1},{5,3},{7,5},{8,14},{10,8},{12,... | collective-permute-start | bytes 196616 | tf_op jit(solution)/shard_map/ppermute | solution.py:88
  217.1 1.9 collective-permute-start.7
  219.4 4.4 %collective-permute-done.7 = bf16[2,64,256]{2,1,0:T(8,128)(2,1)S(1)} collective-permute-done((bf16[2,64,256]{2,1,0:T(8,128)(2,1)S(1)}, bf16[2,64,256]{2,1,0:T(8,128)(2,1)S(1)}, u32[]{:S(2)}, u32[]{:S(2)}) %collective-permute-start.7) | collective-permute-done | bytes 65568 | tf_op jit(solution)/shard_map/ppermute | solution.py:85
  223.8 1.9 collective-permute-start.8
  225.7 4.7 %collective-permute-done.8 = bf16[2,64,256]{2,1,0:T(8,128)(2,1)S(1)} collective-permute-done((bf16[2,64,256]{2,1,0:T(8,128)(2,1)S(1)}, bf16[2,64,256]{2,1,0:T(8,128)(2,1)S(1)}, u32[]{:S(2)}, u32[]{:S(2)}) %collective-permute-start.8) | collective-permute-done | bytes 65568 | tf_op jit(solution)/shard_map/ppermute | solution.py:85
  230.5 5.9 %collective-permute-start.9 = (bf16[4,2,64,256]{3,2,1,0:T(8,128)(2,1)S(1)}, bf16[4,2,64,256]{3,2,1,0:T(8,128)(2,1)S(1)}, u32[]{:S(2)}, u32[]{:S(2)}) collective-permute-start(bf16[4,2,64,256]{3,2,1,0:T(8,128)(2,1)S(1)} %constant_dynamic-slice_fusion.4), channel_id=1, source_target_pairs={{0,1},{1,0},{2,3},{3,2},{4,5},{5,4},{6,7},{7,6},{8,9},{9,8},{10,11... | collective-permute-start | bytes 786440 | tf_op jit(solution)/shard_map/ppermute | solution.py:85
  240.8 7.0 %all-gather.8.cloned.1.call-done = bf16[256,8192]{0,1:T(8,128)(2,1)} async-done(((bf16[256,2048]{0,1:T(8,128)(2,1)}), bf16[256,8192]{0,1:T(8,128)(2,1)}) %all-gather.8.cloned.1.call-update) | async-done | bytes 4194320 | tf_op jit(solution)/shard_map/all_gather | solution.py:141
  247.9 3.5 %convolution_convert_fusion = bf16[256,8192]{1,0:T(8,128)(2,1)S(1)} fusion(bf16[256,8192]{0,1:T(8,128)(2,1)} %all-gather.8.cloned.1.call-done, bf16[32,8,2,128]{3,2,1,0:T(2,128)(2,1)S(1)} %bitcast.154), kind=kOutput, calls=%fused_computation.2 | convolution fusion | flops 1075838976 | bytes 8519680 | tf_op jit(solution)/shard_map/dot_general | solution.py:167
  252.0 1.1 copy.82
  253.1 2.6 collective-permute-start.10
  255.8 1.9 collective-permute-start.15
  258.3 1.5 convert_add_fusion.1
  259.8 3.1 collective-permute-start.11
  263.0 4.3 %collective-permute-start.12 = (bf16[2,16,4096]{2,1,0:T(8,128)(2,1)S(1)}, bf16[2,16,4096]{2,1,0:T(8,128)(2,1)S(1)}, u32[]{:S(2)}, u32[]{:S(2)}) collective-permute-start(bf16[2,16,4096]{2,1,0:T(8,128)(2,1)S(1)} %get-tuple-element.26), channel_id=1, source_target_pairs={{0,4},{2,6},{4,0},{6,2},{1,5},{3,7},{5,1},{7,3},{8,12},{10,14},{12... | collective-permute-start | bytes 786440 | tf_op jit(solution)/shard_map/ppermute | solution.py:120
  267.3 3.1 collective-permute-start.13
  270.8 2.2 collective-permute-start.16
  273.0 2.8 collective-permute-start.17
  275.8 3.4 %collective-permute-start.18 = (bf16[2,16,4096]{2,1,0:T(8,128)(2,1)S(1)}, bf16[2,16,4096]{2,1,0:T(8,128)(2,1)S(1)}, u32[]{:S(2)}, u32[]{:S(2)}) collective-permute-start(bf16[2,16,4096]{2,1,0:T(8,128)(2,1)S(1)} %get-tuple-element.30), channel_id=1, source_target_pairs={{0,6},{2,0},{4,2},{6,4},{1,7},{3,1},{5,3},{7,5},{8,14},{10,8},{12,... | collective-permute-start | bytes 786440 | tf_op jit(solution)/shard_map/ppermute | solution.py:120
  279.4 12.5 %collective-permute-start.14 = (bf16[16,4096]{1,0:T(8,128)(2,1)S(1)}, bf16[16,4096]{1,0:T(8,128)(2,1)S(1)}, u32[]{:S(2)}, u32[]{:S(2)}) collective-permute-start(bf16[16,4096]{1,0:T(8,128)(2,1)S(1)} %fusion.27), channel_id=1, source_target_pairs={{0,8},{8,0},{1,9},{9,1},{2,10},{10,2},{3,11},{11,3},{4,12},{12,4},... | collective-permute-start | bytes 393224 | tf_op jit(solution)/shard_map/ppermute | solution.py:121
  292.1 10.0 %collective-permute-start.19 = (bf16[16,4096]{1,0:T(8,128)(2,1)S(1)}, bf16[16,4096]{1,0:T(8,128)(2,1)S(1)}, u32[]{:S(2)}, u32[]{:S(2)}) collective-permute-start(bf16[16,4096]{1,0:T(8,128)(2,1)S(1)} %fusion.28), channel_id=1, source_target_pairs={{0,8},{8,0},{1,9},{9,1},{2,10},{10,2},{3,11},{11,3},{4,12},{12,4},... | collective-permute-start | bytes 393224 | tf_op jit(solution)/shard_map/ppermute | solution.py:121
  302.2 13.6 %collective-permute-done.19 = bf16[16,4096]{1,0:T(8,128)(2,1)S(1)} collective-permute-done((bf16[16,4096]{1,0:T(8,128)(2,1)S(1)}, bf16[16,4096]{1,0:T(8,128)(2,1)S(1)}, u32[]{:S(2)}, u32[]{:S(2)}) %collective-permute-start.19) | collective-permute-done | bytes 131104 | tf_op jit(solution)/shard_map/ppermute | solution.py:121
  (86 shorter events, 13.6 us)
Async XLA Ops:
  6.5 96.7 %all-gather.4.cloned.1.call-start = ((), (), s32[]{:S(2)}) async-start(), calls=%async_computation | async-start | bytes 2949120 | tf_op jit(solution)/shard_map/all_gather | solution.py:133
  13.2 175.8 %all-gather.6.cloned.1.call-start = ((), (), s32[]{:S(2)}) async-start(), calls=%async_computation.1 | async-start | bytes 7864320 | tf_op jit(solution)/shard_map/all_gather | solution.py:139
  13.3 21.5 %collective-permute-start = (bf16[16,8192]{1,0:T(8,128)(2,1)S(1)}, bf16[16,8192]{1,0:T(8,128)(2,1)S(1)}, u32[]{:S(2)}, u32[]{:S(2)}) collective-permute-start(bf16[16,8192]{1,0:T(8,128)(2,1)S(1)} %fusion.8), channel_id=1, source_target_pairs={{0,8},{8,0},{1,9},{9,1},{2,10},{10,2},{3,11},{11,3},{4,12},{12,4},... | collective-permute-start | bytes 786440 | tf_op jit(solution)/shard_map/ppermute | solution.py:85
  109.1 21.8 %collective-permute-start.1 = (bf16[2,16,8192]{2,1,0:T(8,128)(2,1)S(1)}, bf16[2,16,8192]{2,1,0:T(8,128)(2,1)S(1)}, u32[]{:S(2)}, u32[]{:S(2)}) collective-permute-start(bf16[2,16,8192]{2,1,0:T(8,128)(2,1)S(1)} %fusion.16), channel_id=1, source_target_pairs={{0,6},{2,0},{4,2},{6,4},{1,7},{3,1},{5,3},{7,5},{8,14},{10,8},{12,... | collective-permute-start | bytes 1572872 | tf_op jit(solution)/shard_map/ppermute | solution.py:88
  113.8 15.2 %collective-permute-start.2 = (bf16[2,16,8192]{2,1,0:T(8,128)(2,1)S(1)}, bf16[2,16,8192]{2,1,0:T(8,128)(2,1)S(1)}, u32[]{:S(2)}, u32[]{:S(2)}) collective-permute-start(bf16[2,16,8192]{2,1,0:T(8,128)(2,1)S(1)} %fusion.16), channel_id=1, source_target_pairs={{0,2},{2,4},{4,6},{6,0},{1,3},{3,5},{5,7},{7,1},{8,10},{10,12},{12... | collective-permute-start | bytes 1572872 | tf_op jit(solution)/shard_map/ppermute | solution.py:85
  116.6 131.3 %all-gather.8.cloned.1.call-start = ((), (), s32[]{:S(2)}) async-start(), calls=%async_computation.2 | async-start | bytes 5242880 | tf_op jit(solution)/shard_map/all_gather | solution.py:141
  129.0 14.4 %collective-permute-start.3 = (bf16[2,16,8192]{2,1,0:T(8,128)(2,1)S(1)}, bf16[2,16,8192]{2,1,0:T(8,128)(2,1)S(1)}, u32[]{:S(2)}, u32[]{:S(2)}) collective-permute-start(bf16[2,16,8192]{2,1,0:T(8,128)(2,1)S(1)} %collective-permute-done.2), channel_id=1, source_target_pairs={{0,2},{2,4},{4,6},{6,0},{1,3},{3,5},{5,7},{7,1},{8,10},{10,12},{12... | collective-permute-start | bytes 1572872 | tf_op jit(solution)/shard_map/ppermute | solution.py:85
  150.1 40.8 %collective-permute-start.4 = (bf16[4,2,16,8192]{3,2,0,1:T(8,128)(2,1)S(1)}, bf16[4,2,16,8192]{3,2,0,1:T(8,128)(2,1)}, u32[]{:S(2)}, u32[]{:S(2)}) collective-permute-start(bf16[4,2,16,8192]{3,2,0,1:T(8,128)(2,1)S(1)} %constant_dynamic-slice_fusion.5), channel_id=1, source_target_pairs={{0,1},{1,0},{2,3},{3,2},{4,5},{5,4},{6,7},{7,6},{8,9},{9,8},{10,11... | collective-permute-start | bytes 6291464 | tf_op jit(solution)/shard_map/ppermute | solution.py:85
  189.1 7.1 %slice-start = ((s8[6291456]{0:T(1024)(128)(4,1)}), s8[4194304]{0:T(1024)(128)(4,1)S(1)}, s32[]{:S(2)}) async-start(s8[6291456]{0:T(1024)(128)(4,1)} %bitcast.144), calls=%async_computation.3 | async-start | bytes 8388608
  191.0 5.2 %slice-start.1 = ((s8[6291456]{0:T(1024)(128)(4,1)}), s8[2097152]{0:T(1024)(128)(4,1)S(1)}, s32[]{:S(2)}) async-start(s8[6291456]{0:T(1024)(128)(4,1)} %bitcast.144), calls=%async_computation.4 | async-start | bytes 4194304
  198.7 14.0 %collective-permute-start.5 = (bf16[64,256]{1,0:T(8,128)(2,1)S(1)}, bf16[64,256]{1,0:T(8,128)(2,1)S(1)}, u32[]{:S(2)}, u32[]{:S(2)}) collective-permute-start(bf16[64,256]{1,0:T(8,128)(2,1)S(1)} %get-tuple-element.41), channel_id=1, source_target_pairs={{0,8},{8,0},{1,9},{9,1},{2,10},{10,2},{3,11},{11,3},{4,12},{12,4},... | collective-permute-start | bytes 98312 | tf_op jit(solution)/shard_map/ppermute | solution.py:85
  212.8 12.9 %collective-permute-start.6 = (bf16[2,64,256]{2,1,0:T(8,128)(2,1)S(1)}, bf16[2,64,256]{2,1,0:T(8,128)(2,1)S(1)}, u32[]{:S(2)}, u32[]{:S(2)}) collective-permute-start(bf16[2,64,256]{2,1,0:T(8,128)(2,1)S(1)} %get-tuple-element.21), channel_id=1, source_target_pairs={{0,6},{2,0},{4,2},{6,4},{1,7},{3,1},{5,3},{7,5},{8,14},{10,8},{12,... | collective-permute-start | bytes 196616 | tf_op jit(solution)/shard_map/ppermute | solution.py:88
  217.1 6.6 %collective-permute-start.7 = (bf16[2,64,256]{2,1,0:T(8,128)(2,1)S(1)}, bf16[2,64,256]{2,1,0:T(8,128)(2,1)S(1)}, u32[]{:S(2)}, u32[]{:S(2)}) collective-permute-start(bf16[2,64,256]{2,1,0:T(8,128)(2,1)S(1)} %get-tuple-element.21), channel_id=1, source_target_pairs={{0,2},{2,4},{4,6},{6,0},{1,3},{3,5},{5,7},{7,1},{8,10},{10,12},{12... | collective-permute-start | bytes 196616 | tf_op jit(solution)/shard_map/ppermute | solution.py:85
  223.8 6.6 %collective-permute-start.8 = (bf16[2,64,256]{2,1,0:T(8,128)(2,1)S(1)}, bf16[2,64,256]{2,1,0:T(8,128)(2,1)S(1)}, u32[]{:S(2)}, u32[]{:S(2)}) collective-permute-start(bf16[2,64,256]{2,1,0:T(8,128)(2,1)S(1)} %collective-permute-done.7), channel_id=1, source_target_pairs={{0,2},{2,4},{4,6},{6,0},{1,3},{3,5},{5,7},{7,1},{8,10},{10,12},{12... | collective-permute-start | bytes 196616 | tf_op jit(solution)/shard_map/ppermute | solution.py:85
  230.5 6.9 %collective-permute-start.9 = (bf16[4,2,64,256]{3,2,1,0:T(8,128)(2,1)S(1)}, bf16[4,2,64,256]{3,2,1,0:T(8,128)(2,1)S(1)}, u32[]{:S(2)}, u32[]{:S(2)}) collective-permute-start(bf16[4,2,64,256]{3,2,1,0:T(8,128)(2,1)S(1)} %constant_dynamic-slice_fusion.4), channel_id=1, source_target_pairs={{0,1},{1,0},{2,3},{3,2},{4,5},{5,4},{6,7},{7,6},{8,9},{9,8},{10,11... | collective-permute-start | bytes 786440 | tf_op jit(solution)/shard_map/ppermute | solution.py:85
  253.1 5.2 %collective-permute-start.10 = (bf16[2,4,16,4096]{3,2,0,1:T(8,128)(2,1)}, bf16[2,4,16,4096]{3,2,0,1:T(8,128)(2,1)}, u32[]{:S(2)}, u32[]{:S(2)}) collective-permute-start(bf16[2,4,16,4096]{3,2,0,1:T(8,128)(2,1)} %bitcast.141), channel_id=1, source_target_pairs={{0,1},{1,0},{2,3},{3,2},{4,5},{5,4},{6,7},{7,6},{8,9},{9,8},{10,11... | collective-permute-start | bytes 3145736 | tf_op jit(solution)/shard_map/ppermute | solution.py:115
  255.8 14.6 %collective-permute-start.15 = (bf16[2,4,16,4096]{3,2,0,1:T(8,128)(2,1)S(1)}, bf16[2,4,16,4096]{3,2,0,1:T(8,128)(2,1)S(1)}, u32[]{:S(2)}, u32[]{:S(2)}) collective-permute-start(bf16[2,4,16,4096]{3,2,0,1:T(8,128)(2,1)S(1)} %bitcast.150), channel_id=1, source_target_pairs={{0,1},{1,0},{2,3},{3,2},{4,5},{5,4},{6,7},{7,6},{8,9},{9,8},{10,11... | collective-permute-start | bytes 3145736 | tf_op jit(solution)/shard_map/ppermute | solution.py:115
  259.8 16.0 %collective-permute-start.11 = (bf16[2,16,4096]{2,1,0:T(8,128)(2,1)S(1)}, bf16[2,16,4096]{2,1,0:T(8,128)(2,1)S(1)}, u32[]{:S(2)}, u32[]{:S(2)}) collective-permute-start(bf16[2,16,4096]{2,1,0:T(8,128)(2,1)S(1)} %get-tuple-element.24), channel_id=1, source_target_pairs={{0,2},{2,4},{4,6},{6,0},{1,3},{3,5},{5,7},{7,1},{8,10},{10,12},{12... | collective-permute-start | bytes 786440 | tf_op jit(solution)/shard_map/ppermute | solution.py:120
  263.0 16.3 %collective-permute-start.12 = (bf16[2,16,4096]{2,1,0:T(8,128)(2,1)S(1)}, bf16[2,16,4096]{2,1,0:T(8,128)(2,1)S(1)}, u32[]{:S(2)}, u32[]{:S(2)}) collective-permute-start(bf16[2,16,4096]{2,1,0:T(8,128)(2,1)S(1)} %get-tuple-element.26), channel_id=1, source_target_pairs={{0,4},{2,6},{4,0},{6,2},{1,5},{3,7},{5,1},{7,3},{8,12},{10,14},{12... | collective-permute-start | bytes 786440 | tf_op jit(solution)/shard_map/ppermute | solution.py:120
  267.3 11.9 %collective-permute-start.13 = (bf16[2,16,4096]{2,1,0:T(8,128)(2,1)S(1)}, bf16[2,16,4096]{2,1,0:T(8,128)(2,1)S(1)}, u32[]{:S(2)}, u32[]{:S(2)}) collective-permute-start(bf16[2,16,4096]{2,1,0:T(8,128)(2,1)S(1)} %get-tuple-element.25), channel_id=1, source_target_pairs={{0,6},{2,0},{4,2},{6,4},{1,7},{3,1},{5,3},{7,5},{8,14},{10,8},{12,... | collective-permute-start | bytes 786440 | tf_op jit(solution)/shard_map/ppermute | solution.py:120
  270.7 45.3 %copy-start = (bf16[16,8192]{1,0:T(8,128)(2,1)S(1)}, bf16[16,8192]{1,0:T(8,128)(2,1)}, u32[]{:S(2)}) copy-start(bf16[16,8192]{1,0:T(8,128)(2,1)} %param.8) | copy-start | bytes 786436
  270.8 21.2 %collective-permute-start.16 = (bf16[2,16,4096]{2,1,0:T(8,128)(2,1)S(1)}, bf16[2,16,4096]{2,1,0:T(8,128)(2,1)S(1)}, u32[]{:S(2)}, u32[]{:S(2)}) collective-permute-start(bf16[2,16,4096]{2,1,0:T(8,128)(2,1)S(1)} %get-tuple-element.29), channel_id=1, source_target_pairs={{0,2},{2,4},{4,6},{6,0},{1,3},{3,5},{5,7},{7,1},{8,10},{10,12},{12... | collective-permute-start | bytes 786440 | tf_op jit(solution)/shard_map/ppermute | solution.py:120
  273.0 19.0 %collective-permute-start.17 = (bf16[2,16,4096]{2,1,0:T(8,128)(2,1)S(1)}, bf16[2,16,4096]{2,1,0:T(8,128)(2,1)S(1)}, u32[]{:S(2)}, u32[]{:S(2)}) collective-permute-start(bf16[2,16,4096]{2,1,0:T(8,128)(2,1)S(1)} %get-tuple-element.31), channel_id=1, source_target_pairs={{0,4},{2,6},{4,0},{6,2},{1,5},{3,7},{5,1},{7,3},{8,12},{10,14},{12... | collective-permute-start | bytes 786440 | tf_op jit(solution)/shard_map/ppermute | solution.py:120
  275.8 16.2 %collective-permute-start.18 = (bf16[2,16,4096]{2,1,0:T(8,128)(2,1)S(1)}, bf16[2,16,4096]{2,1,0:T(8,128)(2,1)S(1)}, u32[]{:S(2)}, u32[]{:S(2)}) collective-permute-start(bf16[2,16,4096]{2,1,0:T(8,128)(2,1)S(1)} %get-tuple-element.30), channel_id=1, source_target_pairs={{0,6},{2,0},{4,2},{6,4},{1,7},{3,1},{5,3},{7,5},{8,14},{10,8},{12,... | collective-permute-start | bytes 786440 | tf_op jit(solution)/shard_map/ppermute | solution.py:120
  279.4 22.8 %collective-permute-start.14 = (bf16[16,4096]{1,0:T(8,128)(2,1)S(1)}, bf16[16,4096]{1,0:T(8,128)(2,1)S(1)}, u32[]{:S(2)}, u32[]{:S(2)}) collective-permute-start(bf16[16,4096]{1,0:T(8,128)(2,1)S(1)} %fusion.27), channel_id=1, source_target_pairs={{0,8},{8,0},{1,9},{9,1},{2,10},{10,2},{3,11},{11,3},{4,12},{12,4},... | collective-permute-start | bytes 393224 | tf_op jit(solution)/shard_map/ppermute | solution.py:121
  292.1 23.7 %collective-permute-start.19 = (bf16[16,4096]{1,0:T(8,128)(2,1)S(1)}, bf16[16,4096]{1,0:T(8,128)(2,1)S(1)}, u32[]{:S(2)}, u32[]{:S(2)}) collective-permute-start(bf16[16,4096]{1,0:T(8,128)(2,1)S(1)} %fusion.28), channel_id=1, source_target_pairs={{0,8},{8,0},{1,9},{9,1},{2,10},{10,2},{3,11},{11,3},{4,12},{12,4},... | collective-permute-start | bytes 393224 | tf_op jit(solution)/shard_map/ppermute | solution.py:121
Sparse Core Ops, SparseCore 0:
  13.3 89.8 all-gather.3
  116.7 72.3 all-gather.5
  191.1 56.6 all-gather.7

commit v12 on v11

--- a/solution.py
+++ b/solution.py
@@ -141,9 +141,9 @@
     out_weights = lax.all_gather(out_part, "x", axis=1, tiled=True)
     gathered = group_gather(normed, crossed=True)
     row_count = gathered.shape[0]
-    projected = jnp.dot(gathered, weights, preferred_element_type=jnp.float32)
-    query_part = projected[:, :q_cols]
-    kv_part = projected[:, q_cols:].astype(jnp.bfloat16)
+    kv_part = jnp.dot(gathered, weights[:, q_cols:], preferred_element_type=jnp.float32).astype(jnp.bfloat16)
+    kv_part, gathered = lax.optimization_barrier((kv_part, gathered))
+    query_part = jnp.dot(gathered, weights[:, :q_cols], preferred_element_type=jnp.float32)
     kv_all = group_gather(kv_part.T)
     kv_all = kv_all.reshape(-1, 2, k_cols, row_count)
     key_whole = jnp.transpose(kv_all[:, 0], (2, 0, 1)).reshape(row_count, -1).astype(jnp.float32)

time: 328 us -> 328 us (level)
  transfers between devices with their start and end apart: 23 -> 23, of which waited for: 12 -> 11; matrix products, arithmetic and copies ran while one was open for 8% -> 8% of each run, Pallas kernels for 0% -> 0%
where the time goes in v12:
time: 328 us; the launch traced here: 323 us
  waiting for transfers between devices  163 us (50%)
  starting transfers between devices  102 us (31%)
  local copies, waits for them, and re-layouts  22.3 us (7%)
  other arithmetic  15.1 us (5%)
  between operations  13.9 us (4%)
  matrix products  7.16 us (2%)
    all_gather x1, waiting for transfers between devices, body(): along_zl = lax.all_gather(payload, 'zl', axis=0, tiled=True)  68 us
    ppermute x8, starting transfers between devices, ring_gather(): ahead = lax.ppermute(ahead, axis_name, forward)  47 us
    ppermute x8, waiting for transfers between devices, ring_gather(): ahead = lax.ppermute(ahead, axis_name, forward)  39 us
    all_gather x1, waiting for transfers between devices, body(): weights = lax.all_gather(in_part, 'x', axis=0, tiled=True)  33.4 us
    ppermute x2, starting transfers between devices, group_reduce_scatter(): lax.ppermute(take(mine, 1 - zh_index, 0).astype(jnp.bfloat16), 'zh', swap)  22.6 us
    ppermute x6, starting transfers between devices, group_reduce_scatter(): lax.ppermute(outgoing, 'y', [(s, (s + shift) % 4) for s in range(4)])  19 us
    ppermute x2, waiting for transfers between devices, group_reduce_scatter(): lax.ppermute(take(mine, 1 - zh_index, 0).astype(jnp.bfloat16), 'zh', swap)  13.6 us
    ppermute x2, starting transfers between devices, ring_gather(): behind = lax.ppermute(behind, axis_name, backward)  9.02 us
  transfers between devices with their start and end apart: 23, of which 11 were waited for; matrix products, arithmetic and copies ran while one was open for 8% of the time, Pallas kernels for 0%

profile of v12, /device:TPU:1, one launch (start us, length us, event | category | flops | bytes accessed | tf_op | source)
XLA Modules:
  0.0 323.2 jit_solution(256429145622917236)
XLA Ops:
  7.4 0.8 copy.31
  8.2 1.1 fusion.13
  9.4 1.1 fusion.15
  10.4 1.0 pad_maximum_fusion.2
  11.4 1.8 pad_maximum_fusion
  13.3 16.3 %collective-permute-start = (bf16[16,8192]{1,0:T(8,128)(2,1)S(1)}, bf16[16,8192]{1,0:T(8,128)(2,1)S(1)}, u32[]{:S(2)}, u32[]{:S(2)}) collective-permute-start(bf16[16,8192]{1,0:T(8,128)(2,1)S(1)} %fusion.15), channel_id=1, source_target_pairs={{0,8},{8,0},{1,9},{9,1},{2,10},{10,2},{3,11},{11,3},{4,12},{12,4},... | collective-permute-start | bytes 786440 | tf_op jit(solution)/shard_map/ppermute | solution.py:85
  29.6 5.2 %collective-permute-done = bf16[16,8192]{1,0:T(8,128)(2,1)S(1)} collective-permute-done((bf16[16,8192]{1,0:T(8,128)(2,1)S(1)}, bf16[16,8192]{1,0:T(8,128)(2,1)S(1)}, u32[]{:S(2)}, u32[]{:S(2)}) %collective-permute-start) | collective-permute-done | bytes 262176 | tf_op jit(solution)/shard_map/ppermute | solution.py:85
  35.2 68.0 %all-gather.4.cloned.1.call-done = bf16[2048,576]{1,0:T(8,128)(2,1)} async-done(((bf16[256,576]{1,0:T(8,128)(2,1)}), bf16[2048,576]{1,0:T(8,128)(2,1)}) %all-gather.4.cloned.1.call-update) | async-done | bytes 2359312 | tf_op jit(solution)/shard_map/all_gather | solution.py:133
  103.2 1.8 slice.53
  105.1 1.3 copy.32
  106.4 2.7 slice.52
  109.1 4.7 %collective-permute-start.1 = (bf16[2,16,8192]{2,1,0:T(8,128)(2,1)S(1)}, bf16[2,16,8192]{2,1,0:T(8,128)(2,1)S(1)}, u32[]{:S(2)}, u32[]{:S(2)}) collective-permute-start(bf16[2,16,8192]{2,1,0:T(8,128)(2,1)S(1)} %fusion.23), channel_id=1, source_target_pairs={{0,6},{2,0},{4,2},{6,4},{1,7},{3,1},{5,3},{7,5},{8,14},{10,8},{12,... | collective-permute-start | bytes 1572872 | tf_op jit(solution)/shard_map/ppermute | solution.py:88
  113.8 1.9 collective-permute-start.2
  115.7 0.8 bitcast_dynamic-update-slice_fusion.4
  116.6 12.3 %collective-permute-done.2 = bf16[2,16,8192]{2,1,0:T(8,128)(2,1)S(1)} collective-permute-done((bf16[2,16,8192]{2,1,0:T(8,128)(2,1)S(1)}, bf16[2,16,8192]{2,1,0:T(8,128)(2,1)S(1)}, u32[]{:S(2)}, u32[]{:S(2)}) %collective-permute-start.2) | collective-permute-done | bytes 524320 | tf_op jit(solution)/shard_map/ppermute | solution.py:85
  129.0 1.9 collective-permute-start.3
  130.9 0.8 bitcast_dynamic-update-slice_fusion.2
  131.7 11.6 %collective-permute-done.3 = bf16[2,16,8192]{2,1,0:T(8,128)(2,1)S(1)} collective-permute-done((bf16[2,16,8192]{2,1,0:T(8,128)(2,1)S(1)}, bf16[2,16,8192]{2,1,0:T(8,128)(2,1)S(1)}, u32[]{:S(2)}, u32[]{:S(2)}) %collective-permute-start.3) | collective-permute-done | bytes 524320 | tf_op jit(solution)/shard_map/ppermute | solution.py:85
  146.6 0.9 bitcast_dynamic-update-slice_fusion.1
  148.3 1.8 constant_dynamic-slice_fusion.5
  150.1 4.9 %collective-permute-start.4 = (bf16[4,2,16,8192]{3,2,0,1:T(8,128)(2,1)S(1)}, bf16[4,2,16,8192]{3,2,0,1:T(8,128)(2,1)}, u32[]{:S(2)}, u32[]{:S(2)}) collective-permute-start(bf16[4,2,16,8192]{3,2,0,1:T(8,128)(2,1)S(1)} %constant_dynamic-slice_fusion.5), channel_id=1, source_target_pairs={{0,1},{1,0},{2,3},{3,2},{4,5},{5,4},{6,7},{7,6},{8,9},{9,8},{10,11... | collective-permute-start | bytes 6291464 | tf_op jit(solution)/shard_map/ppermute | solution.py:85
  155.7 33.4 %all-gather.6.cloned.1.call-done = bf16[8192,320]{1,0:T(8,128)(2,1)} async-done(((bf16[2048,320]{1,0:T(8,128)(2,1)}), bf16[8192,320]{1,0:T(8,128)(2,1)}) %all-gather.6.cloned.1.call-update) | async-done | bytes 5242896 | tf_op jit(solution)/shard_map/all_gather | solution.py:139
  189.1 1.9 fusion.56
  191.0 5.2 %fusion.2 = bf16[2,4,2,16,8192]{4,3,0,1,2:T(8,128)(2,1)S(1)} fusion(s32[]{:T(128)S(6)} %select_n.152, bf16[1,4,2,16,8192]{4,3,0,1,2:T(8,128)(2,1)S(1)} %fusion.56, bf16[1,4,2,16,8192]{4,3,0,1,2:T(8,128)(2,1)} %bitcast.16), kind=kLoop, calls=%fused_computation.9 | loop fusion | flops 6291456 | bytes 8388612 | tf_op jit(solution)/shard_map/jit(_roll_dynamic)/concatenate | solution.py:91
  196.3 1.4 fusion.10
  197.7 12.6 %collective-permute-start.5 = (bf16[64,256]{1,0:T(8,128)(2,1)S(1)}, bf16[64,256]{1,0:T(8,128)(2,1)S(1)}, u32[]{:S(2)}, u32[]{:S(2)}) collective-permute-start(bf16[64,256]{1,0:T(8,128)(2,1)S(1)} %bitcast.156), channel_id=1, source_target_pairs={{0,8},{8,0},{1,9},{9,1},{2,10},{10,2},{3,11},{11,3},{4,12},{12,4},... | collective-permute-start | bytes 98312 | tf_op jit(solution)/shard_map/ppermute | solution.py:85
  210.2 1.8 fusion.3
  212.2 4.4 %collective-permute-start.6 = (bf16[2,64,256]{2,1,0:T(8,128)(2,1)S(1)}, bf16[2,64,256]{2,1,0:T(8,128)(2,1)S(1)}, u32[]{:S(2)}, u32[]{:S(2)}) collective-permute-start(bf16[2,64,256]{2,1,0:T(8,128)(2,1)S(1)} %get-tuple-element.25), channel_id=1, source_target_pairs={{0,6},{2,0},{4,2},{6,4},{1,7},{3,1},{5,3},{7,5},{8,14},{10,8},{12,... | collective-permute-start | bytes 196616 | tf_op jit(solution)/shard_map/ppermute | solution.py:88
  216.5 1.9 collective-permute-start.7
  218.8 4.4 %collective-permute-done.7 = bf16[2,64,256]{2,1,0:T(8,128)(2,1)S(1)} collective-permute-done((bf16[2,64,256]{2,1,0:T(8,128)(2,1)S(1)}, bf16[2,64,256]{2,1,0:T(8,128)(2,1)S(1)}, u32[]{:S(2)}, u32[]{:S(2)}) %collective-permute-start.7) | collective-permute-done | bytes 65568 | tf_op jit(solution)/shard_map/ppermute | solution.py:85
  223.2 1.9 collective-permute-start.8
  225.1 4.7 %collective-permute-done.8 = bf16[2,64,256]{2,1,0:T(8,128)(2,1)S(1)} collective-permute-done((bf16[2,64,256]{2,1,0:T(8,128)(2,1)S(1)}, bf16[2,64,256]{2,1,0:T(8,128)(2,1)S(1)}, u32[]{:S(2)}, u32[]{:S(2)}) %collective-permute-start.8) | collective-permute-done | bytes 65568 | tf_op jit(solution)/shard_map/ppermute | solution.py:85
  229.9 5.5 %collective-permute-start.9 = (bf16[4,2,64,256]{3,2,1,0:T(8,128)(2,1)S(1)}, bf16[4,2,64,256]{3,2,1,0:T(8,128)(2,1)S(1)}, u32[]{:S(2)}, u32[]{:S(2)}) collective-permute-start(bf16[4,2,64,256]{3,2,1,0:T(8,128)(2,1)S(1)} %constant_dynamic-slice_fusion.4), channel_id=1, source_target_pairs={{0,1},{1,0},{2,3},{3,2},{4,5},{5,4},{6,7},{7,6},{8,9},{9,8},{10,11... | collective-permute-start | bytes 786440 | tf_op jit(solution)/shard_map/ppermute | solution.py:85
  239.8 8.1 %all-gather.8.cloned.1.call-done = bf16[256,8192]{0,1:T(8,128)(2,1)} async-done(((bf16[256,2048]{0,1:T(8,128)(2,1)}), bf16[256,8192]{0,1:T(8,128)(2,1)}) %all-gather.8.cloned.1.call-update) | async-done | bytes 4194320 | tf_op jit(solution)/shard_map/all_gather | solution.py:141
  247.9 3.5 %convolution_convert_fusion = bf16[256,8192]{1,0:T(8,128)(2,1)S(1)} fusion(bf16[256,8192]{0,1:T(8,128)(2,1)} %all-gather.8.cloned.1.call-done, bf16[32,8,2,128]{3,2,1,0:T(2,128)(2,1)S(1)} %bitcast.152), kind=kOutput, calls=%fused_computation.2 | convolution fusion | flops 1075838976 | bytes 8519680 | tf_op jit(solution)/shard_map/dot_general | solution.py:167
  252.0 1.1 copy.82
  253.1 2.6 collective-permute-start.10
  255.8 1.9 collective-permute-start.15
  258.3 1.5 convert_add_fusion.1
  259.9 3.1 collective-permute-start.11
  263.0 4.3 %collective-permute-start.12 = (bf16[2,16,4096]{2,1,0:T(8,128)(2,1)S(1)}, bf16[2,16,4096]{2,1,0:T(8,128)(2,1)S(1)}, u32[]{:S(2)}, u32[]{:S(2)}) collective-permute-start(bf16[2,16,4096]{2,1,0:T(8,128)(2,1)S(1)} %get-tuple-element.30), channel_id=1, source_target_pairs={{0,4},{2,6},{4,0},{6,2},{1,5},{3,7},{5,1},{7,3},{8,12},{10,14},{12... | collective-permute-start | bytes 786440 | tf_op jit(solution)/shard_map/ppermute | solution.py:120
  267.3 3.1 collective-permute-start.13
  270.8 2.2 collective-permute-start.16
  273.0 2.8 collective-permute-start.17
  275.8 3.4 %collective-permute-start.18 = (bf16[2,16,4096]{2,1,0:T(8,128)(2,1)S(1)}, bf16[2,16,4096]{2,1,0:T(8,128)(2,1)S(1)}, u32[]{:S(2)}, u32[]{:S(2)}) collective-permute-start(bf16[2,16,4096]{2,1,0:T(8,128)(2,1)S(1)} %get-tuple-element.34), channel_id=1, source_target_pairs={{0,6},{2,0},{4,2},{6,4},{1,7},{3,1},{5,3},{7,5},{8,14},{10,8},{12,... | collective-permute-start | bytes 786440 | tf_op jit(solution)/shard_map/ppermute | solution.py:120
  279.4 12.5 %collective-permute-start.14 = (bf16[16,4096]{1,0:T(8,128)(2,1)S(1)}, bf16[16,4096]{1,0:T(8,128)(2,1)S(1)}, u32[]{:S(2)}, u32[]{:S(2)}) collective-permute-start(bf16[16,4096]{1,0:T(8,128)(2,1)S(1)} %fusion.34), channel_id=1, source_target_pairs={{0,8},{8,0},{1,9},{9,1},{2,10},{10,2},{3,11},{11,3},{4,12},{12,4},... | collective-permute-start | bytes 393224 | tf_op jit(solution)/shard_map/ppermute | solution.py:121
  292.2 10.0 %collective-permute-start.19 = (bf16[16,4096]{1,0:T(8,128)(2,1)S(1)}, bf16[16,4096]{1,0:T(8,128)(2,1)S(1)}, u32[]{:S(2)}, u32[]{:S(2)}) collective-permute-start(bf16[16,4096]{1,0:T(8,128)(2,1)S(1)} %fusion.35), channel_id=1, source_target_pairs={{0,8},{8,0},{1,9},{9,1},{2,10},{10,2},{3,11},{11,3},{4,12},{12,4},... | collective-permute-start | bytes 393224 | tf_op jit(solution)/shard_map/ppermute | solution.py:121
  302.3 13.6 %collective-permute-done.19 = bf16[16,4096]{1,0:T(8,128)(2,1)S(1)} collective-permute-done((bf16[16,4096]{1,0:T(8,128)(2,1)S(1)}, bf16[16,4096]{1,0:T(8,128)(2,1)S(1)}, u32[]{:S(2)}, u32[]{:S(2)}) %collective-permute-start.19) | collective-permute-done | bytes 131104 | tf_op jit(solution)/shard_map/ppermute | solution.py:121
  (85 shorter events, 13.5 us)
Async XLA Ops:
  6.5 96.7 %all-gather.4.cloned.1.call-start = ((), (), s32[]{:S(2)}) async-start(), calls=%async_computation | async-start | bytes 2949120 | tf_op jit(solution)/shard_map/all_gather | solution.py:133
  13.2 175.8 %all-gather.6.cloned.1.call-start = ((), (), s32[]{:S(2)}) async-start(), calls=%async_computation.1 | async-start | bytes 7864320 | tf_op jit(solution)/shard_map/all_gather | solution.py:139
  13.3 21.5 %collective-permute-start = (bf16[16,8192]{1,0:T(8,128)(2,1)S(1)}, bf16[16,8192]{1,0:T(8,128)(2,1)S(1)}, u32[]{:S(2)}, u32[]{:S(2)}) collective-permute-start(bf16[16,8192]{1,0:T(8,128)(2,1)S(1)} %fusion.15), channel_id=1, source_target_pairs={{0,8},{8,0},{1,9},{9,1},{2,10},{10,2},{3,11},{11,3},{4,12},{12,4},... | collective-permute-start | bytes 786440 | tf_op jit(solution)/shard_map/ppermute | solution.py:85
  109.1 21.8 %collective-permute-start.1 = (bf16[2,16,8192]{2,1,0:T(8,128)(2,1)S(1)}, bf16[2,16,8192]{2,1,0:T(8,128)(2,1)S(1)}, u32[]{:S(2)}, u32[]{:S(2)}) collective-permute-start(bf16[2,16,8192]{2,1,0:T(8,128)(2,1)S(1)} %fusion.23), channel_id=1, source_target_pairs={{0,6},{2,0},{4,2},{6,4},{1,7},{3,1},{5,3},{7,5},{8,14},{10,8},{12,... | collective-permute-start | bytes 1572872 | tf_op jit(solution)/shard_map/ppermute | solution.py:88
  113.8 15.2 %collective-permute-start.2 = (bf16[2,16,8192]{2,1,0:T(8,128)(2,1)S(1)}, bf16[2,16,8192]{2,1,0:T(8,128)(2,1)S(1)}, u32[]{:S(2)}, u32[]{:S(2)}) collective-permute-start(bf16[2,16,8192]{2,1,0:T(8,128)(2,1)S(1)} %fusion.23), channel_id=1, source_target_pairs={{0,2},{2,4},{4,6},{6,0},{1,3},{3,5},{5,7},{7,1},{8,10},{10,12},{12... | collective-permute-start | bytes 1572872 | tf_op jit(solution)/shard_map/ppermute | solution.py:85
  116.6 131.3 %all-gather.8.cloned.1.call-start = ((), (), s32[]{:S(2)}) async-start(), calls=%async_computation.2 | async-start | bytes 5242880 | tf_op jit(solution)/shard_map/all_gather | solution.py:141
  129.0 14.4 %collective-permute-start.3 = (bf16[2,16,8192]{2,1,0:T(8,128)(2,1)S(1)}, bf16[2,16,8192]{2,1,0:T(8,128)(2,1)S(1)}, u32[]{:S(2)}, u32[]{:S(2)}) collective-permute-start(bf16[2,16,8192]{2,1,0:T(8,128)(2,1)S(1)} %collective-permute-done.2), channel_id=1, source_target_pairs={{0,2},{2,4},{4,6},{6,0},{1,3},{3,5},{5,7},{7,1},{8,10},{10,12},{12... | collective-permute-start | bytes 1572872 | tf_op jit(solution)/shard_map/ppermute | solution.py:85
  150.1 40.9 %collective-permute-start.4 = (bf16[4,2,16,8192]{3,2,0,1:T(8,128)(2,1)S(1)}, bf16[4,2,16,8192]{3,2,0,1:T(8,128)(2,1)}, u32[]{:S(2)}, u32[]{:S(2)}) collective-permute-start(bf16[4,2,16,8192]{3,2,0,1:T(8,128)(2,1)S(1)} %constant_dynamic-slice_fusion.5), channel_id=1, source_target_pairs={{0,1},{1,0},{2,3},{3,2},{4,5},{5,4},{6,7},{7,6},{8,9},{9,8},{10,11... | collective-permute-start | bytes 6291464 | tf_op jit(solution)/shard_map/ppermute | solution.py:85
  189.1 7.1 %slice-start = ((s8[6291456]{0:T(1024)(128)(4,1)}), s8[4194304]{0:T(1024)(128)(4,1)S(1)}, s32[]{:S(2)}) async-start(s8[6291456]{0:T(1024)(128)(4,1)} %bitcast.149), calls=%async_computation.3 | async-start | bytes 8388608
  191.0 5.2 %slice-start.1 = ((s8[6291456]{0:T(1024)(128)(4,1)}), s8[2097152]{0:T(1024)(128)(4,1)S(1)}, s32[]{:S(2)}) async-start(s8[6291456]{0:T(1024)(128)(4,1)} %bitcast.149), calls=%async_computation.4 | async-start | bytes 4194304
  197.7 14.4 %collective-permute-start.5 = (bf16[64,256]{1,0:T(8,128)(2,1)S(1)}, bf16[64,256]{1,0:T(8,128)(2,1)S(1)}, u32[]{:S(2)}, u32[]{:S(2)}) collective-permute-start(bf16[64,256]{1,0:T(8,128)(2,1)S(1)} %bitcast.156), channel_id=1, source_target_pairs={{0,8},{8,0},{1,9},{9,1},{2,10},{10,2},{3,11},{11,3},{4,12},{12,4},... | collective-permute-start | bytes 98312 | tf_op jit(solution)/shard_map/ppermute | solution.py:85
  212.2 12.9 %collective-permute-start.6 = (bf16[2,64,256]{2,1,0:T(8,128)(2,1)S(1)}, bf16[2,64,256]{2,1,0:T(8,128)(2,1)S(1)}, u32[]{:S(2)}, u32[]{:S(2)}) collective-permute-start(bf16[2,64,256]{2,1,0:T(8,128)(2,1)S(1)} %get-tuple-element.25), channel_id=1, source_target_pairs={{0,6},{2,0},{4,2},{6,4},{1,7},{3,1},{5,3},{7,5},{8,14},{10,8},{12,... | collective-permute-start | bytes 196616 | tf_op jit(solution)/shard_map/ppermute | solution.py:88
  216.5 6.6 %collective-permute-start.7 = (bf16[2,64,256]{2,1,0:T(8,128)(2,1)S(1)}, bf16[2,64,256]{2,1,0:T(8,128)(2,1)S(1)}, u32[]{:S(2)}, u32[]{:S(2)}) collective-permute-start(bf16[2,64,256]{2,1,0:T(8,128)(2,1)S(1)} %get-tuple-element.25), channel_id=1, source_target_pairs={{0,2},{2,4},{4,6},{6,0},{1,3},{3,5},{5,7},{7,1},{8,10},{10,12},{12... | collective-permute-start | bytes 196616 | tf_op jit(solution)/shard_map/ppermute | solution.py:85
  223.2 6.6 %collective-permute-start.8 = (bf16[2,64,256]{2,1,0:T(8,128)(2,1)S(1)}, bf16[2,64,256]{2,1,0:T(8,128)(2,1)S(1)}, u32[]{:S(2)}, u32[]{:S(2)}) collective-permute-start(bf16[2,64,256]{2,1,0:T(8,128)(2,1)S(1)} %collective-permute-done.7), channel_id=1, source_target_pairs={{0,2},{2,4},{4,6},{6,0},{1,3},{3,5},{5,7},{7,1},{8,10},{10,12},{12... | collective-permute-start | bytes 196616 | tf_op jit(solution)/shard_map/ppermute | solution.py:85
  229.9 6.5 %collective-permute-start.9 = (bf16[4,2,64,256]{3,2,1,0:T(8,128)(2,1)S(1)}, bf16[4,2,64,256]{3,2,1,0:T(8,128)(2,1)S(1)}, u32[]{:S(2)}, u32[]{:S(2)}) collective-permute-start(bf16[4,2,64,256]{3,2,1,0:T(8,128)(2,1)S(1)} %constant_dynamic-slice_fusion.4), channel_id=1, source_target_pairs={{0,1},{1,0},{2,3},{3,2},{4,5},{5,4},{6,7},{7,6},{8,9},{9,8},{10,11... | collective-permute-start | bytes 786440 | tf_op jit(solution)/shard_map/ppermute | solution.py:85
  253.1 5.2 %collective-permute-start.10 = (bf16[2,4,16,4096]{3,2,0,1:T(8,128)(2,1)}, bf16[2,4,16,4096]{3,2,0,1:T(8,128)(2,1)}, u32[]{:S(2)}, u32[]{:S(2)}) collective-permute-start(bf16[2,4,16,4096]{3,2,0,1:T(8,128)(2,1)} %bitcast.139), channel_id=1, source_target_pairs={{0,1},{1,0},{2,3},{3,2},{4,5},{5,4},{6,7},{7,6},{8,9},{9,8},{10,11... | collective-permute-start | bytes 3145736 | tf_op jit(solution)/shard_map/ppermute | solution.py:115
  255.8 14.6 %collective-permute-start.15 = (bf16[2,4,16,4096]{3,2,0,1:T(8,128)(2,1)S(1)}, bf16[2,4,16,4096]{3,2,0,1:T(8,128)(2,1)S(1)}, u32[]{:S(2)}, u32[]{:S(2)}) collective-permute-start(bf16[2,4,16,4096]{3,2,0,1:T(8,128)(2,1)S(1)} %bitcast.147), channel_id=1, source_target_pairs={{0,1},{1,0},{2,3},{3,2},{4,5},{5,4},{6,7},{7,6},{8,9},{9,8},{10,11... | collective-permute-start | bytes 3145736 | tf_op jit(solution)/shard_map/ppermute | solution.py:115
  259.9 16.0 %collective-permute-start.11 = (bf16[2,16,4096]{2,1,0:T(8,128)(2,1)S(1)}, bf16[2,16,4096]{2,1,0:T(8,128)(2,1)S(1)}, u32[]{:S(2)}, u32[]{:S(2)}) collective-permute-start(bf16[2,16,4096]{2,1,0:T(8,128)(2,1)S(1)} %get-tuple-element.28), channel_id=1, source_target_pairs={{0,2},{2,4},{4,6},{6,0},{1,3},{3,5},{5,7},{7,1},{8,10},{10,12},{12... | collective-permute-start | bytes 786440 | tf_op jit(solution)/shard_map/ppermute | solution.py:120
  263.0 16.3 %collective-permute-start.12 = (bf16[2,16,4096]{2,1,0:T(8,128)(2,1)S(1)}, bf16[2,16,4096]{2,1,0:T(8,128)(2,1)S(1)}, u32[]{:S(2)}, u32[]{:S(2)}) collective-permute-start(bf16[2,16,4096]{2,1,0:T(8,128)(2,1)S(1)} %get-tuple-element.30), channel_id=1, source_target_pairs={{0,4},{2,6},{4,0},{6,2},{1,5},{3,7},{5,1},{7,3},{8,12},{10,14},{12... | collective-permute-start | bytes 786440 | tf_op jit(solution)/shard_map/ppermute | solution.py:120
  267.3 11.9 %collective-permute-start.13 = (bf16[2,16,4096]{2,1,0:T(8,128)(2,1)S(1)}, bf16[2,16,4096]{2,1,0:T(8,128)(2,1)S(1)}, u32[]{:S(2)}, u32[]{:S(2)}) collective-permute-start(bf16[2,16,4096]{2,1,0:T(8,128)(2,1)S(1)} %get-tuple-element.29), channel_id=1, source_target_pairs={{0,6},{2,0},{4,2},{6,4},{1,7},{3,1},{5,3},{7,5},{8,14},{10,8},{12,... | collective-permute-start | bytes 786440 | tf_op jit(solution)/shard_map/ppermute | solution.py:120
  270.7 45.3 %copy-start = (bf16[16,8192]{1,0:T(8,128)(2,1)S(1)}, bf16[16,8192]{1,0:T(8,128)(2,1)}, u32[]{:S(2)}) copy-start(bf16[16,8192]{1,0:T(8,128)(2,1)} %param.8) | copy-start | bytes 786436
  270.8 21.2 %collective-permute-start.16 = (bf16[2,16,4096]{2,1,0:T(8,128)(2,1)S(1)}, bf16[2,16,4096]{2,1,0:T(8,128)(2,1)S(1)}, u32[]{:S(2)}, u32[]{:S(2)}) collective-permute-start(bf16[2,16,4096]{2,1,0:T(8,128)(2,1)S(1)} %get-tuple-element.33), channel_id=1, source_target_pairs={{0,2},{2,4},{4,6},{6,0},{1,3},{3,5},{5,7},{7,1},{8,10},{10,12},{12... | collective-permute-start | bytes 786440 | tf_op jit(solution)/shard_map/ppermute | solution.py:120
  273.0 19.0 %collective-permute-start.17 = (bf16[2,16,4096]{2,1,0:T(8,128)(2,1)S(1)}, bf16[2,16,4096]{2,1,0:T(8,128)(2,1)S(1)}, u32[]{:S(2)}, u32[]{:S(2)}) collective-permute-start(bf16[2,16,4096]{2,1,0:T(8,128)(2,1)S(1)} %get-tuple-element.35), channel_id=1, source_target_pairs={{0,4},{2,6},{4,0},{6,2},{1,5},{3,7},{5,1},{7,3},{8,12},{10,14},{12... | collective-permute-start | bytes 786440 | tf_op jit(solution)/shard_map/ppermute | solution.py:120
  275.8 16.2 %collective-permute-start.18 = (bf16[2,16,4096]{2,1,0:T(8,128)(2,1)S(1)}, bf16[2,16,4096]{2,1,0:T(8,128)(2,1)S(1)}, u32[]{:S(2)}, u32[]{:S(2)}) collective-permute-start(bf16[2,16,4096]{2,1,0:T(8,128)(2,1)S(1)} %get-tuple-element.34), channel_id=1, source_target_pairs={{0,6},{2,0},{4,2},{6,4},{1,7},{3,1},{5,3},{7,5},{8,14},{10,8},{12,... | collective-permute-start | bytes 786440 | tf_op jit(solution)/shard_map/ppermute | solution.py:120
  279.4 22.8 %collective-permute-start.14 = (bf16[16,4096]{1,0:T(8,128)(2,1)S(1)}, bf16[16,4096]{1,0:T(8,128)(2,1)S(1)}, u32[]{:S(2)}, u32[]{:S(2)}) collective-permute-start(bf16[16,4096]{1,0:T(8,128)(2,1)S(1)} %fusion.34), channel_id=1, source_target_pairs={{0,8},{8,0},{1,9},{9,1},{2,10},{10,2},{3,11},{11,3},{4,12},{12,4},... | collective-permute-start | bytes 393224 | tf_op jit(solution)/shard_map/ppermute | solution.py:121
  292.2 23.7 %collective-permute-start.19 = (bf16[16,4096]{1,0:T(8,128)(2,1)S(1)}, bf16[16,4096]{1,0:T(8,128)(2,1)S(1)}, u32[]{:S(2)}, u32[]{:S(2)}) collective-permute-start(bf16[16,4096]{1,0:T(8,128)(2,1)S(1)} %fusion.35), channel_id=1, source_target_pairs={{0,8},{8,0},{1,9},{9,1},{2,10},{10,2},{3,11},{11,3},{4,12},{12,4},... | collective-permute-start | bytes 393224 | tf_op jit(solution)/shard_map/ppermute | solution.py:121
Sparse Core Ops, SparseCore 0:
  13.4 89.8 all-gather.3
  116.7 72.3 all-gather.5
  191.2 56.6 all-gather.7
